TPU v7x, 32 devices: a whole 2x2x4 slice. The times are simulated.
32 devices in a mesh: space: 16 (over z, x, core), tm: 2 (over y).
Axes of the slice: x: 2, y: 2, z: 4, core: 2. Of those that a mesh axis runs over, the one named last changes fastest.
Arguments:
- guess_pressure: float32 [2, 32, 64, 128], P('tm', 'space'), may hold values from -6 to 6
- guess_velocity: float32 [2, 3, 32, 64, 128], P('tm', None, 'space'), may hold values from -6 to 6
- initial_pressure: float32 [32, 64, 128], P('space'), may hold values from -6 to 6
- initial_velocity: float32 [3, 32, 64, 128], P(None, 'space'), may hold values from -6 to 6
- stiffness: float32 [32, 64, 128], P('space'), may hold values from 0.5 to 2
- inv_mass: float32 [32, 64, 128], P('space'), may hold values from 0.5 to 2
Outputs:
- corrected_pressure: float32 [2, 32, 64, 128], P('tm', 'space')
- corrected_velocity: float32 [2, 3, 32, 64, 128], P('tm', None, 'space')
- residual_pressure: float32 [2, 32, 64, 128], P('tm', 'space')
- residual_velocity: float32 [2, 3, 32, 64, 128], P('tm', None, 'space')
All inputs are finite; a program needn't handle non-finite values.
Results may differ from a plain program's by a relative error of at most 0.00002.
Values sent between devices are 32-bit elements; how exact they have to be, the bound alone decides.
No kernel may reach another device: no remote copies, remote signals or barrier semaphores. Data moves between devices by JAX's collectives and lax.ppermute only.
A program may use at most 64 MiB of HBM per device.

v0:
```python
import jax
import jax.numpy as jnp
from jax import lax
from jax.sharding import PartitionSpec as P

STEPS = 4


DT_COARSE = 0.4


def from_behind(x, axis, by):
    size = lax.axis_size(axis)
    pairs = [(i, i + by) for i in range(size) if 0 <= i + by < size]
    return lax.ppermute(x, axis, pairs)


def neighbour_sum(values, offset, axis):
    return values + jnp.roll(values, offset, axis=axis)


def node_forces(pressure, lower_zones):
    combined = pressure + lower_zones
    force_x = 0.25 * (
        neighbour_sum(neighbour_sum(lower_zones, 1, -1), 1, -2)
        - neighbour_sum(neighbour_sum(pressure, 1, -1), 1, -2)
    )
    across_z = neighbour_sum(combined, 1, -1)
    force_y = 0.25 * (jnp.roll(across_z, 1, axis=-2) - across_z)
    across_y = neighbour_sum(combined, 1, -2)
    force_z = 0.25 * (jnp.roll(across_y, 1, axis=-1) - across_y)
    return jnp.stack([force_x, force_y, force_z])


def zone_divergence(velocity, upper_nodes):
    diff_x = neighbour_sum(neighbour_sum(upper_nodes[0] - velocity[0], -1, -1), -1, -2)
    sum_y = neighbour_sum(velocity[1] + upper_nodes[1], -1, -1)
    diff_y = jnp.roll(sum_y, -1, axis=-2) - sum_y
    sum_z = neighbour_sum(velocity[2] + upper_nodes[2], -1, -2)
    diff_z = jnp.roll(sum_z, -1, axis=-1) - sum_z
    return 0.25 * (diff_x + diff_y + diff_z)


def advance(pressure, velocity, stiffness, inv_mass, step_size):
    empty_plane = jnp.zeros_like(pressure[:1])
    lower_zones = jnp.concatenate([empty_plane, pressure[:-1]], axis=0)
    forces = node_forces(pressure, lower_zones)
    outgoing = node_forces(empty_plane, pressure[-1:])
    incoming = from_behind(outgoing, "space", 1)
    forces = jnp.concatenate([forces[:, :1] + incoming, forces[:, 1:]], axis=1)
    velocity = velocity + step_size * inv_mass * forces
    edge_nodes = from_behind(velocity[:, :1], "space", -1)
    upper_nodes = jnp.concatenate([velocity[:, 1:], edge_nodes], axis=1)
    pressure = pressure - step_size * stiffness * zone_divergence(velocity, upper_nodes)
    return (pressure, velocity)


def propagate(pressure, velocity, stiffness, inv_mass):
    fine_size = DT_COARSE / STEPS
    for repeat in range(STEPS):
        pressure, velocity = advance(pressure, velocity, stiffness, inv_mass, fine_size)
    return (pressure, velocity)


def on_device(
    guess_pressure, guess_velocity, initial_pressure, initial_velocity, stiffness, inv_mass
):
    relaxed_p, relaxed_v = propagate(guess_pressure[0], guess_velocity[0], stiffness, inv_mass)
    shifted_p, shifted_v = from_behind((relaxed_p, relaxed_v), "tm", 1)
    first_group = lax.axis_index("tm") == 0
    second_p = jnp.where(first_group, initial_pressure, shifted_p)
    second_v = jnp.where(first_group, initial_velocity, shifted_v)
    end_p, end_v = propagate(second_p, second_v, stiffness, inv_mass)
    resid_p = end_p - relaxed_p
    resid_v = end_v - relaxed_v
    error_p, error_v = (resid_p, resid_v)
    groups = lax.axis_size("tm")
    carried_p, carried_v = (resid_p, resid_v)
    for repeat in range(groups - 1):
        carried_p, carried_v = from_behind((carried_p, carried_v), "tm", 1)
        carried_p, carried_v = advance(carried_p, carried_v, stiffness, inv_mass, DT_COARSE)
        error_p = error_p + carried_p
        error_v = error_v + carried_v
    corrected_p = relaxed_p + error_p
    corrected_v = relaxed_v + error_v
    return (corrected_p[None], corrected_v[None], resid_p[None], resid_v[None])


def solution(mesh):
    placed = (
        P("tm", "space", None, None),
        P("tm", None, "space", None, None),
        P("space", None, None),
        P(None, "space", None, None),
        P("space", None, None),
        P("space", None, None),
    )
    return jax.shard_map(
        on_device,
        mesh=mesh,
        in_specs=placed,
        out_specs=(
            P("tm", "space", None, None),
            P("tm", None, "space", None, None),
            P("tm", "space", None, None),
            P("tm", None, "space", None, None),
        ),
        check_vma=False,
    )
```

profile of v0, /device:TPU:7, one launch (start us, length us, event | category | flops | bytes accessed | tf_op | source)
XLA Modules:
  0.0 134.6 jit_solution(8019663817314503757)
XLA Ops:
  2.6 3.7 %collective-permute-start = (f32[3,1,64,128]{3,2,1,0:T(8,128)S(1)}, f32[3,1,64,128]{3,2,1,0:T(8,128)S(1)}, u32[]{:S(2)}, u32[]{:S(2)}) collective-permute-start(f32[3,1,64,128]{3,2,1,0:T(8,128)S(1)} %pad_maximum_fusion.9), channel_id=1, source_target_pairs={{0,2},{2,4},{4,6},{6,8},{8,10},{10,12},{12,14},{14,16},{16,18},{18... | collective-permute-start | bytes 294920 | tf_op jit(solution)/shard_map/ppermute | solution.py:15
  8.9 2.4 %collective-permute-start.1 = (f32[3,1,64,128]{3,2,1,0:T(8,128)S(1)}, f32[3,1,64,128]{3,2,1,0:T(8,128)S(1)}, u32[]{:S(2)}, u32[]{:S(2)}) collective-permute-start(f32[3,1,64,128]{3,2,1,0:T(8,128)S(1)} %get-tuple-element.67), channel_id=1, source_target_pairs={{2,0},{4,2},{6,4},{8,6},{10,8},{12,10},{14,12},{16,14},{18,16},{20... | collective-permute-start | bytes 294920 | tf_op jit(solution)/shard_map/ppermute | solution.py:15
  11.2 4.5 %collective-permute-done.1 = f32[3,1,64,128]{3,2,1,0:T(8,128)S(1)} collective-permute-done((f32[3,1,64,128]{3,2,1,0:T(8,128)S(1)}, f32[3,1,64,128]{3,2,1,0:T(8,128)S(1)}, u32[]{:S(2)}, u32[]{:S(2)}) %collective-permute-start.1) | collective-permute-done | bytes 98336 | tf_op jit(solution)/shard_map/ppermute | solution.py:15
  18.1 1.9 %collective-permute-start.2 = (f32[3,1,64,128]{3,2,1,0:T(8,128)S(1)}, f32[3,1,64,128]{3,2,1,0:T(8,128)S(1)}, u32[]{:S(2)}, u32[]{:S(2)}) collective-permute-start(f32[3,1,64,128]{3,2,1,0:T(8,128)S(1)} %pad_maximum_fusion.10), channel_id=1, source_target_pairs={{0,2},{2,4},{4,6},{6,8},{8,10},{10,12},{12,14},{14,16},{16,18},{18... | collective-permute-start | bytes 294920 | tf_op jit(solution)/shard_map/ppermute | solution.py:15
  21.8 2.3 %collective-permute-start.3 = (f32[3,1,64,128]{3,2,1,0:T(8,128)S(1)}, f32[3,1,64,128]{3,2,1,0:T(8,128)S(1)}, u32[]{:S(2)}, u32[]{:S(2)}) collective-permute-start(f32[3,1,64,128]{3,2,1,0:T(8,128)S(1)} %get-tuple-element.63), channel_id=1, source_target_pairs={{2,0},{4,2},{6,4},{8,6},{10,8},{12,10},{14,12},{16,14},{18,16},{20... | collective-permute-start | bytes 294920 | tf_op jit(solution)/shard_map/ppermute | solution.py:15
  24.0 5.2 %collective-permute-done.3 = f32[3,1,64,128]{3,2,1,0:T(8,128)S(1)} collective-permute-done((f32[3,1,64,128]{3,2,1,0:T(8,128)S(1)}, f32[3,1,64,128]{3,2,1,0:T(8,128)S(1)}, u32[]{:S(2)}, u32[]{:S(2)}) %collective-permute-start.3) | collective-permute-done | bytes 98336 | tf_op jit(solution)/shard_map/ppermute | solution.py:15
  30.9 1.9 %collective-permute-start.4 = (f32[3,1,64,128]{3,2,1,0:T(8,128)S(1)}, f32[3,1,64,128]{3,2,1,0:T(8,128)S(1)}, u32[]{:S(2)}, u32[]{:S(2)}) collective-permute-start(f32[3,1,64,128]{3,2,1,0:T(8,128)S(1)} %pad_maximum_fusion.11), channel_id=1, source_target_pairs={{0,2},{2,4},{4,6},{6,8},{8,10},{10,12},{12,14},{14,16},{16,18},{18... | collective-permute-start | bytes 294920 | tf_op jit(solution)/shard_map/ppermute | solution.py:15
  34.6 1.9 %collective-permute-start.5 = (f32[3,1,64,128]{3,2,1,0:T(8,128)S(1)}, f32[3,1,64,128]{3,2,1,0:T(8,128)S(1)}, u32[]{:S(2)}, u32[]{:S(2)}) collective-permute-start(f32[3,1,64,128]{3,2,1,0:T(8,128)S(1)} %get-tuple-element.59), channel_id=1, source_target_pairs={{2,0},{4,2},{6,4},{8,6},{10,8},{12,10},{14,12},{16,14},{18,16},{20... | collective-permute-start | bytes 294920 | tf_op jit(solution)/shard_map/ppermute | solution.py:15
  36.5 5.6 %collective-permute-done.5 = f32[3,1,64,128]{3,2,1,0:T(8,128)S(1)} collective-permute-done((f32[3,1,64,128]{3,2,1,0:T(8,128)S(1)}, f32[3,1,64,128]{3,2,1,0:T(8,128)S(1)}, u32[]{:S(2)}, u32[]{:S(2)}) %collective-permute-start.5) | collective-permute-done | bytes 98336 | tf_op jit(solution)/shard_map/ppermute | solution.py:15
  43.7 1.9 %collective-permute-start.6 = (f32[3,1,64,128]{3,2,1,0:T(8,128)S(1)}, f32[3,1,64,128]{3,2,1,0:T(8,128)S(1)}, u32[]{:S(2)}, u32[]{:S(2)}) collective-permute-start(f32[3,1,64,128]{3,2,1,0:T(8,128)S(1)} %pad_maximum_fusion.12), channel_id=1, source_target_pairs={{0,2},{2,4},{4,6},{6,8},{8,10},{10,12},{12,14},{14,16},{16,18},{18... | collective-permute-start | bytes 294920 | tf_op jit(solution)/shard_map/ppermute | solution.py:15
  47.4 1.9 %collective-permute-start.7 = (f32[3,1,64,128]{3,2,1,0:T(8,128)S(1)}, f32[3,1,64,128]{3,2,1,0:T(8,128)S(1)}, u32[]{:S(2)}, u32[]{:S(2)}) collective-permute-start(f32[3,1,64,128]{3,2,1,0:T(8,128)S(1)} %get-tuple-element.55), channel_id=1, source_target_pairs={{2,0},{4,2},{6,4},{8,6},{10,8},{12,10},{14,12},{16,14},{18,16},{20... | collective-permute-start | bytes 294920 | tf_op jit(solution)/shard_map/ppermute | solution.py:15
  49.3 5.6 %collective-permute-done.7 = f32[3,1,64,128]{3,2,1,0:T(8,128)S(1)} collective-permute-done((f32[3,1,64,128]{3,2,1,0:T(8,128)S(1)}, f32[3,1,64,128]{3,2,1,0:T(8,128)S(1)}, u32[]{:S(2)}, u32[]{:S(2)}) %collective-permute-start.7) | collective-permute-done | bytes 98336 | tf_op jit(solution)/shard_map/ppermute | solution.py:15
  58.2 2.7 %collective-permute-done.8 = f32[2,64,128]{2,1,0:T(8,128)S(1)} collective-permute-done((f32[2,64,128]{2,1,0:T(8,128)S(1)}, f32[2,64,128]{2,1,0:T(8,128)S(1)}, u32[]{:S(2)}, u32[]{:S(2)}) %collective-permute-start.8) | collective-permute-done | bytes 65568 | tf_op jit(solution)/shard_map/ppermute | solution.py:15
  61.9 3.4 %collective-permute-start.10 = (f32[3,1,64,128]{3,2,1,0:T(8,128)S(1)}, f32[3,1,64,128]{3,2,1,0:T(8,128)S(1)}, u32[]{:S(2)}, u32[]{:S(2)}) collective-permute-start(f32[3,1,64,128]{3,2,1,0:T(8,128)S(1)} %pad_maximum_fusion.13), channel_id=1, source_target_pairs={{0,2},{2,4},{4,6},{6,8},{8,10},{10,12},{12,14},{14,16},{16,18},{18... | collective-permute-start | bytes 294920 | tf_op jit(solution)/shard_map/ppermute | solution.py:15
  67.0 1.9 %collective-permute-start.11 = (f32[3,1,64,128]{3,2,1,0:T(8,128)S(1)}, f32[3,1,64,128]{3,2,1,0:T(8,128)S(1)}, u32[]{:S(2)}, u32[]{:S(2)}) collective-permute-start(f32[3,1,64,128]{3,2,1,0:T(8,128)S(1)} %get-tuple-element.51), channel_id=1, source_target_pairs={{2,0},{4,2},{6,4},{8,6},{10,8},{12,10},{14,12},{16,14},{18,16},{20... | collective-permute-start | bytes 294920 | tf_op jit(solution)/shard_map/ppermute | solution.py:15
  68.9 5.6 %collective-permute-done.11 = f32[3,1,64,128]{3,2,1,0:T(8,128)S(1)} collective-permute-done((f32[3,1,64,128]{3,2,1,0:T(8,128)S(1)}, f32[3,1,64,128]{3,2,1,0:T(8,128)S(1)}, u32[]{:S(2)}, u32[]{:S(2)}) %collective-permute-start.11) | collective-permute-done | bytes 98336 | tf_op jit(solution)/shard_map/ppermute | solution.py:15
  79.8 1.9 %collective-permute-start.13 = (f32[3,1,64,128]{3,2,1,0:T(8,128)S(1)}, f32[3,1,64,128]{3,2,1,0:T(8,128)S(1)}, u32[]{:S(2)}, u32[]{:S(2)}) collective-permute-start(f32[3,1,64,128]{3,2,1,0:T(8,128)S(1)} %get-tuple-element.47), channel_id=1, source_target_pairs={{2,0},{4,2},{6,4},{8,6},{10,8},{12,10},{14,12},{16,14},{18,16},{20... | collective-permute-start | bytes 294920 | tf_op jit(solution)/shard_map/ppermute | solution.py:15
  81.7 5.6 %collective-permute-done.13 = f32[3,1,64,128]{3,2,1,0:T(8,128)S(1)} collective-permute-done((f32[3,1,64,128]{3,2,1,0:T(8,128)S(1)}, f32[3,1,64,128]{3,2,1,0:T(8,128)S(1)}, u32[]{:S(2)}, u32[]{:S(2)}) %collective-permute-start.13) | collective-permute-done | bytes 98336 | tf_op jit(solution)/shard_map/ppermute | solution.py:15
  94.5 5.6 %collective-permute-done.15 = f32[3,1,64,128]{3,2,1,0:T(8,128)S(1)} collective-permute-done((f32[3,1,64,128]{3,2,1,0:T(8,128)S(1)}, f32[3,1,64,128]{3,2,1,0:T(8,128)S(1)}, u32[]{:S(2)}, u32[]{:S(2)}) %collective-permute-start.15) | collective-permute-done | bytes 98336 | tf_op jit(solution)/shard_map/ppermute | solution.py:15
  101.7 1.9 %collective-permute-start.16 = (f32[3,1,64,128]{3,2,1,0:T(8,128)S(1)}, f32[3,1,64,128]{3,2,1,0:T(8,128)S(1)}, u32[]{:S(2)}, u32[]{:S(2)}) collective-permute-start(f32[3,1,64,128]{3,2,1,0:T(8,128)S(1)} %pad_maximum_fusion.16), channel_id=1, source_target_pairs={{0,2},{2,4},{4,6},{6,8},{8,10},{10,12},{12,14},{14,16},{16,18},{18... | collective-permute-start | bytes 294920 | tf_op jit(solution)/shard_map/ppermute | solution.py:15
  107.4 5.6 %collective-permute-done.17 = f32[3,1,64,128]{3,2,1,0:T(8,128)S(1)} collective-permute-done((f32[3,1,64,128]{3,2,1,0:T(8,128)S(1)}, f32[3,1,64,128]{3,2,1,0:T(8,128)S(1)}, u32[]{:S(2)}, u32[]{:S(2)}) %collective-permute-start.17) | collective-permute-done | bytes 98336 | tf_op jit(solution)/shard_map/ppermute | solution.py:15
  116.3 2.7 %collective-permute-done.18 = f32[2,64,128]{2,1,0:T(8,128)S(1)} collective-permute-done((f32[2,64,128]{2,1,0:T(8,128)S(1)}, f32[2,64,128]{2,1,0:T(8,128)S(1)}, u32[]{:S(2)}, u32[]{:S(2)}) %collective-permute-start.18) | collective-permute-done | bytes 65568 | tf_op jit(solution)/shard_map/ppermute | solution.py:15
  119.9 3.4 %collective-permute-start.20 = (f32[3,1,64,128]{3,2,1,0:T(8,128)S(1)}, f32[3,1,64,128]{3,2,1,0:T(8,128)S(1)}, u32[]{:S(2)}, u32[]{:S(2)}) collective-permute-start(f32[3,1,64,128]{3,2,1,0:T(8,128)S(1)} %pad_maximum_fusion.17), channel_id=1, source_target_pairs={{0,2},{2,4},{4,6},{6,8},{8,10},{10,12},{12,14},{14,16},{16,18},{18... | collective-permute-start | bytes 294920 | tf_op jit(solution)/shard_map/ppermute | solution.py:15
  127.7 5.6 %collective-permute-done.21 = f32[3,1,64,128]{3,2,1,0:T(8,128)S(1)} collective-permute-done((f32[3,1,64,128]{3,2,1,0:T(8,128)S(1)}, f32[3,1,64,128]{3,2,1,0:T(8,128)S(1)}, u32[]{:S(2)}, u32[]{:S(2)}) %collective-permute-start.21) | collective-permute-done | bytes 98336 | tf_op jit(solution)/shard_map/ppermute | solution.py:15
  (417 shorter events, 47.3 us)
Async XLA Ops:
  2.6 5.4 %collective-permute-start = (f32[3,1,64,128]{3,2,1,0:T(8,128)S(1)}, f32[3,1,64,128]{3,2,1,0:T(8,128)S(1)}, u32[]{:S(2)}, u32[]{:S(2)}) collective-permute-start(f32[3,1,64,128]{3,2,1,0:T(8,128)S(1)} %pad_maximum_fusion.9), channel_id=1, source_target_pairs={{0,2},{2,4},{4,6},{6,8},{8,10},{10,12},{12,14},{14,16},{16,18},{18... | collective-permute-start | bytes 294920 | tf_op jit(solution)/shard_map/ppermute | solution.py:15
  8.9 6.8 %collective-permute-start.1 = (f32[3,1,64,128]{3,2,1,0:T(8,128)S(1)}, f32[3,1,64,128]{3,2,1,0:T(8,128)S(1)}, u32[]{:S(2)}, u32[]{:S(2)}) collective-permute-start(f32[3,1,64,128]{3,2,1,0:T(8,128)S(1)} %get-tuple-element.67), channel_id=1, source_target_pairs={{2,0},{4,2},{6,4},{8,6},{10,8},{12,10},{14,12},{16,14},{18,16},{20... | collective-permute-start | bytes 294920 | tf_op jit(solution)/shard_map/ppermute | solution.py:15
  18.1 3.5 %collective-permute-start.2 = (f32[3,1,64,128]{3,2,1,0:T(8,128)S(1)}, f32[3,1,64,128]{3,2,1,0:T(8,128)S(1)}, u32[]{:S(2)}, u32[]{:S(2)}) collective-permute-start(f32[3,1,64,128]{3,2,1,0:T(8,128)S(1)} %pad_maximum_fusion.10), channel_id=1, source_target_pairs={{0,2},{2,4},{4,6},{6,8},{8,10},{10,12},{12,14},{14,16},{16,18},{18... | collective-permute-start | bytes 294920 | tf_op jit(solution)/shard_map/ppermute | solution.py:15
  21.8 7.5 %collective-permute-start.3 = (f32[3,1,64,128]{3,2,1,0:T(8,128)S(1)}, f32[3,1,64,128]{3,2,1,0:T(8,128)S(1)}, u32[]{:S(2)}, u32[]{:S(2)}) collective-permute-start(f32[3,1,64,128]{3,2,1,0:T(8,128)S(1)} %get-tuple-element.63), channel_id=1, source_target_pairs={{2,0},{4,2},{6,4},{8,6},{10,8},{12,10},{14,12},{16,14},{18,16},{20... | collective-permute-start | bytes 294920 | tf_op jit(solution)/shard_map/ppermute | solution.py:15
  30.9 3.5 %collective-permute-start.4 = (f32[3,1,64,128]{3,2,1,0:T(8,128)S(1)}, f32[3,1,64,128]{3,2,1,0:T(8,128)S(1)}, u32[]{:S(2)}, u32[]{:S(2)}) collective-permute-start(f32[3,1,64,128]{3,2,1,0:T(8,128)S(1)} %pad_maximum_fusion.11), channel_id=1, source_target_pairs={{0,2},{2,4},{4,6},{6,8},{8,10},{10,12},{12,14},{14,16},{16,18},{18... | collective-permute-start | bytes 294920 | tf_op jit(solution)/shard_map/ppermute | solution.py:15
  34.6 7.5 %collective-permute-start.5 = (f32[3,1,64,128]{3,2,1,0:T(8,128)S(1)}, f32[3,1,64,128]{3,2,1,0:T(8,128)S(1)}, u32[]{:S(2)}, u32[]{:S(2)}) collective-permute-start(f32[3,1,64,128]{3,2,1,0:T(8,128)S(1)} %get-tuple-element.59), channel_id=1, source_target_pairs={{2,0},{4,2},{6,4},{8,6},{10,8},{12,10},{14,12},{16,14},{18,16},{20... | collective-permute-start | bytes 294920 | tf_op jit(solution)/shard_map/ppermute | solution.py:15
  43.7 3.5 %collective-permute-start.6 = (f32[3,1,64,128]{3,2,1,0:T(8,128)S(1)}, f32[3,1,64,128]{3,2,1,0:T(8,128)S(1)}, u32[]{:S(2)}, u32[]{:S(2)}) collective-permute-start(f32[3,1,64,128]{3,2,1,0:T(8,128)S(1)} %pad_maximum_fusion.12), channel_id=1, source_target_pairs={{0,2},{2,4},{4,6},{6,8},{8,10},{10,12},{12,14},{14,16},{16,18},{18... | collective-permute-start | bytes 294920 | tf_op jit(solution)/shard_map/ppermute | solution.py:15
  47.4 7.5 %collective-permute-start.7 = (f32[3,1,64,128]{3,2,1,0:T(8,128)S(1)}, f32[3,1,64,128]{3,2,1,0:T(8,128)S(1)}, u32[]{:S(2)}, u32[]{:S(2)}) collective-permute-start(f32[3,1,64,128]{3,2,1,0:T(8,128)S(1)} %get-tuple-element.55), channel_id=1, source_target_pairs={{2,0},{4,2},{6,4},{8,6},{10,8},{12,10},{14,12},{16,14},{18,16},{20... | collective-permute-start | bytes 294920 | tf_op jit(solution)/shard_map/ppermute | solution.py:15
  55.6 5.3 %collective-permute-start.8 = (f32[2,64,128]{2,1,0:T(8,128)S(1)}, f32[2,64,128]{2,1,0:T(8,128)S(1)}, u32[]{:S(2)}, u32[]{:S(2)}) collective-permute-start(f32[2,64,128]{2,1,0:T(8,128)S(1)} %fusion.128), channel_id=1, source_target_pairs={{0,1},{2,3},{4,5},{6,7},{8,9},{10,11},{12,13},{14,15},{16,17},{18,... | collective-permute-start | bytes 196616 | tf_op jit(solution)/shard_map/ppermute | solution.py:15
  56.9 10.0 %collective-permute-start.9 = (f32[3,2,64,128]{3,2,1,0:T(8,128)S(1)}, f32[3,2,64,128]{3,2,1,0:T(8,128)S(1)}, u32[]{:S(2)}, u32[]{:S(2)}) collective-permute-start(f32[3,2,64,128]{3,2,1,0:T(8,128)S(1)} %fusion.3), channel_id=1, source_target_pairs={{0,1},{2,3},{4,5},{6,7},{8,9},{10,11},{12,13},{14,15},{16,17},{18,... | collective-permute-start | bytes 589832 | tf_op jit(solution)/shard_map/ppermute | solution.py:15
  61.9 5.0 %collective-permute-start.10 = (f32[3,1,64,128]{3,2,1,0:T(8,128)S(1)}, f32[3,1,64,128]{3,2,1,0:T(8,128)S(1)}, u32[]{:S(2)}, u32[]{:S(2)}) collective-permute-start(f32[3,1,64,128]{3,2,1,0:T(8,128)S(1)} %pad_maximum_fusion.13), channel_id=1, source_target_pairs={{0,2},{2,4},{4,6},{6,8},{8,10},{10,12},{12,14},{14,16},{16,18},{18... | collective-permute-start | bytes 294920 | tf_op jit(solution)/shard_map/ppermute | solution.py:15
  67.0 7.5 %collective-permute-start.11 = (f32[3,1,64,128]{3,2,1,0:T(8,128)S(1)}, f32[3,1,64,128]{3,2,1,0:T(8,128)S(1)}, u32[]{:S(2)}, u32[]{:S(2)}) collective-permute-start(f32[3,1,64,128]{3,2,1,0:T(8,128)S(1)} %get-tuple-element.51), channel_id=1, source_target_pairs={{2,0},{4,2},{6,4},{8,6},{10,8},{12,10},{14,12},{16,14},{18,16},{20... | collective-permute-start | bytes 294920 | tf_op jit(solution)/shard_map/ppermute | solution.py:15
  76.1 3.5 %collective-permute-start.12 = (f32[3,1,64,128]{3,2,1,0:T(8,128)S(1)}, f32[3,1,64,128]{3,2,1,0:T(8,128)S(1)}, u32[]{:S(2)}, u32[]{:S(2)}) collective-permute-start(f32[3,1,64,128]{3,2,1,0:T(8,128)S(1)} %pad_maximum_fusion.14), channel_id=1, source_target_pairs={{0,2},{2,4},{4,6},{6,8},{8,10},{10,12},{12,14},{14,16},{16,18},{18... | collective-permute-start | bytes 294920 | tf_op jit(solution)/shard_map/ppermute | solution.py:15
  79.8 7.5 %collective-permute-start.13 = (f32[3,1,64,128]{3,2,1,0:T(8,128)S(1)}, f32[3,1,64,128]{3,2,1,0:T(8,128)S(1)}, u32[]{:S(2)}, u32[]{:S(2)}) collective-permute-start(f32[3,1,64,128]{3,2,1,0:T(8,128)S(1)} %get-tuple-element.47), channel_id=1, source_target_pairs={{2,0},{4,2},{6,4},{8,6},{10,8},{12,10},{14,12},{16,14},{18,16},{20... | collective-permute-start | bytes 294920 | tf_op jit(solution)/shard_map/ppermute | solution.py:15
  88.9 3.5 %collective-permute-start.14 = (f32[3,1,64,128]{3,2,1,0:T(8,128)S(1)}, f32[3,1,64,128]{3,2,1,0:T(8,128)S(1)}, u32[]{:S(2)}, u32[]{:S(2)}) collective-permute-start(f32[3,1,64,128]{3,2,1,0:T(8,128)S(1)} %pad_maximum_fusion.15), channel_id=1, source_target_pairs={{0,2},{2,4},{4,6},{6,8},{8,10},{10,12},{12,14},{14,16},{16,18},{18... | collective-permute-start | bytes 294920 | tf_op jit(solution)/shard_map/ppermute | solution.py:15
  92.5 7.5 %collective-permute-start.15 = (f32[3,1,64,128]{3,2,1,0:T(8,128)S(1)}, f32[3,1,64,128]{3,2,1,0:T(8,128)S(1)}, u32[]{:S(2)}, u32[]{:S(2)}) collective-permute-start(f32[3,1,64,128]{3,2,1,0:T(8,128)S(1)} %get-tuple-element.43), channel_id=1, source_target_pairs={{2,0},{4,2},{6,4},{8,6},{10,8},{12,10},{14,12},{16,14},{18,16},{20... | collective-permute-start | bytes 294920 | tf_op jit(solution)/shard_map/ppermute | solution.py:15
  101.7 3.5 %collective-permute-start.16 = (f32[3,1,64,128]{3,2,1,0:T(8,128)S(1)}, f32[3,1,64,128]{3,2,1,0:T(8,128)S(1)}, u32[]{:S(2)}, u32[]{:S(2)}) collective-permute-start(f32[3,1,64,128]{3,2,1,0:T(8,128)S(1)} %pad_maximum_fusion.16), channel_id=1, source_target_pairs={{0,2},{2,4},{4,6},{6,8},{8,10},{10,12},{12,14},{14,16},{16,18},{18... | collective-permute-start | bytes 294920 | tf_op jit(solution)/shard_map/ppermute | solution.py:15
  105.4 19.5 %copy-start.3 = (f32[3,2,64,128]{3,2,1,0:T(8,128)}, f32[3,2,64,128]{3,2,1,0:T(8,128)S(1)}, u32[]{:S(2)}) copy-start(f32[3,2,64,128]{3,2,1,0:T(8,128)S(1)} %get-tuple-element.6) | copy-start | bytes 589828
  105.5 7.5 %collective-permute-start.17 = (f32[3,1,64,128]{3,2,1,0:T(8,128)S(1)}, f32[3,1,64,128]{3,2,1,0:T(8,128)S(1)}, u32[]{:S(2)}, u32[]{:S(2)}) collective-permute-start(f32[3,1,64,128]{3,2,1,0:T(8,128)S(1)} %get-tuple-element.39), channel_id=1, source_target_pairs={{2,0},{4,2},{6,4},{8,6},{10,8},{12,10},{14,12},{16,14},{18,16},{20... | collective-permute-start | bytes 294920 | tf_op jit(solution)/shard_map/ppermute | solution.py:15
  113.6 20.2 %copy-start.4 = (f32[2,64,128]{2,1,0:T(8,128)}, f32[2,64,128]{2,1,0:T(8,128)S(1)}, u32[]{:S(2)}) copy-start(f32[2,64,128]{2,1,0:T(8,128)S(1)} %fusion.177) | copy-start | bytes 196612
  113.7 5.3 %collective-permute-start.18 = (f32[2,64,128]{2,1,0:T(8,128)S(1)}, f32[2,64,128]{2,1,0:T(8,128)S(1)}, u32[]{:S(2)}, u32[]{:S(2)}) collective-permute-start(f32[2,64,128]{2,1,0:T(8,128)S(1)} %fusion.177), channel_id=1, source_target_pairs={{0,1},{2,3},{4,5},{6,7},{8,9},{10,11},{12,13},{14,15},{16,17},{18,... | collective-permute-start | bytes 196616 | tf_op jit(solution)/shard_map/ppermute | solution.py:15
  115.0 10.0 %collective-permute-start.19 = (f32[3,2,64,128]{3,2,1,0:T(8,128)S(1)}, f32[3,2,64,128]{3,2,1,0:T(8,128)S(1)}, u32[]{:S(2)}, u32[]{:S(2)}) collective-permute-start(f32[3,2,64,128]{3,2,1,0:T(8,128)S(1)} %get-tuple-element.6), channel_id=1, source_target_pairs={{0,1},{2,3},{4,5},{6,7},{8,9},{10,11},{12,13},{14,15},{16,17},{18,... | collective-permute-start | bytes 589832 | tf_op jit(solution)/shard_map/ppermute | solution.py:15
  119.9 5.0 %collective-permute-start.20 = (f32[3,1,64,128]{3,2,1,0:T(8,128)S(1)}, f32[3,1,64,128]{3,2,1,0:T(8,128)S(1)}, u32[]{:S(2)}, u32[]{:S(2)}) collective-permute-start(f32[3,1,64,128]{3,2,1,0:T(8,128)S(1)} %pad_maximum_fusion.17), channel_id=1, source_target_pairs={{0,2},{2,4},{4,6},{6,8},{8,10},{10,12},{12,14},{14,16},{16,18},{18... | collective-permute-start | bytes 294920 | tf_op jit(solution)/shard_map/ppermute | solution.py:15
  125.8 7.5 %collective-permute-start.21 = (f32[3,1,64,128]{3,2,1,0:T(8,128)S(1)}, f32[3,1,64,128]{3,2,1,0:T(8,128)S(1)}, u32[]{:S(2)}, u32[]{:S(2)}) collective-permute-start(f32[3,1,64,128]{3,2,1,0:T(8,128)S(1)} %get-tuple-element.35), channel_id=1, source_target_pairs={{2,0},{4,2},{6,4},{8,6},{10,8},{12,10},{14,12},{16,14},{18,16},{20... | collective-permute-start | bytes 294920 | tf_op jit(solution)/shard_map/ppermute | solution.py:15
  (6 other events, 10.4 us)
where the time goes:
time: 136 us; the launch traced here: 135 us
  waiting for transfers between devices  65.8 us (48%)
  starting transfers between devices  45.3 us (33%)
  local copies, waits for them, and re-layouts  10.9 us (8%)
  other arithmetic  9.99 us (7%)
  between operations  2.66 us (2%)
    ppermute x22, waiting for transfers between devices, from_behind(): return lax.ppermute(x, axis, pairs)  65.8 us
    ppermute x22, starting transfers between devices, from_behind(): return lax.ppermute(x, axis, pairs)  45.3 us
    slice x157, local copies, waits for them, and re-layouts, neighbour_sum(): return values + jnp.roll(values, offset, axis=axis)  4.53 us
    add x54, other arithmetic, neighbour_sum(): return values + jnp.roll(values, offset, axis=axis)  4.43 us
    unnamed x16, local copies, waits for them, and re-layouts  3.18 us
  transfers between devices with their start and end apart: 22, of which 20 were waited for; matrix products, arithmetic and copies ran while one was open for 3% of the time, Pallas kernels for 0%

commit v1 on v0

v1 whole, which is shorter than its diff:
```python
import jax
import jax.numpy as jnp
from jax import lax
from jax.sharding import PartitionSpec as P

STEPS = 4


DT_COARSE = 0.4


def from_behind(x, axis, by):
    size = lax.axis_size(axis)
    pairs = [(i, i + by) for i in range(size) if 0 <= i + by < size]
    return lax.ppermute(x, axis, pairs)


def neighbour_sum(values, offset, axis):
    return values + jnp.roll(values, offset, axis=axis)


def node_forces(pressure, lower_zones):
    combined = pressure + lower_zones
    force_x = 0.25 * (
        neighbour_sum(neighbour_sum(lower_zones, 1, -1), 1, -2)
        - neighbour_sum(neighbour_sum(pressure, 1, -1), 1, -2)
    )
    across_z = neighbour_sum(combined, 1, -1)
    force_y = 0.25 * (jnp.roll(across_z, 1, axis=-2) - across_z)
    across_y = neighbour_sum(combined, 1, -2)
    force_z = 0.25 * (jnp.roll(across_y, 1, axis=-1) - across_y)
    return jnp.stack([force_x, force_y, force_z], axis=-4)


def zone_divergence(velocity, upper_nodes):
    v0, v1, v2 = velocity[..., 0, :, :, :], velocity[..., 1, :, :, :], velocity[..., 2, :, :, :]
    u0, u1, u2 = upper_nodes[..., 0, :, :, :], upper_nodes[..., 1, :, :, :], upper_nodes[..., 2, :, :, :]
    diff_x = neighbour_sum(neighbour_sum(u0 - v0, -1, -1), -1, -2)
    sum_y = neighbour_sum(v1 + u1, -1, -1)
    diff_y = jnp.roll(sum_y, -1, axis=-2) - sum_y
    sum_z = neighbour_sum(v2 + u2, -1, -2)
    diff_z = jnp.roll(sum_z, -1, axis=-1) - sum_z
    return 0.25 * (diff_x + diff_y + diff_z)


def window_step(pressure, velocity, stiffness, inv_mass, step_size):
    forces = node_forces(pressure[..., 1:, :, :], pressure[..., :-1, :, :])
    velocity = velocity + step_size * inv_mass * forces
    pressure = pressure[..., 1:-1, :, :] - step_size * stiffness * zone_divergence(
        velocity[..., :-1, :, :], velocity[..., 1:, :, :]
    )
    return pressure, velocity


def window_propagate(pressure, velocity, stiffness, inv_mass, steps, step_size):
    for j in range(steps):
        width = pressure.shape[-3]
        pressure, velocity = window_step(
            pressure, velocity, stiffness[j : j + width - 2], inv_mass[j : j + width - 1], step_size
        )
        if j + 1 < steps:
            velocity = velocity[..., 1:-1, :, :]
    n = pressure.shape[-3]
    return pressure, velocity[..., :n, :, :]


def halo(blocks, widths):
    n = blocks[0].shape[1]
    reach = [-(-w // n) for w in widths]
    lefts = [[] for _ in blocks]
    rights = [[] for _ in blocks]
    for d in range(1, max(reach) + 1):
        chosen = [i for i, q in enumerate(reach) if q >= d]
        sizes = [blocks[i].shape[0] for i in chosen]
        packed = jnp.concatenate([blocks[i] for i in chosen], axis=0)
        from_left = from_behind(packed, "space", d)
        from_right = from_behind(packed, "space", -d)
        offset = 0
        for i, s in zip(chosen, sizes):
            lefts[i].insert(0, from_left[offset : offset + s])
            rights[i].append(from_right[offset : offset + s])
            offset += s
    out = []
    for i, b in enumerate(blocks):
        ext = jnp.concatenate(lefts[i] + [b] + rights[i], axis=1)
        start = reach[i] * n - widths[i]
        out.append(ext[:, start : start + n + 2 * widths[i]])
    return out


def on_device(
    guess_pressure, guess_velocity, initial_pressure, initial_velocity, stiffness, inv_mass
):
    fine_size = DT_COARSE / STEPS
    n = stiffness.shape[0]
    groups = lax.axis_size("tm")
    group = lax.axis_index("tm")

    state = jnp.concatenate(
        [
            guess_pressure[0][None],
            initial_pressure[None],
            guess_velocity[0],
            initial_velocity,
            stiffness[None],
            inv_mass[None],
        ],
        axis=0,
    )
    (ext,) = halo([state], [STEPS])
    ext_p = ext[0:2]
    ext_v = ext[2:8, 1:].reshape(2, 3, n + 2 * STEPS - 1, *ext.shape[2:])
    ext_k = ext[8, 1:-1]
    ext_m = ext[9, 1:]
    first_p, first_v = window_propagate(ext_p, ext_v, ext_k, ext_m, STEPS, fine_size)
    relaxed_p, relaxed_v = first_p[0], first_v[0]
    own_end_p, own_end_v = first_p[1], first_v[1]
    early_p = own_end_p - relaxed_p
    early_v = own_end_v - relaxed_v

    sent = jnp.concatenate([relaxed_p[None], relaxed_v, early_p[None], early_v], axis=0)
    got = from_behind(sent, "tm", 1)
    got_relaxed, got_resid = halo([got[0:4], got[4:8]], [STEPS, 1])

    late_p, late_v = window_propagate(
        got_relaxed[0],
        got_relaxed[1:4, 1:],
        ext_k,
        ext_m,
        STEPS,
        fine_size,
    )
    first_group = group == 0
    end_p = jnp.where(first_group, own_end_p, late_p)
    end_v = jnp.where(first_group, own_end_v, late_v)
    resid_p = end_p - relaxed_p
    resid_v = end_v - relaxed_v

    coarse_k = ext_k[STEPS - 1 : STEPS - 1 + n]
    coarse_m = ext_m[STEPS - 1 : STEPS - 1 + n + 1]
    if groups == 2:
        moved_p, moved_v = window_propagate(
            got_resid[0], got_resid[1:4, 1:], coarse_k, coarse_m, 1, DT_COARSE
        )
        error_p = resid_p + moved_p
        error_v = resid_v + moved_v
    else:
        error_p, error_v = resid_p, resid_v
        carried_p, carried_v = resid_p, resid_v
        for repeat in range(groups - 1):
            carried = from_behind(
                jnp.concatenate([carried_p[None], carried_v], axis=0), "tm", 1
            )
            (carried,) = halo([carried], [1])
            carried_p, carried_v = window_propagate(
                carried[0], carried[1:4, 1:], coarse_k, coarse_m, 1, DT_COARSE
            )
            error_p = error_p + carried_p
            error_v = error_v + carried_v
    corrected_p = relaxed_p + error_p
    corrected_v = relaxed_v + error_v
    return (corrected_p[None], corrected_v[None], resid_p[None], resid_v[None])


def solution(mesh):
    placed = (
        P("tm", "space", None, None),
        P("tm", None, "space", None, None),
        P("space", None, None),
        P(None, "space", None, None),
        P("space", None, None),
        P("space", None, None),
    )
    return jax.shard_map(
        on_device,
        mesh=mesh,
        in_specs=placed,
        out_specs=(
            P("tm", "space", None, None),
            P("tm", None, "space", None, None),
            P("tm", "space", None, None),
            P("tm", None, "space", None, None),
        ),
        check_vma=False,
    )
```

time: 136 us -> 130 us (0.956)
  the two profiles are of different devices: /device:TPU:7 before, /device:TPU:13 now
where the time goes in v1:
time: 130 us; the launch traced here: 129 us
  waiting for transfers between devices  57.1 us (44%)
  starting transfers between devices  26.9 us (21%)
  local copies, waits for them, and re-layouts  23.6 us (18%)
  other arithmetic  18.3 us (14%)
  between operations  2.86 us (2%)
    ppermute x9, waiting for transfers between devices, from_behind(): return lax.ppermute(x, axis, pairs)  57.1 us
    ppermute x9, starting transfers between devices, from_behind(): return lax.ppermute(x, axis, pairs)  26.9 us
    unnamed x58, local copies, waits for them, and re-layouts  11.7 us
    add x46, other arithmetic, neighbour_sum(): return values + jnp.roll(values, offset, axis=axis)  6.21 us
    slice x104, local copies, waits for them, and re-layouts, neighbour_sum(): return values + jnp.roll(values, offset, axis=axis)  6.09 us
  transfers between devices with their start and end apart: 9, of which 5 were waited for; matrix products, arithmetic and copies ran while one was open for 6% of the time, Pallas kernels for 0%

profile of v1, /device:TPU:13, one launch (start us, length us, event | category | flops | bytes accessed | tf_op | source)
XLA Modules:
  0.0 128.9 jit_solution(5228280288601288078)
XLA Ops:
  0.6 0.8 constant_dynamic-update-slice_fusion.1
  2.3 0.9 bitcast_dynamic-update-slice_fusion.1
  3.3 1.0 constant_dynamic-update-slice_fusion
  5.1 0.9 bitcast_dynamic-update-slice_fusion.3
  6.0 3.1 %collective-permute-start = (f32[10,2,64,128]{3,2,1,0:T(8,128)S(1)}, f32[10,2,64,128]{3,2,1,0:T(8,128)S(1)}, u32[]{:S(2)}, u32[]{:S(2)}) collective-permute-start(f32[10,2,64,128]{3,2,1,0:T(8,128)S(1)} %bitcast_dynamic-update-slice_fusion.3), channel_id=1, source_target_pairs={{0,4},{2,6},{4,8},{6,10},{8,12},{10,14},{12,16},{14,18},{16,20},{1... | collective-permute-start | bytes 1966088 | tf_op jit(solution)/shard_map/ppermute | solution.py:15
  9.1 4.0 %collective-permute-start.1 = (f32[10,2,64,128]{3,2,1,0:T(8,128)S(1)}, f32[10,2,64,128]{3,2,1,0:T(8,128)S(1)}, u32[]{:S(2)}, u32[]{:S(2)}) collective-permute-start(f32[10,2,64,128]{3,2,1,0:T(8,128)S(1)} %bitcast_dynamic-update-slice_fusion.3), channel_id=1, source_target_pairs={{0,2},{2,4},{4,6},{6,8},{8,10},{10,12},{12,14},{14,16},{16,18},{18... | collective-permute-start | bytes 1966088 | tf_op jit(solution)/shard_map/ppermute | solution.py:15
  13.2 1.9 %collective-permute-start.2 = (f32[10,2,64,128]{3,2,1,0:T(8,128)S(1)}, f32[10,2,64,128]{3,2,1,0:T(8,128)S(1)}, u32[]{:S(2)}, u32[]{:S(2)}) collective-permute-start(f32[10,2,64,128]{3,2,1,0:T(8,128)S(1)} %bitcast_dynamic-update-slice_fusion.3), channel_id=1, source_target_pairs={{2,0},{4,2},{6,4},{8,6},{10,8},{12,10},{14,12},{16,14},{18,16},{20... | collective-permute-start | bytes 1966088 | tf_op jit(solution)/shard_map/ppermute | solution.py:15
  15.1 3.0 %collective-permute-start.3 = (f32[10,2,64,128]{3,2,1,0:T(8,128)S(1)}, f32[10,2,64,128]{3,2,1,0:T(8,128)S(1)}, u32[]{:S(2)}, u32[]{:S(2)}) collective-permute-start(f32[10,2,64,128]{3,2,1,0:T(8,128)S(1)} %bitcast_dynamic-update-slice_fusion.3), channel_id=1, source_target_pairs={{4,0},{6,2},{8,4},{10,6},{12,8},{14,10},{16,12},{18,14},{20,16},{2... | collective-permute-start | bytes 1966088 | tf_op jit(solution)/shard_map/ppermute | solution.py:15
  18.1 0.8 broadcast_multiply_fusion
  19.0 24.6 %collective-permute-done = f32[10,2,64,128]{3,2,1,0:T(8,128)S(1)} collective-permute-done((f32[10,2,64,128]{3,2,1,0:T(8,128)S(1)}, f32[10,2,64,128]{3,2,1,0:T(8,128)S(1)}, u32[]{:S(2)}, u32[]{:S(2)}) %collective-permute-start) | collective-permute-done | bytes 655392 | tf_op jit(solution)/shard_map/ppermute | solution.py:15
  43.7 8.1 %collective-permute-done.1 = f32[10,2,64,128]{3,2,1,0:T(8,128)S(1)} collective-permute-done((f32[10,2,64,128]{3,2,1,0:T(8,128)S(1)}, f32[10,2,64,128]{3,2,1,0:T(8,128)S(1)}, u32[]{:S(2)}, u32[]{:S(2)}) %collective-permute-start.1) | collective-permute-done | bytes 655392 | tf_op jit(solution)/shard_map/ppermute | solution.py:15
  69.4 1.3 %collective-permute-start.4 = (f32[8,2,64,128]{3,2,1,0:T(8,128)S(1)}, f32[8,2,64,128]{3,2,1,0:T(8,128)}, u32[]{:S(2)}, u32[]{:S(2)}) collective-permute-start(f32[8,2,64,128]{3,2,1,0:T(8,128)S(1)} %pad_maximum_fusion), channel_id=1, source_target_pairs={{0,1},{2,3},{4,5},{6,7},{8,9},{10,11},{12,13},{14,15},{16,17},{18,... | collective-permute-start | bytes 1572872 | tf_op jit(solution)/shard_map/ppermute | solution.py:15
  70.7 12.2 %collective-permute-done.4 = f32[8,2,64,128]{3,2,1,0:T(8,128)} collective-permute-done((f32[8,2,64,128]{3,2,1,0:T(8,128)S(1)}, f32[8,2,64,128]{3,2,1,0:T(8,128)}, u32[]{:S(2)}, u32[]{:S(2)}) %collective-permute-start.4) | collective-permute-done | bytes 524320 | tf_op jit(solution)/shard_map/ppermute | solution.py:15
  82.9 2.1 %collective-permute-start.6 = (f32[8,2,64,128]{3,2,1,0:T(8,128)}, f32[8,2,64,128]{3,2,1,0:T(8,128)}, u32[]{:S(2)}, u32[]{:S(2)}) collective-permute-start(f32[8,2,64,128]{3,2,1,0:T(8,128)} %collective-permute-done.4), channel_id=1, source_target_pairs={{0,2},{2,4},{4,6},{6,8},{8,10},{10,12},{12,14},{14,16},{16,18},{18... | collective-permute-start | bytes 1572872 | tf_op jit(solution)/shard_map/ppermute | solution.py:15
  84.9 1.7 %slice.1841 = f32[4,2,64,128]{3,2,1,0:T(8,128)} slice(f32[8,2,64,128]{3,2,1,0:T(8,128)} %collective-permute-done.4), slice={[0:4], [0:2], [0:64], [0:128]} | slice | bytes 524288 | tf_op jit(solution)/shard_map/slice | solution.py:123
  86.6 6.9 %collective-permute-start.5 = (f32[4,2,64,128]{3,2,1,0:T(8,128)}, f32[4,2,64,128]{3,2,1,0:T(8,128)}, u32[]{:S(2)}, u32[]{:S(2)}) collective-permute-start(f32[4,2,64,128]{3,2,1,0:T(8,128)} %slice.1841), channel_id=1, source_target_pairs={{0,4},{2,6},{4,8},{6,10},{8,12},{10,14},{12,16},{14,18},{16,20},{1... | collective-permute-start | bytes 786440 | tf_op jit(solution)/shard_map/ppermute | solution.py:15
  93.6 1.9 %collective-permute-start.8 = (f32[4,2,64,128]{3,2,1,0:T(8,128)}, f32[4,2,64,128]{3,2,1,0:T(8,128)S(1)}, u32[]{:S(2)}, u32[]{:S(2)}) collective-permute-start(f32[4,2,64,128]{3,2,1,0:T(8,128)} %slice.1841), channel_id=1, source_target_pairs={{4,0},{6,2},{8,4},{10,6},{12,8},{14,10},{16,12},{18,14},{20,16},{2... | collective-permute-start | bytes 786440 | tf_op jit(solution)/shard_map/ppermute | solution.py:15
  95.5 2.6 %collective-permute-start.7 = (f32[8,2,64,128]{3,2,1,0:T(8,128)}, f32[8,2,64,128]{3,2,1,0:T(8,128)S(1)}, u32[]{:S(2)}, u32[]{:S(2)}) collective-permute-start(f32[8,2,64,128]{3,2,1,0:T(8,128)} %collective-permute-done.4), channel_id=1, source_target_pairs={{2,0},{4,2},{6,4},{8,6},{10,8},{12,10},{14,12},{16,14},{18,16},{20... | collective-permute-start | bytes 1572872 | tf_op jit(solution)/shard_map/ppermute | solution.py:15
  98.2 10.9 %collective-permute-done.5 = f32[4,2,64,128]{3,2,1,0:T(8,128)} collective-permute-done((f32[4,2,64,128]{3,2,1,0:T(8,128)}, f32[4,2,64,128]{3,2,1,0:T(8,128)}, u32[]{:S(2)}, u32[]{:S(2)}) %collective-permute-start.5) | collective-permute-done | bytes 262176 | tf_op jit(solution)/shard_map/ppermute | solution.py:15
  109.1 1.0 constant_dynamic-update-slice_fusion.10
  110.1 1.1 slice_dynamic-update-slice_fusion.1
  111.2 1.1 constant_dynamic-update-slice_fusion.9
  112.2 1.3 collective-permute-done.7
  127.3 1.6 %fusion.135 = (f32[1,2,64,128]{3,2,1,0:T(8,128)}, f32[2,64,128]{2,1,0:T(8,128)}) fusion(f32[8,2,64,128]{3,2,1,0:T(8,128)} %collective-permute-done.4, f32[2,64,128]{2,1,0:T(8,128)S(1)} %maximum_add_fusion.90, f32[2,1,128]{2,1,0:T(1,128)S(1)} %slice.2023, f32[2,63,128]{2,1,0:T(8,128)S(1)} %slice.2022, f32[2,64,128]{2,1,0:T(8,128)S(1)} %maximum_add_fusion.92, ...), kind=kLoop, calls=%fused_computation.361 | loop fusion | flops 458752 | bytes 1245185 | tf_op jit(solution)/shard_map/broadcast_in_dim | solution.py:162
  (337 shorter events, 31.1 us)
Async XLA Ops:
  3.3 48.6 %copy-start.17 = (f32[1,2,64,128]{3,2,1,0:T(8,128)S(1)}, f32[1,2,64,128]{3,2,1,0:T(8,128)}, u32[]{:S(2)}) copy-start(f32[1,2,64,128]{3,2,1,0:T(8,128)} %param.6) | copy-start | bytes 196612
  3.3 48.6 %copy-start.18 = (f32[2,64,128]{2,1,0:T(8,128)S(1)}, f32[2,64,128]{2,1,0:T(8,128)}, u32[]{:S(2)}) copy-start(f32[2,64,128]{2,1,0:T(8,128)} %param.8) | copy-start | bytes 196612
  3.3 48.6 %copy-start.13 = (f32[1,3,2,64,128]{4,3,2,1,0:T(8,128)S(1)}, f32[1,3,2,64,128]{4,3,2,1,0:T(8,128)}, u32[]{:S(2)}) copy-start(f32[1,3,2,64,128]{4,3,2,1,0:T(8,128)} %param.7) | copy-start | bytes 589828
  5.1 46.8 %copy-start.14 = (f32[3,2,64,128]{3,2,1,0:T(8,128)S(1)}, f32[3,2,64,128]{3,2,1,0:T(8,128)}, u32[]{:S(2)}) copy-start(f32[3,2,64,128]{3,2,1,0:T(8,128)} %param.9) | copy-start | bytes 589828
  6.0 37.6 %collective-permute-start = (f32[10,2,64,128]{3,2,1,0:T(8,128)S(1)}, f32[10,2,64,128]{3,2,1,0:T(8,128)S(1)}, u32[]{:S(2)}, u32[]{:S(2)}) collective-permute-start(f32[10,2,64,128]{3,2,1,0:T(8,128)S(1)} %bitcast_dynamic-update-slice_fusion.3), channel_id=1, source_target_pairs={{0,4},{2,6},{4,8},{6,10},{8,12},{10,14},{12,16},{14,18},{16,20},{1... | collective-permute-start | bytes 1966088 | tf_op jit(solution)/shard_map/ppermute | solution.py:15
  9.1 42.6 %collective-permute-start.1 = (f32[10,2,64,128]{3,2,1,0:T(8,128)S(1)}, f32[10,2,64,128]{3,2,1,0:T(8,128)S(1)}, u32[]{:S(2)}, u32[]{:S(2)}) collective-permute-start(f32[10,2,64,128]{3,2,1,0:T(8,128)S(1)} %bitcast_dynamic-update-slice_fusion.3), channel_id=1, source_target_pairs={{0,2},{2,4},{4,6},{6,8},{8,10},{10,12},{12,14},{14,16},{16,18},{18... | collective-permute-start | bytes 1966088 | tf_op jit(solution)/shard_map/ppermute | solution.py:15
  13.2 38.8 %collective-permute-start.2 = (f32[10,2,64,128]{3,2,1,0:T(8,128)S(1)}, f32[10,2,64,128]{3,2,1,0:T(8,128)S(1)}, u32[]{:S(2)}, u32[]{:S(2)}) collective-permute-start(f32[10,2,64,128]{3,2,1,0:T(8,128)S(1)} %bitcast_dynamic-update-slice_fusion.3), channel_id=1, source_target_pairs={{2,0},{4,2},{6,4},{8,6},{10,8},{12,10},{14,12},{16,14},{18,16},{20... | collective-permute-start | bytes 1966088 | tf_op jit(solution)/shard_map/ppermute | solution.py:15
  15.1 37.0 %collective-permute-start.3 = (f32[10,2,64,128]{3,2,1,0:T(8,128)S(1)}, f32[10,2,64,128]{3,2,1,0:T(8,128)S(1)}, u32[]{:S(2)}, u32[]{:S(2)}) collective-permute-start(f32[10,2,64,128]{3,2,1,0:T(8,128)S(1)} %bitcast_dynamic-update-slice_fusion.3), channel_id=1, source_target_pairs={{4,0},{6,2},{8,4},{10,6},{12,8},{14,10},{16,12},{18,14},{20,16},{2... | collective-permute-start | bytes 1966088 | tf_op jit(solution)/shard_map/ppermute | solution.py:15
  19.0 33.0 %copy-start.8 = (f32[2,64,128]{2,1,0:T(8,128)S(1)}, f32[2,64,128]{2,1,0:T(8,128)}, u32[]{:S(2)}) copy-start(f32[2,64,128]{2,1,0:T(8,128)} %param.10) | copy-start | bytes 196612
  19.0 33.0 %copy-start.19 = (f32[2,64,128]{2,1,0:T(8,128)S(1)}, f32[2,64,128]{2,1,0:T(8,128)}, u32[]{:S(2)}) copy-start(f32[2,64,128]{2,1,0:T(8,128)} %param.11) | copy-start | bytes 196612
  53.5 1.2 copy-start.2
  69.4 13.5 %collective-permute-start.4 = (f32[8,2,64,128]{3,2,1,0:T(8,128)S(1)}, f32[8,2,64,128]{3,2,1,0:T(8,128)}, u32[]{:S(2)}, u32[]{:S(2)}) collective-permute-start(f32[8,2,64,128]{3,2,1,0:T(8,128)S(1)} %pad_maximum_fusion), channel_id=1, source_target_pairs={{0,1},{2,3},{4,5},{6,7},{8,9},{10,11},{12,13},{14,15},{16,17},{18,... | collective-permute-start | bytes 1572872 | tf_op jit(solution)/shard_map/ppermute | solution.py:15
  82.9 27.2 %collective-permute-start.6 = (f32[8,2,64,128]{3,2,1,0:T(8,128)}, f32[8,2,64,128]{3,2,1,0:T(8,128)}, u32[]{:S(2)}, u32[]{:S(2)}) collective-permute-start(f32[8,2,64,128]{3,2,1,0:T(8,128)} %collective-permute-done.4), channel_id=1, source_target_pairs={{0,2},{2,4},{4,6},{6,8},{8,10},{10,12},{12,14},{14,16},{16,18},{18... | collective-permute-start | bytes 1572872 | tf_op jit(solution)/shard_map/ppermute | solution.py:15
  86.6 22.5 %collective-permute-start.5 = (f32[4,2,64,128]{3,2,1,0:T(8,128)}, f32[4,2,64,128]{3,2,1,0:T(8,128)}, u32[]{:S(2)}, u32[]{:S(2)}) collective-permute-start(f32[4,2,64,128]{3,2,1,0:T(8,128)} %slice.1841), channel_id=1, source_target_pairs={{0,4},{2,6},{4,8},{6,10},{8,12},{10,14},{12,16},{14,18},{16,20},{1... | collective-permute-start | bytes 786440 | tf_op jit(solution)/shard_map/ppermute | solution.py:15
  93.6 21.9 %collective-permute-start.8 = (f32[4,2,64,128]{3,2,1,0:T(8,128)}, f32[4,2,64,128]{3,2,1,0:T(8,128)S(1)}, u32[]{:S(2)}, u32[]{:S(2)}) collective-permute-start(f32[4,2,64,128]{3,2,1,0:T(8,128)} %slice.1841), channel_id=1, source_target_pairs={{4,0},{6,2},{8,4},{10,6},{12,8},{14,10},{16,12},{18,14},{20,16},{2... | collective-permute-start | bytes 786440 | tf_op jit(solution)/shard_map/ppermute | solution.py:15
  95.5 18.0 %collective-permute-start.7 = (f32[8,2,64,128]{3,2,1,0:T(8,128)}, f32[8,2,64,128]{3,2,1,0:T(8,128)S(1)}, u32[]{:S(2)}, u32[]{:S(2)}) collective-permute-start(f32[8,2,64,128]{3,2,1,0:T(8,128)} %collective-permute-done.4), channel_id=1, source_target_pairs={{2,0},{4,2},{6,4},{8,6},{10,8},{12,10},{14,12},{16,14},{18,16},{20... | collective-permute-start | bytes 1572872 | tf_op jit(solution)/shard_map/ppermute | solution.py:15
  114.1 0.9 copy-start.16
  117.1 1.0 copy-start.3
  121.0 0.9 copy-start.12
  122.4 0.9 copy-start.5
  123.5 0.9 copy-start.15
  125.4 1.1 copy-start.1
  125.4 1.8 %copy-start.7 = (f32[2,2,64,128]{3,2,1,0:T(8,128)S(1)}, f32[2,2,64,128]{3,2,1,0:T(8,128)}, u32[]{:S(2)}) copy-start(f32[2,2,64,128]{3,2,1,0:T(8,128)} %copy-done.6) | copy-start | bytes 393220
  125.5 1.8 %copy-start.9 = (f32[2,64,128]{2,1,0:T(8,128)S(1)}, f32[2,64,128]{2,1,0:T(8,128)}, u32[]{:S(2)}) copy-start(f32[2,64,128]{2,1,0:T(8,128)} %param.10) | copy-start | bytes 196612
  (5 other events, 3.7 us)

commit v2 on v0

v2 whole, which is shorter than its diff:
```python
import jax
import jax.numpy as jnp
from jax import lax
from jax.sharding import PartitionSpec as P

STEPS = 4


DT_COARSE = 0.4


def from_behind(x, axis, by):
    size = lax.axis_size(axis)
    pairs = [(i, i + by) for i in range(size) if 0 <= i + by < size]
    return lax.ppermute(x, axis, pairs)


def neighbour_sum(values, offset, axis):
    return values + jnp.roll(values, offset, axis=axis)


def node_forces(pressure, lower_zones):
    combined = pressure + lower_zones
    force_x = 0.25 * (
        neighbour_sum(neighbour_sum(lower_zones, 1, -1), 1, -2)
        - neighbour_sum(neighbour_sum(pressure, 1, -1), 1, -2)
    )
    across_z = neighbour_sum(combined, 1, -1)
    force_y = 0.25 * (jnp.roll(across_z, 1, axis=-2) - across_z)
    across_y = neighbour_sum(combined, 1, -2)
    force_z = 0.25 * (jnp.roll(across_y, 1, axis=-1) - across_y)
    return jnp.stack([force_x, force_y, force_z], axis=-4)


def parts(velocity):
    return velocity[..., 0, :, :, :], velocity[..., 1, :, :, :], velocity[..., 2, :, :, :]


def zone_divergence(velocity, upper_nodes):
    v0, v1, v2 = parts(velocity)
    u0, u1, u2 = parts(upper_nodes)
    diff_x = neighbour_sum(neighbour_sum(u0 - v0, -1, -1), -1, -2)
    sum_y = neighbour_sum(v1 + u1, -1, -1)
    diff_y = jnp.roll(sum_y, -1, axis=-2) - sum_y
    sum_z = neighbour_sum(v2 + u2, -1, -2)
    diff_z = jnp.roll(sum_z, -1, axis=-1) - sum_z
    return 0.25 * (diff_x + diff_y + diff_z)


def upper_part(upper_nodes):
    u0, u1, u2 = parts(upper_nodes)
    diff_x = neighbour_sum(neighbour_sum(u0, -1, -1), -1, -2)
    sum_y = neighbour_sum(u1, -1, -1)
    diff_y = jnp.roll(sum_y, -1, axis=-2) - sum_y
    sum_z = neighbour_sum(u2, -1, -2)
    diff_z = jnp.roll(sum_z, -1, axis=-1) - sum_z
    return diff_x + diff_y + diff_z


def lower_part(velocity):
    v0, v1, v2 = parts(velocity)
    diff_x = neighbour_sum(neighbour_sum(-v0, -1, -1), -1, -2)
    sum_y = neighbour_sum(v1, -1, -1)
    diff_y = jnp.roll(sum_y, -1, axis=-2) - sum_y
    sum_z = neighbour_sum(v2, -1, -2)
    diff_z = jnp.roll(sum_z, -1, axis=-1) - sum_z
    return diff_x + diff_y + diff_z


def advance(pressure, velocity, stiffness, inv_mass, next_mass, step_size):
    first = pressure[..., :1, :, :]
    last = pressure[..., -1:, :, :]
    empty = jnp.zeros_like(first)
    partial = velocity[..., :1, :, :] + step_size * inv_mass[:1] * node_forces(first, empty)
    from_left = from_behind(last, "space", 1)
    from_right = from_behind(upper_part(partial), "space", -1)
    lower_zones = jnp.concatenate([from_left, pressure[..., :-1, :, :]], axis=-3)
    forces = node_forces(pressure, lower_zones)
    velocity = velocity + step_size * inv_mass * forces
    inner = zone_divergence(velocity[..., :-1, :, :], velocity[..., 1:, :, :])
    own_share = upper_part(step_size * next_mass * node_forces(empty, last))
    edge = 0.25 * (lower_part(velocity[..., -1:, :, :]) + (from_right + own_share))
    div = jnp.concatenate([inner, edge], axis=-3)
    pressure = pressure - step_size * stiffness * div
    return pressure, velocity


def propagate(pressure, velocity, stiffness, inv_mass, next_mass):
    fine_size = DT_COARSE / STEPS
    for repeat in range(STEPS):
        pressure, velocity = advance(pressure, velocity, stiffness, inv_mass, next_mass, fine_size)
    return pressure, velocity


def on_device(
    guess_pressure, guess_velocity, initial_pressure, initial_velocity, stiffness, inv_mass
):
    groups = lax.axis_size("tm")
    group = lax.axis_index("tm")
    next_mass = from_behind(inv_mass[:1], "space", -1)

    both_p = jnp.stack([guess_pressure[0], initial_pressure])
    both_v = jnp.stack([guess_velocity[0], initial_velocity])
    first_p, first_v = propagate(both_p, both_v, stiffness, inv_mass, next_mass)
    relaxed_p, relaxed_v = first_p[0], first_v[0]
    own_end_p, own_end_v = first_p[1], first_v[1]

    shifted_p, shifted_v = from_behind((relaxed_p, relaxed_v), "tm", 1)
    late_p, late_v = propagate(shifted_p, shifted_v, stiffness, inv_mass, next_mass)
    first_group = group == 0
    end_p = jnp.where(first_group, own_end_p, late_p)
    end_v = jnp.where(first_group, own_end_v, late_v)
    resid_p = end_p - relaxed_p
    resid_v = end_v - relaxed_v

    if groups == 2:
        early_p = own_end_p - relaxed_p
        early_v = own_end_v - relaxed_v
        carried_p, carried_v = from_behind((early_p, early_v), "tm", 1)
        moved_p, moved_v = advance(carried_p, carried_v, stiffness, inv_mass, next_mass, DT_COARSE)
        error_p = resid_p + moved_p
        error_v = resid_v + moved_v
    else:
        error_p, error_v = resid_p, resid_v
        carried_p, carried_v = resid_p, resid_v
        for repeat in range(groups - 1):
            carried_p, carried_v = from_behind((carried_p, carried_v), "tm", 1)
            carried_p, carried_v = advance(
                carried_p, carried_v, stiffness, inv_mass, next_mass, DT_COARSE
            )
            error_p = error_p + carried_p
            error_v = error_v + carried_v
    corrected_p = relaxed_p + error_p
    corrected_v = relaxed_v + error_v
    return (corrected_p[None], corrected_v[None], resid_p[None], resid_v[None])


def solution(mesh):
    placed = (
        P("tm", "space", None, None),
        P("tm", None, "space", None, None),
        P("space", None, None),
        P(None, "space", None, None),
        P("space", None, None),
        P("space", None, None),
    )
    return jax.shard_map(
        on_device,
        mesh=mesh,
        in_specs=placed,
        out_specs=(
            P("tm", "space", None, None),
            P("tm", None, "space", None, None),
            P("tm", "space", None, None),
            P("tm", None, "space", None, None),
        ),
        check_vma=False,
    )
```

time: 136 us -> 180 us (1.32)
  local copies, waits for them, and re-layouts: 10.9 us -> 61 us
  waiting for transfers between devices: 65.8 us -> 19.9 us
  other arithmetic: 9.99 us -> 33.6 us
  starting transfers between devices: 45.3 us -> 58.6 us
  between operations: 2.66 us -> 5.28 us
    ppermute x22 -> x23, waiting for transfers between devices: 65.8 us -> 19.9 us  [from_behind(): return lax.ppermute(x, axis, pairs)]
    concatenate x6 -> x62, local copies, waits for them, and re-layouts: 0.1 us -> 15.7 us  [neighbour_sum(): return values + jnp.roll(values, offset, axis=axis)]
    ppermute x22 -> x23, starting transfers between devices: 45.3 us -> 58.6 us  [from_behind(): return lax.ppermute(x, axis, pairs)]
    unnamed x16 -> x110, local copies, waits for them, and re-layouts: 3.18 us -> 14.2 us
    mul x0 -> x37, other arithmetic: none -> 9.27 us  [the longest x9 3.43 us: advance(): 0.25 * (lower_part(velocity[..., -1:, :, :]) + (from_right + own_share))]
    slice x157 -> x299, local copies, waits for them, and re-layouts: 4.53 us -> 13.6 us  [neighbour_sum(): return values + jnp.roll(values, offset, axis=axis)]
    slice x10 -> x84, local copies, waits for them, and re-layouts: 0.9 us -> 7.96 us  [the longest x36 3.81 us: upper_part(): diff_y = jnp.roll(sum_y, -1, axis=-2) - sum_y]
    add x54 -> x81, other arithmetic: 4.43 us -> 10.1 us  [neighbour_sum(): return values + jnp.roll(values, offset, axis=axis)]
  transfers between devices with their start and end apart: 22 -> 23, of which waited for: 20 -> 8; matrix products, arithmetic and copies ran while one was open for 3% -> 37% of each run, Pallas kernels for 0% -> 0%
where the time goes in v2:
time: 180 us; the launch traced here: 178 us
  local copies, waits for them, and re-layouts  61 us (34%)
  starting transfers between devices  58.6 us (33%)
  other arithmetic  33.6 us (19%)
  waiting for transfers between devices  19.9 us (11%)
  between operations  5.28 us (3%)
    ppermute x23, starting transfers between devices, from_behind(): return lax.ppermute(x, axis, pairs)  58.6 us
    ppermute x23, waiting for transfers between devices, from_behind(): return lax.ppermute(x, axis, pairs)  19.9 us
    concatenate x62, local copies, waits for them, and re-layouts, neighbour_sum(): return values + jnp.roll(values, offset, axis=axis)  15.7 us
    unnamed x110, local copies, waits for them, and re-layouts  14.2 us
    slice x299, local copies, waits for them, and re-layouts, neighbour_sum(): return values + jnp.roll(values, offset, axis=axis)  13.6 us
    add x81, other arithmetic, neighbour_sum(): return values + jnp.roll(values, offset, axis=axis)  10.1 us
    slice x36, local copies, waits for them, and re-layouts, upper_part(): diff_y = jnp.roll(sum_y, -1, axis=-2) - sum_y  3.81 us
  transfers between devices with their start and end apart: 23, of which 8 were waited for; matrix products, arithmetic and copies ran while one was open for 37% of the time, Pallas kernels for 0%

profile of v2, /device:TPU:7, one launch (start us, length us, event | category | flops | bytes accessed | tf_op | source)
XLA Modules:
  0.0 178.3 jit_solution(1881360692080863907)
XLA Ops:
  2.1 2.6 %collective-permute-start.2 = (f32[1,64,128]{2,1,0:T(8,128)S(1)}, f32[1,64,128]{2,1,0:T(8,128)S(1)}, u32[]{:S(2)}, u32[]{:S(2)}) collective-permute-start(f32[1,64,128]{2,1,0:T(8,128)S(1)} %get-tuple-element.386), channel_id=1, source_target_pairs={{2,0},{4,2},{6,4},{8,6},{10,8},{12,10},{14,12},{16,14},{18,16},{20... | collective-permute-start | bytes 98312 | tf_op jit(solution)/shard_map/ppermute | solution.py:15
  4.9 3.9 %collective-permute-start = (f32[2,1,64,128]{3,2,0,1:T(8,128)S(1)}, f32[2,1,64,128]{3,2,0,1:T(8,128)S(1)}, u32[]{:S(2)}, u32[]{:S(2)}) collective-permute-start(f32[2,1,64,128]{3,2,0,1:T(8,128)S(1)} %get-tuple-element.17), channel_id=1, source_target_pairs={{0,2},{2,4},{4,6},{6,8},{8,10},{10,12},{12,14},{14,16},{16,18},{18... | collective-permute-start | bytes 196616 | tf_op jit(solution)/shard_map/ppermute | solution.py:15
  10.6 1.9 %collective-permute-start.1 = (f32[2,1,64,128]{3,2,0,1:T(8,128)S(1)}, f32[2,1,64,128]{3,2,0,1:T(8,128)S(1)}, u32[]{:S(2)}, u32[]{:S(2)}) collective-permute-start(f32[2,1,64,128]{3,2,0,1:T(8,128)S(1)} %fusion.92), channel_id=1, source_target_pairs={{2,0},{4,2},{6,4},{8,6},{10,8},{12,10},{14,12},{16,14},{18,16},{20... | collective-permute-start | bytes 196616 | tf_op jit(solution)/shard_map/ppermute | solution.py:15
  21.0 4.5 %collective-permute-start.3 = (f32[2,1,64,128]{3,2,0,1:T(8,128)S(1)}, f32[2,1,64,128]{3,2,0,1:T(8,128)S(1)}, u32[]{:S(2)}, u32[]{:S(2)}) collective-permute-start(f32[2,1,64,128]{3,2,0,1:T(8,128)S(1)} %get-tuple-element.233), channel_id=1, source_target_pairs={{0,2},{2,4},{4,6},{6,8},{8,10},{10,12},{12,14},{14,16},{16,18},{18... | collective-permute-start | bytes 196616 | tf_op jit(solution)/shard_map/ppermute | solution.py:15
  30.2 1.9 %collective-permute-start.4 = (f32[2,1,64,128]{3,2,0,1:T(8,128)}, f32[2,1,64,128]{3,2,0,1:T(8,128)}, u32[]{:S(2)}, u32[]{:S(2)}) collective-permute-start(f32[2,1,64,128]{3,2,0,1:T(8,128)} %fusion.112), channel_id=1, source_target_pairs={{2,0},{4,2},{6,4},{8,6},{10,8},{12,10},{14,12},{16,14},{18,16},{20... | collective-permute-start | bytes 196616 | tf_op jit(solution)/shard_map/ppermute | solution.py:15
  40.0 4.5 %collective-permute-start.5 = (f32[2,1,64,128]{3,2,0,1:T(8,128)S(1)}, f32[2,1,64,128]{3,2,0,1:T(8,128)S(1)}, u32[]{:S(2)}, u32[]{:S(2)}) collective-permute-start(f32[2,1,64,128]{3,2,0,1:T(8,128)S(1)} %get-tuple-element.205), channel_id=1, source_target_pairs={{0,2},{2,4},{4,6},{6,8},{8,10},{10,12},{12,14},{14,16},{16,18},{18... | collective-permute-start | bytes 196616 | tf_op jit(solution)/shard_map/ppermute | solution.py:15
  49.8 1.9 %collective-permute-start.6 = (f32[2,1,64,128]{3,2,0,1:T(8,128)}, f32[2,1,64,128]{3,2,0,1:T(8,128)}, u32[]{:S(2)}, u32[]{:S(2)}) collective-permute-start(f32[2,1,64,128]{3,2,0,1:T(8,128)} %fusion.132), channel_id=1, source_target_pairs={{2,0},{4,2},{6,4},{8,6},{10,8},{12,10},{14,12},{16,14},{18,16},{20... | collective-permute-start | bytes 196616 | tf_op jit(solution)/shard_map/ppermute | solution.py:15
  80.1 4.7 %collective-permute-start.7 = (f32[2,1,64,128]{3,2,0,1:T(8,128)}, f32[2,1,64,128]{3,2,0,1:T(8,128)S(1)}, u32[]{:S(2)}, u32[]{:S(2)}) collective-permute-start(f32[2,1,64,128]{3,2,0,1:T(8,128)} %get-tuple-element.177), channel_id=1, source_target_pairs={{0,2},{2,4},{4,6},{6,8},{8,10},{10,12},{12,14},{14,16},{16,18},{18... | collective-permute-start | bytes 196616 | tf_op jit(solution)/shard_map/ppermute | solution.py:15
  90.0 1.9 %collective-permute-start.8 = (f32[2,1,64,128]{3,2,0,1:T(8,128)}, f32[2,1,64,128]{3,2,0,1:T(8,128)}, u32[]{:S(2)}, u32[]{:S(2)}) collective-permute-start(f32[2,1,64,128]{3,2,0,1:T(8,128)} %fusion.151), channel_id=1, source_target_pairs={{2,0},{4,2},{6,4},{8,6},{10,8},{12,10},{14,12},{16,14},{18,16},{20... | collective-permute-start | bytes 196616 | tf_op jit(solution)/shard_map/ppermute | solution.py:15
  114.8 5.5 %collective-permute-start.11 = (f32[1,64,128]{2,1,0:T(8,128)S(1)}, f32[1,64,128]{2,1,0:T(8,128)S(1)}, u32[]{:S(2)}, u32[]{:S(2)}) collective-permute-start(f32[1,64,128]{2,1,0:T(8,128)S(1)} %get-tuple-element.442), channel_id=1, source_target_pairs={{0,2},{2,4},{4,6},{6,8},{8,10},{10,12},{12,14},{14,16},{16,18},{18... | collective-permute-start | bytes 98312 | tf_op jit(solution)/shard_map/ppermute | solution.py:15
  120.5 1.9 %collective-permute-start.21 = (f32[1,64,128]{2,1,0:T(8,128)S(1)}, f32[1,64,128]{2,1,0:T(8,128)S(1)}, u32[]{:S(2)}, u32[]{:S(2)}) collective-permute-start(f32[1,64,128]{2,1,0:T(8,128)S(1)} %get-tuple-element.375), channel_id=1, source_target_pairs={{0,2},{2,4},{4,6},{6,8},{8,10},{10,12},{12,14},{14,16},{16,18},{18... | collective-permute-start | bytes 98312 | tf_op jit(solution)/shard_map/ppermute | solution.py:15
  125.8 2.4 %collective-permute-start.12 = (f32[1,64,128]{2,1,0:T(8,128)S(1)}, f32[1,64,128]{2,1,0:T(8,128)S(1)}, u32[]{:S(2)}, u32[]{:S(2)}) collective-permute-start(f32[1,64,128]{2,1,0:T(8,128)S(1)} %fusion.235), channel_id=1, source_target_pairs={{2,0},{4,2},{6,4},{8,6},{10,8},{12,10},{14,12},{16,14},{18,16},{20... | collective-permute-start | bytes 98312 | tf_op jit(solution)/shard_map/ppermute | solution.py:15
  128.5 3.9 %collective-permute-done.12 = f32[1,64,128]{2,1,0:T(8,128)S(1)} collective-permute-done((f32[1,64,128]{2,1,0:T(8,128)S(1)}, f32[1,64,128]{2,1,0:T(8,128)S(1)}, u32[]{:S(2)}, u32[]{:S(2)}) %collective-permute-start.12) | collective-permute-done | bytes 32800 | tf_op jit(solution)/shard_map/ppermute | solution.py:15
  133.5 1.9 %collective-permute-start.13 = (f32[1,64,128]{2,1,0:T(8,128)S(1)}, f32[1,64,128]{2,1,0:T(8,128)S(1)}, u32[]{:S(2)}, u32[]{:S(2)}) collective-permute-start(f32[1,64,128]{2,1,0:T(8,128)S(1)} %get-tuple-element.423), channel_id=1, source_target_pairs={{0,2},{2,4},{4,6},{6,8},{8,10},{10,12},{12,14},{14,16},{16,18},{18... | collective-permute-start | bytes 98312 | tf_op jit(solution)/shard_map/ppermute | solution.py:15
  135.9 2.4 %collective-permute-start.14 = (f32[1,64,128]{2,1,0:T(8,128)S(1)}, f32[1,64,128]{2,1,0:T(8,128)S(1)}, u32[]{:S(2)}, u32[]{:S(2)}) collective-permute-start(f32[1,64,128]{2,1,0:T(8,128)S(1)} %fusion.251), channel_id=1, source_target_pairs={{2,0},{4,2},{6,4},{8,6},{10,8},{12,10},{14,12},{16,14},{18,16},{20... | collective-permute-start | bytes 98312 | tf_op jit(solution)/shard_map/ppermute | solution.py:15
  140.1 2.0 %collective-permute-done.14 = f32[1,64,128]{2,1,0:T(8,128)S(1)} collective-permute-done((f32[1,64,128]{2,1,0:T(8,128)S(1)}, f32[1,64,128]{2,1,0:T(8,128)S(1)}, u32[]{:S(2)}, u32[]{:S(2)}) %collective-permute-start.14) | collective-permute-done | bytes 32800 | tf_op jit(solution)/shard_map/ppermute | solution.py:15
  143.2 2.1 %collective-permute-start.15 = (f32[1,64,128]{2,1,0:T(8,128)S(1)}, f32[1,64,128]{2,1,0:T(8,128)S(1)}, u32[]{:S(2)}, u32[]{:S(2)}) collective-permute-start(f32[1,64,128]{2,1,0:T(8,128)S(1)} %get-tuple-element.404), channel_id=1, source_target_pairs={{0,2},{2,4},{4,6},{6,8},{8,10},{10,12},{12,14},{14,16},{16,18},{18... | collective-permute-start | bytes 98312 | tf_op jit(solution)/shard_map/ppermute | solution.py:15
  145.8 2.2 %collective-permute-start.16 = (f32[1,64,128]{2,1,0:T(8,128)S(1)}, f32[1,64,128]{2,1,0:T(8,128)S(1)}, u32[]{:S(2)}, u32[]{:S(2)}) collective-permute-start(f32[1,64,128]{2,1,0:T(8,128)S(1)} %fusion.267), channel_id=1, source_target_pairs={{2,0},{4,2},{6,4},{8,6},{10,8},{12,10},{14,12},{16,14},{18,16},{20... | collective-permute-start | bytes 98312 | tf_op jit(solution)/shard_map/ppermute | solution.py:15
  149.8 2.1 %collective-permute-done.16 = f32[1,64,128]{2,1,0:T(8,128)S(1)} collective-permute-done((f32[1,64,128]{2,1,0:T(8,128)S(1)}, f32[1,64,128]{2,1,0:T(8,128)S(1)}, u32[]{:S(2)}, u32[]{:S(2)}) %collective-permute-start.16) | collective-permute-done | bytes 32800 | tf_op jit(solution)/shard_map/ppermute | solution.py:15
  153.1 2.1 %collective-permute-start.17 = (f32[1,64,128]{2,1,0:T(8,128)S(1)}, f32[1,64,128]{2,1,0:T(8,128)S(1)}, u32[]{:S(2)}, u32[]{:S(2)}) collective-permute-start(f32[1,64,128]{2,1,0:T(8,128)S(1)} %get-tuple-element.361), channel_id=1, source_target_pairs={{0,2},{2,4},{4,6},{6,8},{8,10},{10,12},{12,14},{14,16},{16,18},{18... | collective-permute-start | bytes 98312 | tf_op jit(solution)/shard_map/ppermute | solution.py:15
  155.8 2.2 %collective-permute-start.18 = (f32[1,64,128]{2,1,0:T(8,128)S(1)}, f32[1,64,128]{2,1,0:T(8,128)S(1)}, u32[]{:S(2)}, u32[]{:S(2)}) collective-permute-start(f32[1,64,128]{2,1,0:T(8,128)S(1)} %fusion.283), channel_id=1, source_target_pairs={{2,0},{4,2},{6,4},{8,6},{10,8},{12,10},{14,12},{16,14},{18,16},{20... | collective-permute-start | bytes 98312 | tf_op jit(solution)/shard_map/ppermute | solution.py:15
  162.1 6.6 %collective-permute-done.20 = f32[3,2,64,128]{3,2,1,0:T(8,128)S(1)} collective-permute-done((f32[3,2,64,128]{3,2,1,0:T(8,128)S(1)}, f32[3,2,64,128]{3,2,1,0:T(8,128)S(1)}, u32[]{:S(2)}, u32[]{:S(2)}) %collective-permute-start.20) | collective-permute-done | bytes 196640 | tf_op jit(solution)/shard_map/ppermute | solution.py:15
  171.4 2.8 %collective-permute-start.22 = (f32[1,64,128]{2,1,0:T(8,128)S(1)}, f32[1,64,128]{2,1,0:T(8,128)S(1)}, u32[]{:S(2)}, u32[]{:S(2)}) collective-permute-start(f32[1,64,128]{2,1,0:T(8,128)S(1)} %fusion.299), channel_id=1, source_target_pairs={{2,0},{4,2},{6,4},{8,6},{10,8},{12,10},{14,12},{16,14},{18,16},{20... | collective-permute-start | bytes 98312 | tf_op jit(solution)/shard_map/ppermute | solution.py:15
  174.5 3.0 %collective-permute-done.22 = f32[1,64,128]{2,1,0:T(8,128)S(1)} collective-permute-done((f32[1,64,128]{2,1,0:T(8,128)S(1)}, f32[1,64,128]{2,1,0:T(8,128)S(1)}, u32[]{:S(2)}, u32[]{:S(2)}) %collective-permute-start.22) | collective-permute-done | bytes 32800 | tf_op jit(solution)/shard_map/ppermute | solution.py:15
  (941 shorter events, 102.0 us)
Async XLA Ops:
  2.1 12.7 %collective-permute-start.2 = (f32[1,64,128]{2,1,0:T(8,128)S(1)}, f32[1,64,128]{2,1,0:T(8,128)S(1)}, u32[]{:S(2)}, u32[]{:S(2)}) collective-permute-start(f32[1,64,128]{2,1,0:T(8,128)S(1)} %get-tuple-element.386), channel_id=1, source_target_pairs={{2,0},{4,2},{6,4},{8,6},{10,8},{12,10},{14,12},{16,14},{18,16},{20... | collective-permute-start | bytes 98312 | tf_op jit(solution)/shard_map/ppermute | solution.py:15
  4.9 11.0 %collective-permute-start = (f32[2,1,64,128]{3,2,0,1:T(8,128)S(1)}, f32[2,1,64,128]{3,2,0,1:T(8,128)S(1)}, u32[]{:S(2)}, u32[]{:S(2)}) collective-permute-start(f32[2,1,64,128]{3,2,0,1:T(8,128)S(1)} %get-tuple-element.17), channel_id=1, source_target_pairs={{0,2},{2,4},{4,6},{6,8},{8,10},{10,12},{12,14},{14,16},{16,18},{18... | collective-permute-start | bytes 196616 | tf_op jit(solution)/shard_map/ppermute | solution.py:15
  10.6 9.1 %collective-permute-start.1 = (f32[2,1,64,128]{3,2,0,1:T(8,128)S(1)}, f32[2,1,64,128]{3,2,0,1:T(8,128)S(1)}, u32[]{:S(2)}, u32[]{:S(2)}) collective-permute-start(f32[2,1,64,128]{3,2,0,1:T(8,128)S(1)} %fusion.92), channel_id=1, source_target_pairs={{2,0},{4,2},{6,4},{8,6},{10,8},{12,10},{14,12},{16,14},{18,16},{20... | collective-permute-start | bytes 196616 | tf_op jit(solution)/shard_map/ppermute | solution.py:15
  21.0 11.1 %collective-permute-start.3 = (f32[2,1,64,128]{3,2,0,1:T(8,128)S(1)}, f32[2,1,64,128]{3,2,0,1:T(8,128)S(1)}, u32[]{:S(2)}, u32[]{:S(2)}) collective-permute-start(f32[2,1,64,128]{3,2,0,1:T(8,128)S(1)} %get-tuple-element.233), channel_id=1, source_target_pairs={{0,2},{2,4},{4,6},{6,8},{8,10},{10,12},{12,14},{14,16},{16,18},{18... | collective-permute-start | bytes 196616 | tf_op jit(solution)/shard_map/ppermute | solution.py:15
  30.2 6.9 %collective-permute-start.4 = (f32[2,1,64,128]{3,2,0,1:T(8,128)}, f32[2,1,64,128]{3,2,0,1:T(8,128)}, u32[]{:S(2)}, u32[]{:S(2)}) collective-permute-start(f32[2,1,64,128]{3,2,0,1:T(8,128)} %fusion.112), channel_id=1, source_target_pairs={{2,0},{4,2},{6,4},{8,6},{10,8},{12,10},{14,12},{16,14},{18,16},{20... | collective-permute-start | bytes 196616 | tf_op jit(solution)/shard_map/ppermute | solution.py:15
  40.0 11.7 %collective-permute-start.5 = (f32[2,1,64,128]{3,2,0,1:T(8,128)S(1)}, f32[2,1,64,128]{3,2,0,1:T(8,128)S(1)}, u32[]{:S(2)}, u32[]{:S(2)}) collective-permute-start(f32[2,1,64,128]{3,2,0,1:T(8,128)S(1)} %get-tuple-element.205), channel_id=1, source_target_pairs={{0,2},{2,4},{4,6},{6,8},{8,10},{10,12},{12,14},{14,16},{16,18},{18... | collective-permute-start | bytes 196616 | tf_op jit(solution)/shard_map/ppermute | solution.py:15
  49.8 26.7 %collective-permute-start.6 = (f32[2,1,64,128]{3,2,0,1:T(8,128)}, f32[2,1,64,128]{3,2,0,1:T(8,128)}, u32[]{:S(2)}, u32[]{:S(2)}) collective-permute-start(f32[2,1,64,128]{3,2,0,1:T(8,128)} %fusion.132), channel_id=1, source_target_pairs={{2,0},{4,2},{6,4},{8,6},{10,8},{12,10},{14,12},{16,14},{18,16},{20... | collective-permute-start | bytes 196616 | tf_op jit(solution)/shard_map/ppermute | solution.py:15
  80.1 11.8 %collective-permute-start.7 = (f32[2,1,64,128]{3,2,0,1:T(8,128)}, f32[2,1,64,128]{3,2,0,1:T(8,128)S(1)}, u32[]{:S(2)}, u32[]{:S(2)}) collective-permute-start(f32[2,1,64,128]{3,2,0,1:T(8,128)} %get-tuple-element.177), channel_id=1, source_target_pairs={{0,2},{2,4},{4,6},{6,8},{8,10},{10,12},{12,14},{14,16},{16,18},{18... | collective-permute-start | bytes 196616 | tf_op jit(solution)/shard_map/ppermute | solution.py:15
  90.0 15.2 %collective-permute-start.8 = (f32[2,1,64,128]{3,2,0,1:T(8,128)}, f32[2,1,64,128]{3,2,0,1:T(8,128)}, u32[]{:S(2)}, u32[]{:S(2)}) collective-permute-start(f32[2,1,64,128]{3,2,0,1:T(8,128)} %fusion.151), channel_id=1, source_target_pairs={{2,0},{4,2},{6,4},{8,6},{10,8},{12,10},{14,12},{16,14},{18,16},{20... | collective-permute-start | bytes 196616 | tf_op jit(solution)/shard_map/ppermute | solution.py:15
  107.0 5.8 %collective-permute-start.19 = (f32[2,64,128]{2,1,0:T(8,128)S(1)}, f32[2,64,128]{2,1,0:T(8,128)S(1)}, u32[]{:S(2)}, u32[]{:S(2)}) collective-permute-start(f32[2,64,128]{2,1,0:T(8,128)S(1)} %fusion.204), channel_id=1, source_target_pairs={{0,1},{2,3},{4,5},{6,7},{8,9},{10,11},{12,13},{14,15},{16,17},{18,... | collective-permute-start | bytes 196616 | tf_op jit(solution)/shard_map/ppermute | solution.py:15
  108.3 6.0 %collective-permute-start.9 = (f32[2,64,128]{2,1,0:T(8,128)S(1)}, f32[2,64,128]{2,1,0:T(8,128)S(1)}, u32[]{:S(2)}, u32[]{:S(2)}) collective-permute-start(f32[2,64,128]{2,1,0:T(8,128)S(1)} %slice_bitcast_fusion.19), channel_id=1, source_target_pairs={{0,1},{2,3},{4,5},{6,7},{8,9},{10,11},{12,13},{14,15},{16,17},{18,... | collective-permute-start | bytes 196616 | tf_op jit(solution)/shard_map/ppermute | solution.py:15
  109.6 15.0 %collective-permute-start.10 = (f32[3,2,64,128]{3,2,1,0:T(8,128)S(1)}, f32[3,2,64,128]{3,2,1,0:T(8,128)S(1)}, u32[]{:S(2)}, u32[]{:S(2)}) collective-permute-start(f32[3,2,64,128]{3,2,1,0:T(8,128)S(1)} %slice_bitcast_fusion.1), channel_id=1, source_target_pairs={{0,1},{2,3},{4,5},{6,7},{8,9},{10,11},{12,13},{14,15},{16,17},{18,... | collective-permute-start | bytes 589832 | tf_op jit(solution)/shard_map/ppermute | solution.py:15
  114.8 8.3 %collective-permute-start.11 = (f32[1,64,128]{2,1,0:T(8,128)S(1)}, f32[1,64,128]{2,1,0:T(8,128)S(1)}, u32[]{:S(2)}, u32[]{:S(2)}) collective-permute-start(f32[1,64,128]{2,1,0:T(8,128)S(1)} %get-tuple-element.442), channel_id=1, source_target_pairs={{0,2},{2,4},{4,6},{6,8},{8,10},{10,12},{12,14},{14,16},{16,18},{18... | collective-permute-start | bytes 98312 | tf_op jit(solution)/shard_map/ppermute | solution.py:15
  120.5 3.1 %collective-permute-start.21 = (f32[1,64,128]{2,1,0:T(8,128)S(1)}, f32[1,64,128]{2,1,0:T(8,128)S(1)}, u32[]{:S(2)}, u32[]{:S(2)}) collective-permute-start(f32[1,64,128]{2,1,0:T(8,128)S(1)} %get-tuple-element.375), channel_id=1, source_target_pairs={{0,2},{2,4},{4,6},{6,8},{8,10},{10,12},{12,14},{14,16},{16,18},{18... | collective-permute-start | bytes 98312 | tf_op jit(solution)/shard_map/ppermute | solution.py:15
  125.8 6.5 %collective-permute-start.12 = (f32[1,64,128]{2,1,0:T(8,128)S(1)}, f32[1,64,128]{2,1,0:T(8,128)S(1)}, u32[]{:S(2)}, u32[]{:S(2)}) collective-permute-start(f32[1,64,128]{2,1,0:T(8,128)S(1)} %fusion.235), channel_id=1, source_target_pairs={{2,0},{4,2},{6,4},{8,6},{10,8},{12,10},{14,12},{16,14},{18,16},{20... | collective-permute-start | bytes 98312 | tf_op jit(solution)/shard_map/ppermute | solution.py:15
  133.5 5.0 %collective-permute-start.13 = (f32[1,64,128]{2,1,0:T(8,128)S(1)}, f32[1,64,128]{2,1,0:T(8,128)S(1)}, u32[]{:S(2)}, u32[]{:S(2)}) collective-permute-start(f32[1,64,128]{2,1,0:T(8,128)S(1)} %get-tuple-element.423), channel_id=1, source_target_pairs={{0,2},{2,4},{4,6},{6,8},{8,10},{10,12},{12,14},{14,16},{16,18},{18... | collective-permute-start | bytes 98312 | tf_op jit(solution)/shard_map/ppermute | solution.py:15
  135.9 6.1 %collective-permute-start.14 = (f32[1,64,128]{2,1,0:T(8,128)S(1)}, f32[1,64,128]{2,1,0:T(8,128)S(1)}, u32[]{:S(2)}, u32[]{:S(2)}) collective-permute-start(f32[1,64,128]{2,1,0:T(8,128)S(1)} %fusion.251), channel_id=1, source_target_pairs={{2,0},{4,2},{6,4},{8,6},{10,8},{12,10},{14,12},{16,14},{18,16},{20... | collective-permute-start | bytes 98312 | tf_op jit(solution)/shard_map/ppermute | solution.py:15
  143.2 5.0 %collective-permute-start.15 = (f32[1,64,128]{2,1,0:T(8,128)S(1)}, f32[1,64,128]{2,1,0:T(8,128)S(1)}, u32[]{:S(2)}, u32[]{:S(2)}) collective-permute-start(f32[1,64,128]{2,1,0:T(8,128)S(1)} %get-tuple-element.404), channel_id=1, source_target_pairs={{0,2},{2,4},{4,6},{6,8},{8,10},{10,12},{12,14},{14,16},{16,18},{18... | collective-permute-start | bytes 98312 | tf_op jit(solution)/shard_map/ppermute | solution.py:15
  145.8 6.1 %collective-permute-start.16 = (f32[1,64,128]{2,1,0:T(8,128)S(1)}, f32[1,64,128]{2,1,0:T(8,128)S(1)}, u32[]{:S(2)}, u32[]{:S(2)}) collective-permute-start(f32[1,64,128]{2,1,0:T(8,128)S(1)} %fusion.267), channel_id=1, source_target_pairs={{2,0},{4,2},{6,4},{8,6},{10,8},{12,10},{14,12},{16,14},{18,16},{20... | collective-permute-start | bytes 98312 | tf_op jit(solution)/shard_map/ppermute | solution.py:15
  153.1 5.0 %collective-permute-start.17 = (f32[1,64,128]{2,1,0:T(8,128)S(1)}, f32[1,64,128]{2,1,0:T(8,128)S(1)}, u32[]{:S(2)}, u32[]{:S(2)}) collective-permute-start(f32[1,64,128]{2,1,0:T(8,128)S(1)} %get-tuple-element.361), channel_id=1, source_target_pairs={{0,2},{2,4},{4,6},{6,8},{8,10},{10,12},{12,14},{14,16},{16,18},{18... | collective-permute-start | bytes 98312 | tf_op jit(solution)/shard_map/ppermute | solution.py:15
  155.8 6.1 %collective-permute-start.18 = (f32[1,64,128]{2,1,0:T(8,128)S(1)}, f32[1,64,128]{2,1,0:T(8,128)S(1)}, u32[]{:S(2)}, u32[]{:S(2)}) collective-permute-start(f32[1,64,128]{2,1,0:T(8,128)S(1)} %fusion.283), channel_id=1, source_target_pairs={{2,0},{4,2},{6,4},{8,6},{10,8},{12,10},{14,12},{16,14},{18,16},{20... | collective-permute-start | bytes 98312 | tf_op jit(solution)/shard_map/ppermute | solution.py:15
  160.4 8.3 %collective-permute-start.20 = (f32[3,2,64,128]{3,2,1,0:T(8,128)S(1)}, f32[3,2,64,128]{3,2,1,0:T(8,128)S(1)}, u32[]{:S(2)}, u32[]{:S(2)}) collective-permute-start(f32[3,2,64,128]{3,2,1,0:T(8,128)S(1)} %get-tuple-element.20), channel_id=1, source_target_pairs={{0,1},{2,3},{4,5},{6,7},{8,9},{10,11},{12,13},{14,15},{16,17},{18,... | collective-permute-start | bytes 589832 | tf_op jit(solution)/shard_map/ppermute | solution.py:15
  162.0 6.7 %copy-start.46 = (f32[64,128]{1,0:T(8,128)S(1)}, f32[64,128]{1,0:T(8,128)}, u32[]{:S(2)}) copy-start(f32[64,128]{1,0:T(8,128)} %get-tuple-element.384) | copy-start | bytes 98308
  171.4 6.1 %collective-permute-start.22 = (f32[1,64,128]{2,1,0:T(8,128)S(1)}, f32[1,64,128]{2,1,0:T(8,128)S(1)}, u32[]{:S(2)}, u32[]{:S(2)}) collective-permute-start(f32[1,64,128]{2,1,0:T(8,128)S(1)} %fusion.299), channel_id=1, source_target_pairs={{2,0},{4,2},{6,4},{8,6},{10,8},{12,10},{14,12},{16,14},{18,16},{20... | collective-permute-start | bytes 98312 | tf_op jit(solution)/shard_map/ppermute | solution.py:15
  (56 other events, 58.0 us)

commit v3 on v2

v3 whole, which is shorter than its diff:
```python
import functools

import jax
import jax.numpy as jnp
from jax import lax
from jax.experimental import pallas as pl
from jax.experimental.pallas import tpu as pltpu
from jax.sharding import PartitionSpec as P

STEPS = 4


DT_COARSE = 0.4


def from_behind(x, axis, by):
    size = lax.axis_size(axis)
    pairs = [(i, i + by) for i in range(size) if 0 <= i + by < size]
    return lax.ppermute(x, axis, pairs)


def roll(x, shift, axis):
    return pltpu.roll(x, shift % x.shape[axis], axis)


def nsum(values, offset, axis):
    return values + roll(values, offset, axis)


def forces(pressure, lower):
    combined = pressure + lower
    force_x = 0.25 * (nsum(nsum(lower, 1, 1), 1, 0) - nsum(nsum(pressure, 1, 1), 1, 0))
    across_z = nsum(combined, 1, 1)
    force_y = 0.25 * (roll(across_z, 1, 0) - across_z)
    across_y = nsum(combined, 1, 0)
    force_z = 0.25 * (roll(across_y, 1, 1) - across_y)
    return force_x, force_y, force_z


def divergence(v, u):
    diff_x = nsum(nsum(u[0] - v[0], -1, 1), -1, 0)
    sum_y = nsum(v[1] + u[1], -1, 1)
    diff_y = roll(sum_y, -1, 0) - sum_y
    sum_z = nsum(v[2] + u[2], -1, 0)
    diff_z = roll(sum_z, -1, 1) - sum_z
    return 0.25 * (diff_x + diff_y + diff_z)


def upper_part(u):
    diff_x = nsum(nsum(u[0], -1, 1), -1, 0)
    sum_y = nsum(u[1], -1, 1)
    diff_y = roll(sum_y, -1, 0) - sum_y
    sum_z = nsum(u[2], -1, 0)
    diff_z = roll(sum_z, -1, 1) - sum_z
    return diff_x + diff_y + diff_z


def lower_part(v):
    diff_x = nsum(nsum(-v[0], -1, 1), -1, 0)
    sum_y = nsum(v[1], -1, 1)
    diff_y = roll(sum_y, -1, 0) - sum_y
    sum_z = nsum(v[2], -1, 0)
    diff_z = roll(sum_z, -1, 1) - sum_z
    return diff_x + diff_y + diff_z


def outgoing(pressure_first, velocity_first, mass_first, step_size):
    f = forces(pressure_first, jnp.zeros_like(pressure_first))
    hm = step_size * mass_first
    return upper_part([velocity_first[c] + hm * f[c] for c in range(3)])


def step_kernel(step_size, next_size, p_ref, v_ref, k_ref, m_ref, mn_ref, left_ref, right_ref,
                p_out, v_out, last_out, part_out):
    batch, n = p_ref.shape[0], p_ref.shape[1]
    for b in range(batch):
        pres = [p_ref[b, i] for i in range(n)]
        lower = [left_ref[b, 0]] + pres[:-1]
        vel = []
        for i in range(n):
            f = forces(pres[i], lower[i])
            hm = step_size * m_ref[i]
            vel.append([v_ref[b, c, i] + hm * f[c] for c in range(3)])
        for i in range(n):
            for c in range(3):
                v_out[b, c, i] = vel[i][c]
        new_p = []
        for i in range(n - 1):
            new_p.append(pres[i] - step_size * k_ref[i] * divergence(vel[i], vel[i + 1]))
        zero = jnp.zeros_like(pres[-1])
        hm_next = step_size * mn_ref[0]
        own_share = upper_part([hm_next * f for f in forces(zero, pres[-1])])
        edge = 0.25 * (lower_part(vel[-1]) + (right_ref[b, 0] + own_share))
        new_p.append(pres[-1] - step_size * k_ref[n - 1] * edge)
        for i in range(n):
            p_out[b, i] = new_p[i]
        last_out[b, 0] = new_p[-1]
        part_out[b, 0] = outgoing(new_p[0], vel[0], m_ref[0], next_size)


def prep_kernel(step_size, p_ref, v_ref, m_ref, last_out, part_out):
    batch, n = p_ref.shape[0], p_ref.shape[1]
    for b in range(batch):
        last_out[b, 0] = p_ref[b, n - 1]
        part_out[b, 0] = outgoing(p_ref[b, 0], [v_ref[b, c, 0] for c in range(3)], m_ref[0], step_size)


def prep(pressure, velocity, inv_mass, step_size):
    plane = jax.ShapeDtypeStruct((pressure.shape[0], 1) + pressure.shape[2:], pressure.dtype)
    return pl.pallas_call(
        functools.partial(prep_kernel, step_size), out_shape=(plane, plane)
    )(pressure, velocity, inv_mass)


def advance(state, stiffness, inv_mass, next_mass, step_size, next_size):
    pressure, velocity, last, share = state
    from_left = from_behind(last, "space", 1)
    from_right = from_behind(share, "space", -1)
    plane = jax.ShapeDtypeStruct(last.shape, last.dtype)
    outs = (
        jax.ShapeDtypeStruct(pressure.shape, pressure.dtype),
        jax.ShapeDtypeStruct(velocity.shape, velocity.dtype),
        plane,
        plane,
    )
    return pl.pallas_call(
        functools.partial(step_kernel, step_size, next_size), out_shape=outs
    )(pressure, velocity, stiffness, inv_mass, next_mass, from_left, from_right)


def propagate(pressure, velocity, stiffness, inv_mass, next_mass, after):
    fine_size = DT_COARSE / STEPS
    last, share = prep(pressure, velocity, inv_mass, fine_size)
    state = (pressure, velocity, last, share)
    for repeat in range(STEPS):
        following = fine_size if repeat + 1 < STEPS else after
        state = advance(state, stiffness, inv_mass, next_mass, fine_size, following)
    return state


def coarse(pressure, velocity, stiffness, inv_mass, next_mass):
    last, share = prep(pressure, velocity, inv_mass, DT_COARSE)
    state = advance((pressure, velocity, last, share), stiffness, inv_mass, next_mass, DT_COARSE, DT_COARSE)
    return state[0][0], state[1][0]


def on_device(
    guess_pressure, guess_velocity, initial_pressure, initial_velocity, stiffness, inv_mass
):
    groups = lax.axis_size("tm")
    group = lax.axis_index("tm")
    next_mass = from_behind(inv_mass[:1], "space", -1)

    both_p = jnp.stack([guess_pressure[0], initial_pressure])
    both_v = jnp.stack([guess_velocity[0], initial_velocity])
    first_p, first_v, _, _ = propagate(both_p, both_v, stiffness, inv_mass, next_mass, DT_COARSE)
    relaxed_p, relaxed_v = first_p[0], first_v[0]
    own_end_p, own_end_v = first_p[1], first_v[1]

    shifted_p, shifted_v = from_behind((relaxed_p, relaxed_v), "tm", 1)
    late_p, late_v, _, _ = propagate(
        shifted_p[None], shifted_v[None], stiffness, inv_mass, next_mass, DT_COARSE
    )
    first_group = group == 0
    end_p = jnp.where(first_group, own_end_p, late_p[0])
    end_v = jnp.where(first_group, own_end_v, late_v[0])
    resid_p = end_p - relaxed_p
    resid_v = end_v - relaxed_v

    if groups == 2:
        early_p = own_end_p - relaxed_p
        early_v = own_end_v - relaxed_v
        carried_p, carried_v = from_behind((early_p, early_v), "tm", 1)
        moved_p, moved_v = coarse(carried_p[None], carried_v[None], stiffness, inv_mass, next_mass)
        error_p = resid_p + moved_p
        error_v = resid_v + moved_v
    else:
        error_p, error_v = resid_p, resid_v
        carried_p, carried_v = resid_p, resid_v
        for repeat in range(groups - 1):
            carried_p, carried_v = from_behind((carried_p, carried_v), "tm", 1)
            carried_p, carried_v = coarse(
                carried_p[None], carried_v[None], stiffness, inv_mass, next_mass
            )
            error_p = error_p + carried_p
            error_v = error_v + carried_v
    corrected_p = relaxed_p + error_p
    corrected_v = relaxed_v + error_v
    return (corrected_p[None], corrected_v[None], resid_p[None], resid_v[None])


def solution(mesh):
    placed = (
        P("tm", "space", None, None),
        P("tm", None, "space", None, None),
        P("space", None, None),
        P(None, "space", None, None),
        P("space", None, None),
        P("space", None, None),
    )
    return jax.shard_map(
        on_device,
        mesh=mesh,
        in_specs=placed,
        out_specs=(
            P("tm", "space", None, None),
            P("tm", None, "space", None, None),
            P("tm", "space", None, None),
            P("tm", None, "space", None, None),
        ),
        check_vma=False,
    )
```

time: 180 us -> 127 us (0.71)
  local copies, waits for them, and re-layouts: 61 us -> 10 us
  other arithmetic: 33.6 us -> 4.96 us
  Pallas kernels: 0 us -> 25.8 us
  waiting for transfers between devices: 19.9 us -> 30.3 us
  starting transfers between devices: 58.6 us -> 52.1 us
  between operations: 5.28 us -> 1.1 us
    pallas_call x0 -> x12, Pallas kernels: none -> 25.8 us  [the longest x9 20.3 us: advance(): pl.pallas_call(functools.partial(step_kernel, step_size, next_size), out_...]
    slice x437 -> x1, local copies, waits for them, and re-layouts: 24.6 us -> 0.01 us  [on_device(): next_mass = from_behind(inv_mass[:1], 'space', -1)]
    concatenate x90 -> x0, local copies, waits for them, and re-layouts: 21.9 us -> none  [the longest x62 15.7 us: neighbour_sum(): return values + jnp.roll(values, offset, axis=axis)]
    mul x42 -> x0, other arithmetic: 12.5 us -> none  [the longest x9 3.43 us: advance(): 0.25 * (lower_part(velocity[..., -1:, :, :]) + (from_right + own_share))]
    add x118 -> x2, other arithmetic: 14.6 us -> 2.43 us  [the longest x1 1.76 us: on_device(): corrected_v = relaxed_v + error_v]
    ppermute x23, waiting for transfers between devices: 19.9 us -> 30.3 us  [from_behind(): return lax.ppermute(x, axis, pairs)]
    ppermute x23, starting transfers between devices: 58.6 us -> 52.1 us  [from_behind(): return lax.ppermute(x, axis, pairs)]
    unnamed x110 -> x62, local copies, waits for them, and re-layouts: 14.2 us -> 8.15 us
  transfers between devices with their start and end apart: 23 -> 23, of which waited for: 8 -> 8; matrix products, arithmetic and copies ran while one was open for 37% -> 1% of each run, Pallas kernels for 0% -> 10%
where the time goes in v3:
time: 127 us; the launch traced here: 124 us
  starting transfers between devices  52.1 us (41%)
  waiting for transfers between devices  30.3 us (24%)
  Pallas kernels  25.8 us (20%)
  local copies, waits for them, and re-layouts  10 us (8%)
  other arithmetic  4.96 us (4%)
    ppermute x23, starting transfers between devices, from_behind(): return lax.ppermute(x, axis, pairs)  52.1 us
    ppermute x23, waiting for transfers between devices, from_behind(): return lax.ppermute(x, axis, pairs)  30.3 us
    pallas_call x9, Pallas kernels, advance(): pl.pallas_call(functools.partial(step_kernel, step_size, next_size), out_...  20.3 us
    unnamed x62, local copies, waits for them, and re-layouts  8.15 us
    pallas_call x3, Pallas kernels, prep(): pl.pallas_call(functools.partial(prep_kernel, step_size), out_shape=(plan...  5.47 us
  transfers between devices with their start and end apart: 23, of which 8 were waited for; matrix products, arithmetic and copies ran while one was open for 1% of the time, Pallas kernels for 10%

profile of v3, /device:TPU:7, one launch (start us, length us, event | category | flops | bytes accessed | tf_op | source)
XLA Modules:
  0.0 124.2 jit_solution(9702346279201090779)
XLA Ops:
  5.1 3.7 %collective-permute-start.1 = (f32[2,1,64,128]{3,2,1,0:T(8,128)}, f32[2,1,64,128]{3,2,1,0:T(8,128)S(1)}, u32[]{:S(2)}, u32[]{:S(2)}) collective-permute-start(f32[2,1,64,128]{3,2,1,0:T(8,128)} %get-tuple-element.40), channel_id=1, source_target_pairs={{0,2},{2,4},{4,6},{6,8},{8,10},{10,12},{12,14},{14,16},{16,18},{18... | collective-permute-start | bytes 196616 | tf_op jit(solution)/shard_map/ppermute | solution.py:19
  10.7 2.5 %collective-permute-start = (f32[1,64,128]{2,1,0:T(8,128)S(1)}, f32[1,64,128]{2,1,0:T(8,128)S(1)}, u32[]{:S(2)}, u32[]{:S(2)}) collective-permute-start(f32[1,64,128]{2,1,0:T(8,128)S(1)} %slice.15), channel_id=1, source_target_pairs={{2,0},{4,2},{6,4},{8,6},{10,8},{12,10},{14,12},{16,14},{18,16},{20... | collective-permute-start | bytes 98312 | tf_op jit(solution)/shard_map/ppermute | solution.py:19
  13.2 3.6 %collective-permute-done.mn_ref = f32[1,64,128]{2,1,0:T(8,128)S(1)} collective-permute-done((f32[1,64,128]{2,1,0:T(8,128)S(1)}, f32[1,64,128]{2,1,0:T(8,128)S(1)}, u32[]{:S(2)}, u32[]{:S(2)}) %collective-permute-start) | collective-permute-done | bytes 32800 | tf_op jit(solution)/shard_map/ppermute | solution.py:19
  18.1 2.5 %shard_map.94 = (f32[2,2,64,128]{3,2,1,0:T(8,128)}, f32[2,3,2,64,128]{4,3,2,1,0:T(8,128)}, f32[2,1,64,128]{3,2,1,0:T(8,128)}, f32[2,1,64,128]{3,2,1,0:T(8,128)}) custom-call(f32[2,2,64,128]{3,2,1,0:T(8,128)} %pad_maximum_fusion.1.p_ref, f32[2,3,2,64,128]{4,3,2,1,0:T(8,128)} %pad_maximum_fusion.v_ref, f32[2,64,128]{2,1,0:T(8,128)} %k_ref.17, ...), custom_call_target="tpu_custom_call" | custom-call | tf_op jit(solution)/shard_map/pallas_call | solution.py:126
  22.6 2.4 %collective-permute-start.4 = (f32[2,1,64,128]{3,2,1,0:T(8,128)}, f32[2,1,64,128]{3,2,1,0:T(8,128)S(1)}, u32[]{:S(2)}, u32[]{:S(2)}) collective-permute-start(f32[2,1,64,128]{3,2,1,0:T(8,128)} %get-tuple-element.45), channel_id=1, source_target_pairs={{2,0},{4,2},{6,4},{8,6},{10,8},{12,10},{14,12},{16,14},{18,16},{20... | collective-permute-start | bytes 196616 | tf_op jit(solution)/shard_map/ppermute | solution.py:19
  25.0 4.3 %collective-permute-done.4.right_ref = f32[2,1,64,128]{3,2,1,0:T(8,128)S(1)} collective-permute-done((f32[2,1,64,128]{3,2,1,0:T(8,128)}, f32[2,1,64,128]{3,2,1,0:T(8,128)S(1)}, u32[]{:S(2)}, u32[]{:S(2)}) %collective-permute-start.4) | collective-permute-done | bytes 65568 | tf_op jit(solution)/shard_map/ppermute | solution.py:19
  29.9 2.5 %shard_map.95 = (f32[2,2,64,128]{3,2,1,0:T(8,128)}, f32[2,3,2,64,128]{4,3,2,1,0:T(8,128)}, f32[2,1,64,128]{3,2,1,0:T(8,128)}, f32[2,1,64,128]{3,2,1,0:T(8,128)}) custom-call(f32[2,2,64,128]{3,2,1,0:T(8,128)} %get-tuple-element.42.p_ref, f32[2,3,2,64,128]{4,3,2,1,0:T(8,128)} %get-tuple-element.43.v_ref, f32[2,64,128]{2,1,0:T(8,128)} %k_ref.17, ...), custom_call_target="tpu_custom_call" | custom-call | tf_op jit(solution)/shard_map/pallas_call | solution.py:126
  34.3 2.4 %collective-permute-start.6 = (f32[2,1,64,128]{3,2,1,0:T(8,128)}, f32[2,1,64,128]{3,2,1,0:T(8,128)S(1)}, u32[]{:S(2)}, u32[]{:S(2)}) collective-permute-start(f32[2,1,64,128]{3,2,1,0:T(8,128)} %get-tuple-element.49), channel_id=1, source_target_pairs={{2,0},{4,2},{6,4},{8,6},{10,8},{12,10},{14,12},{16,14},{18,16},{20... | collective-permute-start | bytes 196616 | tf_op jit(solution)/shard_map/ppermute | solution.py:19
  36.7 4.3 %collective-permute-done.6.right_ref = f32[2,1,64,128]{3,2,1,0:T(8,128)S(1)} collective-permute-done((f32[2,1,64,128]{3,2,1,0:T(8,128)}, f32[2,1,64,128]{3,2,1,0:T(8,128)S(1)}, u32[]{:S(2)}, u32[]{:S(2)}) %collective-permute-start.6) | collective-permute-done | bytes 65568 | tf_op jit(solution)/shard_map/ppermute | solution.py:19
  41.7 2.5 %shard_map.96 = (f32[2,2,64,128]{3,2,1,0:T(8,128)}, f32[2,3,2,64,128]{4,3,2,1,0:T(8,128)}, f32[2,1,64,128]{3,2,1,0:T(8,128)}, f32[2,1,64,128]{3,2,1,0:T(8,128)}) custom-call(f32[2,2,64,128]{3,2,1,0:T(8,128)} %get-tuple-element.46.p_ref, f32[2,3,2,64,128]{4,3,2,1,0:T(8,128)} %get-tuple-element.47.v_ref, f32[2,64,128]{2,1,0:T(8,128)} %k_ref.17, ...), custom_call_target="tpu_custom_call" | custom-call | tf_op jit(solution)/shard_map/pallas_call | solution.py:126
  46.1 2.4 %collective-permute-start.8 = (f32[2,1,64,128]{3,2,1,0:T(8,128)}, f32[2,1,64,128]{3,2,1,0:T(8,128)S(1)}, u32[]{:S(2)}, u32[]{:S(2)}) collective-permute-start(f32[2,1,64,128]{3,2,1,0:T(8,128)} %get-tuple-element.53), channel_id=1, source_target_pairs={{2,0},{4,2},{6,4},{8,6},{10,8},{12,10},{14,12},{16,14},{18,16},{20... | collective-permute-start | bytes 196616 | tf_op jit(solution)/shard_map/ppermute | solution.py:19
  48.5 4.3 %collective-permute-done.8.right_ref = f32[2,1,64,128]{3,2,1,0:T(8,128)S(1)} collective-permute-done((f32[2,1,64,128]{3,2,1,0:T(8,128)}, f32[2,1,64,128]{3,2,1,0:T(8,128)S(1)}, u32[]{:S(2)}, u32[]{:S(2)}) %collective-permute-start.8) | collective-permute-done | bytes 65568 | tf_op jit(solution)/shard_map/ppermute | solution.py:19
  53.5 2.5 %shard_map.97 = (f32[2,2,64,128]{3,2,1,0:T(8,128)}, f32[2,3,2,64,128]{4,3,2,1,0:T(8,128)}, f32[2,1,64,128]{3,2,1,0:T(8,128)}, f32[2,1,64,128]{3,2,1,0:T(8,128)}) custom-call(f32[2,2,64,128]{3,2,1,0:T(8,128)} %get-tuple-element.50.p_ref, f32[2,3,2,64,128]{4,3,2,1,0:T(8,128)} %get-tuple-element.51.v_ref, f32[2,64,128]{2,1,0:T(8,128)} %k_ref.17, ...), custom_call_target="tpu_custom_call" | custom-call | tf_op jit(solution)/shard_map/pallas_call | solution.py:126
  61.7 5.4 %collective-permute-done.9 = f32[2,64,128]{2,1,0:T(8,128)S(1)} collective-permute-done((f32[2,64,128]{2,1,0:T(8,128)S(1)}, f32[2,64,128]{2,1,0:T(8,128)S(1)}, u32[]{:S(2)}, u32[]{:S(2)}) %collective-permute-start.9) | collective-permute-done | bytes 65568 | tf_op jit(solution)/shard_map/ppermute | solution.py:19
  69.7 2.8 %collective-permute-start.11 = (f32[1,1,64,128]{3,2,1,0:T(8,128)}, f32[1,1,64,128]{3,2,1,0:T(8,128)S(1)}, u32[]{:S(2)}, u32[]{:S(2)}) collective-permute-start(f32[1,1,64,128]{3,2,1,0:T(8,128)} %get-tuple-element.56), channel_id=1, source_target_pairs={{0,2},{2,4},{4,6},{6,8},{8,10},{10,12},{12,14},{14,16},{16,18},{18... | collective-permute-start | bytes 98312 | tf_op jit(solution)/shard_map/ppermute | solution.py:19
  75.8 3.1 %collective-permute-done.12.right_ref = f32[1,1,64,128]{3,2,1,0:T(8,128)S(1)} collective-permute-done((f32[1,1,64,128]{3,2,1,0:T(8,128)}, f32[1,1,64,128]{3,2,1,0:T(8,128)S(1)}, u32[]{:S(2)}, u32[]{:S(2)}) %collective-permute-start.12) | collective-permute-done | bytes 32800 | tf_op jit(solution)/shard_map/ppermute | solution.py:19
  79.5 2.1 %shard_map.99 = (f32[1,2,64,128]{3,2,1,0:T(8,128)}, f32[1,3,2,64,128]{4,3,2,1,0:T(8,128)}, f32[1,1,64,128]{3,2,1,0:T(8,128)}, f32[1,1,64,128]{3,2,1,0:T(8,128)}) custom-call(f32[1,2,64,128]{3,2,1,0:T(8,128)} %bitcast.25, f32[1,3,2,64,128]{4,3,2,1,0:T(8,128)} %bitcast.21, f32[2,64,128]{2,1,0:T(8,128)} %k_ref.17, f32[2,64,128]{2,1,0:T(8,128)} %m_ref.23, ...), custom_call_target="tpu_custom_call" | custom-call | tf_op jit(solution)/shard_map/pallas_call | solution.py:126
  83.6 2.3 %collective-permute-start.14 = (f32[1,1,64,128]{3,2,1,0:T(8,128)}, f32[1,1,64,128]{3,2,1,0:T(8,128)S(1)}, u32[]{:S(2)}, u32[]{:S(2)}) collective-permute-start(f32[1,1,64,128]{3,2,1,0:T(8,128)} %get-tuple-element.61), channel_id=1, source_target_pairs={{2,0},{4,2},{6,4},{8,6},{10,8},{12,10},{14,12},{16,14},{18,16},{20... | collective-permute-start | bytes 98312 | tf_op jit(solution)/shard_map/ppermute | solution.py:19
  85.9 4.1 %collective-permute-done.14.right_ref = f32[1,1,64,128]{3,2,1,0:T(8,128)S(1)} collective-permute-done((f32[1,1,64,128]{3,2,1,0:T(8,128)}, f32[1,1,64,128]{3,2,1,0:T(8,128)S(1)}, u32[]{:S(2)}, u32[]{:S(2)}) %collective-permute-start.14) | collective-permute-done | bytes 32800 | tf_op jit(solution)/shard_map/ppermute | solution.py:19
  94.6 2.3 %collective-permute-start.16 = (f32[1,1,64,128]{3,2,1,0:T(8,128)}, f32[1,1,64,128]{3,2,1,0:T(8,128)S(1)}, u32[]{:S(2)}, u32[]{:S(2)}) collective-permute-start(f32[1,1,64,128]{3,2,1,0:T(8,128)} %get-tuple-element.65), channel_id=1, source_target_pairs={{2,0},{4,2},{6,4},{8,6},{10,8},{12,10},{14,12},{16,14},{18,16},{20... | collective-permute-start | bytes 98312 | tf_op jit(solution)/shard_map/ppermute | solution.py:19
  99.4 4.1 %collective-permute-start.21 = (f32[1,1,64,128]{3,2,1,0:T(8,128)}, f32[1,1,64,128]{3,2,1,0:T(8,128)S(1)}, u32[]{:S(2)}, u32[]{:S(2)}) collective-permute-start(f32[1,1,64,128]{3,2,1,0:T(8,128)} %get-tuple-element.71), channel_id=1, source_target_pairs={{0,2},{2,4},{4,6},{6,8},{8,10},{10,12},{12,14},{14,16},{16,18},{18... | collective-permute-start | bytes 98312 | tf_op jit(solution)/shard_map/ppermute | solution.py:19
  108.2 4.5 %collective-permute-start.17 = (f32[1,1,64,128]{3,2,1,0:T(8,128)}, f32[1,1,64,128]{3,2,1,0:T(8,128)S(1)}, u32[]{:S(2)}, u32[]{:S(2)}) collective-permute-start(f32[1,1,64,128]{3,2,1,0:T(8,128)} %get-tuple-element.68), channel_id=1, source_target_pairs={{0,2},{2,4},{4,6},{6,8},{8,10},{10,12},{12,14},{14,16},{16,18},{18... | collective-permute-start | bytes 98312 | tf_op jit(solution)/shard_map/ppermute | solution.py:19
  115.9 2.1 %shard_map.104 = (f32[1,2,64,128]{3,2,1,0:T(8,128)}, f32[1,3,2,64,128]{4,3,2,1,0:T(8,128)}, f32[1,1,64,128]{3,2,1,0:T(8,128)}, f32[1,1,64,128]{3,2,1,0:T(8,128)}) custom-call(f32[1,2,64,128]{3,2,1,0:T(8,128)} %bitcast.23, f32[1,3,2,64,128]{4,3,2,1,0:T(8,128)} %bitcast.19, f32[2,64,128]{2,1,0:T(8,128)} %k_ref.17, f32[2,64,128]{2,1,0:T(8,128)} %m_ref.23, ...), custom_call_target="tpu_custom_call" | custom-call | tf_op jit(solution)/shard_map/pallas_call | solution.py:126
  119.7 2.1 %shard_map.102 = (f32[1,2,64,128]{3,2,1,0:T(8,128)}, f32[1,3,2,64,128]{4,3,2,1,0:T(8,128)}, f32[1,1,64,128]{3,2,1,0:T(8,128)}, f32[1,1,64,128]{3,2,1,0:T(8,128)}) custom-call(f32[1,2,64,128]{3,2,1,0:T(8,128)} %get-tuple-element.66.p_ref, f32[1,3,2,64,128]{4,3,2,1,0:T(8,128)} %get-tuple-element.67.v_ref, f32[2,64,128]{2,1,0:T(8,128)} %k_ref.17, ...), custom_call_target="tpu_custom_call" | custom-call | tf_op jit(solution)/shard_map/pallas_call | solution.py:126
  (105 shorter events, 48.5 us)
Async XLA Ops:
  3.1 7.6 %copy-start = (f32[2,64,128]{2,1,0:T(8,128)S(1)}, f32[2,64,128]{2,1,0:T(8,128)}, u32[]{:S(2)}) copy-start(f32[2,64,128]{2,1,0:T(8,128)} %m_ref.23) | copy-start | bytes 196612
  5.1 11.8 %collective-permute-start.1 = (f32[2,1,64,128]{3,2,1,0:T(8,128)}, f32[2,1,64,128]{3,2,1,0:T(8,128)S(1)}, u32[]{:S(2)}, u32[]{:S(2)}) collective-permute-start(f32[2,1,64,128]{3,2,1,0:T(8,128)} %get-tuple-element.40), channel_id=1, source_target_pairs={{0,2},{2,4},{4,6},{6,8},{8,10},{10,12},{12,14},{14,16},{16,18},{18... | collective-permute-start | bytes 196616 | tf_op jit(solution)/shard_map/ppermute | solution.py:19
  8.8 8.1 %collective-permute-start.2 = (f32[2,1,64,128]{3,2,1,0:T(8,128)}, f32[2,1,64,128]{3,2,1,0:T(8,128)S(1)}, u32[]{:S(2)}, u32[]{:S(2)}) collective-permute-start(f32[2,1,64,128]{3,2,1,0:T(8,128)} %get-tuple-element.41), channel_id=1, source_target_pairs={{2,0},{4,2},{6,4},{8,6},{10,8},{12,10},{14,12},{16,14},{18,16},{20... | collective-permute-start | bytes 196616 | tf_op jit(solution)/shard_map/ppermute | solution.py:19
  10.7 6.1 %collective-permute-start = (f32[1,64,128]{2,1,0:T(8,128)S(1)}, f32[1,64,128]{2,1,0:T(8,128)S(1)}, u32[]{:S(2)}, u32[]{:S(2)}) collective-permute-start(f32[1,64,128]{2,1,0:T(8,128)S(1)} %slice.15), channel_id=1, source_target_pairs={{2,0},{4,2},{6,4},{8,6},{10,8},{12,10},{14,12},{16,14},{18,16},{20... | collective-permute-start | bytes 98312 | tf_op jit(solution)/shard_map/ppermute | solution.py:19
  20.6 4.3 %collective-permute-start.3 = (f32[2,1,64,128]{3,2,1,0:T(8,128)}, f32[2,1,64,128]{3,2,1,0:T(8,128)S(1)}, u32[]{:S(2)}, u32[]{:S(2)}) collective-permute-start(f32[2,1,64,128]{3,2,1,0:T(8,128)} %get-tuple-element.44), channel_id=1, source_target_pairs={{0,2},{2,4},{4,6},{6,8},{8,10},{10,12},{12,14},{14,16},{16,18},{18... | collective-permute-start | bytes 196616 | tf_op jit(solution)/shard_map/ppermute | solution.py:19
  22.6 6.7 %collective-permute-start.4 = (f32[2,1,64,128]{3,2,1,0:T(8,128)}, f32[2,1,64,128]{3,2,1,0:T(8,128)S(1)}, u32[]{:S(2)}, u32[]{:S(2)}) collective-permute-start(f32[2,1,64,128]{3,2,1,0:T(8,128)} %get-tuple-element.45), channel_id=1, source_target_pairs={{2,0},{4,2},{6,4},{8,6},{10,8},{12,10},{14,12},{16,14},{18,16},{20... | collective-permute-start | bytes 196616 | tf_op jit(solution)/shard_map/ppermute | solution.py:19
  32.4 4.3 %collective-permute-start.5 = (f32[2,1,64,128]{3,2,1,0:T(8,128)}, f32[2,1,64,128]{3,2,1,0:T(8,128)S(1)}, u32[]{:S(2)}, u32[]{:S(2)}) collective-permute-start(f32[2,1,64,128]{3,2,1,0:T(8,128)} %get-tuple-element.48), channel_id=1, source_target_pairs={{0,2},{2,4},{4,6},{6,8},{8,10},{10,12},{12,14},{14,16},{16,18},{18... | collective-permute-start | bytes 196616 | tf_op jit(solution)/shard_map/ppermute | solution.py:19
  34.3 6.7 %collective-permute-start.6 = (f32[2,1,64,128]{3,2,1,0:T(8,128)}, f32[2,1,64,128]{3,2,1,0:T(8,128)S(1)}, u32[]{:S(2)}, u32[]{:S(2)}) collective-permute-start(f32[2,1,64,128]{3,2,1,0:T(8,128)} %get-tuple-element.49), channel_id=1, source_target_pairs={{2,0},{4,2},{6,4},{8,6},{10,8},{12,10},{14,12},{16,14},{18,16},{20... | collective-permute-start | bytes 196616 | tf_op jit(solution)/shard_map/ppermute | solution.py:19
  44.2 4.3 %collective-permute-start.7 = (f32[2,1,64,128]{3,2,1,0:T(8,128)}, f32[2,1,64,128]{3,2,1,0:T(8,128)S(1)}, u32[]{:S(2)}, u32[]{:S(2)}) collective-permute-start(f32[2,1,64,128]{3,2,1,0:T(8,128)} %get-tuple-element.52), channel_id=1, source_target_pairs={{0,2},{2,4},{4,6},{6,8},{8,10},{10,12},{12,14},{14,16},{16,18},{18... | collective-permute-start | bytes 196616 | tf_op jit(solution)/shard_map/ppermute | solution.py:19
  46.1 6.7 %collective-permute-start.8 = (f32[2,1,64,128]{3,2,1,0:T(8,128)}, f32[2,1,64,128]{3,2,1,0:T(8,128)S(1)}, u32[]{:S(2)}, u32[]{:S(2)}) collective-permute-start(f32[2,1,64,128]{3,2,1,0:T(8,128)} %get-tuple-element.53), channel_id=1, source_target_pairs={{2,0},{4,2},{6,4},{8,6},{10,8},{12,10},{14,12},{16,14},{18,16},{20... | collective-permute-start | bytes 196616 | tf_op jit(solution)/shard_map/ppermute | solution.py:19
  57.0 10.2 %collective-permute-start.10 = (f32[3,2,64,128]{3,2,1,0:T(8,128)S(1)}, f32[3,2,64,128]{3,2,1,0:T(8,128)S(1)}, u32[]{:S(2)}, u32[]{:S(2)}) collective-permute-start(f32[3,2,64,128]{3,2,1,0:T(8,128)S(1)} %slice_bitcast_fusion), channel_id=1, source_target_pairs={{0,1},{2,3},{4,5},{6,7},{8,9},{10,11},{12,13},{14,15},{16,17},{18,... | collective-permute-start | bytes 589832 | tf_op jit(solution)/shard_map/ppermute | solution.py:19
  59.1 8.1 %collective-permute-start.9 = (f32[2,64,128]{2,1,0:T(8,128)S(1)}, f32[2,64,128]{2,1,0:T(8,128)S(1)}, u32[]{:S(2)}, u32[]{:S(2)}) collective-permute-start(f32[2,64,128]{2,1,0:T(8,128)S(1)} %slice_bitcast_fusion.1), channel_id=1, source_target_pairs={{0,1},{2,3},{4,5},{6,7},{8,9},{10,11},{12,13},{14,15},{16,17},{18,... | collective-permute-start | bytes 196616 | tf_op jit(solution)/shard_map/ppermute | solution.py:19
  60.4 36.5 %collective-permute-start.20 = (f32[3,2,64,128]{3,2,1,0:T(8,128)S(1)}, f32[3,2,64,128]{3,2,1,0:T(8,128)S(1)}, u32[]{:S(2)}, u32[]{:S(2)}) collective-permute-start(f32[3,2,64,128]{3,2,1,0:T(8,128)S(1)} %bitcast_subtract_fusion), channel_id=1, source_target_pairs={{0,1},{2,3},{4,5},{6,7},{8,9},{10,11},{12,13},{14,15},{16,17},{18,... | collective-permute-start | bytes 589832 | tf_op jit(solution)/shard_map/ppermute | solution.py:19
  69.7 6.1 %collective-permute-start.11 = (f32[1,1,64,128]{3,2,1,0:T(8,128)}, f32[1,1,64,128]{3,2,1,0:T(8,128)S(1)}, u32[]{:S(2)}, u32[]{:S(2)}) collective-permute-start(f32[1,1,64,128]{3,2,1,0:T(8,128)} %get-tuple-element.56), channel_id=1, source_target_pairs={{0,2},{2,4},{4,6},{6,8},{8,10},{10,12},{12,14},{14,16},{16,18},{18... | collective-permute-start | bytes 98312 | tf_op jit(solution)/shard_map/ppermute | solution.py:19
  72.5 6.3 %collective-permute-start.12 = (f32[1,1,64,128]{3,2,1,0:T(8,128)}, f32[1,1,64,128]{3,2,1,0:T(8,128)S(1)}, u32[]{:S(2)}, u32[]{:S(2)}) collective-permute-start(f32[1,1,64,128]{3,2,1,0:T(8,128)} %get-tuple-element.57), channel_id=1, source_target_pairs={{2,0},{4,2},{6,4},{8,6},{10,8},{12,10},{14,12},{16,14},{18,16},{20... | collective-permute-start | bytes 98312 | tf_op jit(solution)/shard_map/ppermute | solution.py:19
  74.5 22.5 %collective-permute-start.19 = (f32[2,64,128]{2,1,0:T(8,128)S(1)}, f32[2,64,128]{2,1,0:T(8,128)S(1)}, u32[]{:S(2)}, u32[]{:S(2)}) collective-permute-start(f32[2,64,128]{2,1,0:T(8,128)S(1)} %bitcast_subtract_fusion.1), channel_id=1, source_target_pairs={{0,1},{2,3},{4,5},{6,7},{8,9},{10,11},{12,13},{14,15},{16,17},{18,... | collective-permute-start | bytes 196616 | tf_op jit(solution)/shard_map/ppermute | solution.py:19
  81.5 4.3 %collective-permute-start.13 = (f32[1,1,64,128]{3,2,1,0:T(8,128)}, f32[1,1,64,128]{3,2,1,0:T(8,128)S(1)}, u32[]{:S(2)}, u32[]{:S(2)}) collective-permute-start(f32[1,1,64,128]{3,2,1,0:T(8,128)} %get-tuple-element.60), channel_id=1, source_target_pairs={{0,2},{2,4},{4,6},{6,8},{8,10},{10,12},{12,14},{14,16},{16,18},{18... | collective-permute-start | bytes 98312 | tf_op jit(solution)/shard_map/ppermute | solution.py:19
  83.6 6.3 %collective-permute-start.14 = (f32[1,1,64,128]{3,2,1,0:T(8,128)}, f32[1,1,64,128]{3,2,1,0:T(8,128)S(1)}, u32[]{:S(2)}, u32[]{:S(2)}) collective-permute-start(f32[1,1,64,128]{3,2,1,0:T(8,128)} %get-tuple-element.61), channel_id=1, source_target_pairs={{2,0},{4,2},{6,4},{8,6},{10,8},{12,10},{14,12},{16,14},{18,16},{20... | collective-permute-start | bytes 98312 | tf_op jit(solution)/shard_map/ppermute | solution.py:19
  92.6 12.9 %collective-permute-start.15 = (f32[1,1,64,128]{3,2,1,0:T(8,128)}, f32[1,1,64,128]{3,2,1,0:T(8,128)S(1)}, u32[]{:S(2)}, u32[]{:S(2)}) collective-permute-start(f32[1,1,64,128]{3,2,1,0:T(8,128)} %get-tuple-element.64), channel_id=1, source_target_pairs={{0,2},{2,4},{4,6},{6,8},{8,10},{10,12},{12,14},{14,16},{16,18},{18... | collective-permute-start | bytes 98312 | tf_op jit(solution)/shard_map/ppermute | solution.py:19
  94.6 10.9 %collective-permute-start.16 = (f32[1,1,64,128]{3,2,1,0:T(8,128)}, f32[1,1,64,128]{3,2,1,0:T(8,128)S(1)}, u32[]{:S(2)}, u32[]{:S(2)}) collective-permute-start(f32[1,1,64,128]{3,2,1,0:T(8,128)} %get-tuple-element.65), channel_id=1, source_target_pairs={{2,0},{4,2},{6,4},{8,6},{10,8},{12,10},{14,12},{16,14},{18,16},{20... | collective-permute-start | bytes 98312 | tf_op jit(solution)/shard_map/ppermute | solution.py:19
  99.4 15.2 %collective-permute-start.21 = (f32[1,1,64,128]{3,2,1,0:T(8,128)}, f32[1,1,64,128]{3,2,1,0:T(8,128)S(1)}, u32[]{:S(2)}, u32[]{:S(2)}) collective-permute-start(f32[1,1,64,128]{3,2,1,0:T(8,128)} %get-tuple-element.71), channel_id=1, source_target_pairs={{0,2},{2,4},{4,6},{6,8},{8,10},{10,12},{12,14},{14,16},{16,18},{18... | collective-permute-start | bytes 98312 | tf_op jit(solution)/shard_map/ppermute | solution.py:19
  103.6 11.1 %collective-permute-start.22 = (f32[1,1,64,128]{3,2,1,0:T(8,128)}, f32[1,1,64,128]{3,2,1,0:T(8,128)S(1)}, u32[]{:S(2)}, u32[]{:S(2)}) collective-permute-start(f32[1,1,64,128]{3,2,1,0:T(8,128)} %get-tuple-element.72), channel_id=1, source_target_pairs={{2,0},{4,2},{6,4},{8,6},{10,8},{12,10},{14,12},{16,14},{18,16},{20... | collective-permute-start | bytes 98312 | tf_op jit(solution)/shard_map/ppermute | solution.py:19
  108.2 9.7 %collective-permute-start.17 = (f32[1,1,64,128]{3,2,1,0:T(8,128)}, f32[1,1,64,128]{3,2,1,0:T(8,128)S(1)}, u32[]{:S(2)}, u32[]{:S(2)}) collective-permute-start(f32[1,1,64,128]{3,2,1,0:T(8,128)} %get-tuple-element.68), channel_id=1, source_target_pairs={{0,2},{2,4},{4,6},{6,8},{8,10},{10,12},{12,14},{14,16},{16,18},{18... | collective-permute-start | bytes 98312 | tf_op jit(solution)/shard_map/ppermute | solution.py:19
  112.7 6.3 %collective-permute-start.18 = (f32[1,1,64,128]{3,2,1,0:T(8,128)}, f32[1,1,64,128]{3,2,1,0:T(8,128)S(1)}, u32[]{:S(2)}, u32[]{:S(2)}) collective-permute-start(f32[1,1,64,128]{3,2,1,0:T(8,128)} %get-tuple-element.69), channel_id=1, source_target_pairs={{2,0},{4,2},{6,4},{8,6},{10,8},{12,10},{14,12},{16,14},{18,16},{20... | collective-permute-start | bytes 98312 | tf_op jit(solution)/shard_map/ppermute | solution.py:19
  (30 other events, 52.2 us)

commit v4 on v3

v4 whole, which is shorter than its diff:
```python
import functools

import jax
import jax.numpy as jnp
from jax import lax
from jax.experimental import pallas as pl
from jax.experimental.pallas import tpu as pltpu
from jax.sharding import PartitionSpec as P

STEPS = 4


DT_COARSE = 0.4


def from_behind(x, axis, by):
    size = lax.axis_size(axis)
    pairs = [(i, i + by) for i in range(size) if 0 <= i + by < size]
    return lax.ppermute(x, axis, pairs)


def roll(x, shift, axis):
    return pltpu.roll(x, shift % x.shape[axis], axis)


def nsum(values, offset, axis):
    return values + roll(values, offset, axis)


def forces(pressure, lower):
    combined = pressure + lower
    force_x = 0.25 * (nsum(nsum(lower, 1, 1), 1, 0) - nsum(nsum(pressure, 1, 1), 1, 0))
    across_z = nsum(combined, 1, 1)
    force_y = 0.25 * (roll(across_z, 1, 0) - across_z)
    across_y = nsum(combined, 1, 0)
    force_z = 0.25 * (roll(across_y, 1, 1) - across_y)
    return force_x, force_y, force_z


def divergence(v, u):
    diff_x = nsum(nsum(u[0] - v[0], -1, 1), -1, 0)
    sum_y = nsum(v[1] + u[1], -1, 1)
    diff_y = roll(sum_y, -1, 0) - sum_y
    sum_z = nsum(v[2] + u[2], -1, 0)
    diff_z = roll(sum_z, -1, 1) - sum_z
    return 0.25 * (diff_x + diff_y + diff_z)


def upper_part(u):
    diff_x = nsum(nsum(u[0], -1, 1), -1, 0)
    sum_y = nsum(u[1], -1, 1)
    diff_y = roll(sum_y, -1, 0) - sum_y
    sum_z = nsum(u[2], -1, 0)
    diff_z = roll(sum_z, -1, 1) - sum_z
    return diff_x + diff_y + diff_z


def lower_part(v):
    diff_x = nsum(nsum(-v[0], -1, 1), -1, 0)
    sum_y = nsum(v[1], -1, 1)
    diff_y = roll(sum_y, -1, 0) - sum_y
    sum_z = nsum(v[2], -1, 0)
    diff_z = roll(sum_z, -1, 1) - sum_z
    return diff_x + diff_y + diff_z


def outgoing(pressure_first, velocity_first, mass_first, step_size):
    f = forces(pressure_first, jnp.zeros_like(pressure_first))
    hm = step_size * mass_first
    return upper_part([velocity_first[c] + hm * f[c] for c in range(3)])


def step_kernel(sizes, next_count, mass_index, emit_mass, s_ref, k_ref, m_ref, mn_ref, left_ref,
                right_ref, s_out, *outs):
    n = s_ref.shape[2]
    next_mass = mn_ref[mass_index, 0]
    for b, step_size in enumerate(sizes):
        pres = [s_ref[b, 0, i] for i in range(n)]
        lower = [left_ref[b, 0]] + pres[:-1]
        vel = []
        for i in range(n):
            f = forces(pres[i], lower[i])
            hm = step_size * m_ref[i]
            vel.append([s_ref[b, 1 + c, i] + hm * f[c] for c in range(3)])
        for i in range(n):
            for c in range(3):
                s_out[b, 1 + c, i] = vel[i][c]
        new_p = []
        for i in range(n - 1):
            new_p.append(pres[i] - step_size * k_ref[i] * divergence(vel[i], vel[i + 1]))
        zero = jnp.zeros_like(pres[-1])
        hm_next = step_size * next_mass
        own_share = upper_part([hm_next * f for f in forces(zero, pres[-1])])
        edge = 0.25 * (lower_part(vel[-1]) + (right_ref[b, 0] + own_share))
        new_p.append(pres[-1] - step_size * k_ref[n - 1] * edge)
        for i in range(n):
            s_out[b, 0, i] = new_p[i]
        if b < next_count:
            outs[0][b, 0] = new_p[-1]
            outs[1][b, 0] = outgoing(new_p[0], vel[0], m_ref[0], step_size)
    if emit_mass:
        outs[-1][0, 0] = next_mass


def plane_shape(count, like):
    return jax.ShapeDtypeStruct((count, 1) + like.shape[-2:], like.dtype)


def advance(state, last, share, stiffness, inv_mass, mass, sizes, next_count, mass_index=0):
    from_left = from_behind(last, "space", 1)
    from_right = from_behind(share, "space", -1)
    if mass is None:
        mass = from_right
    emit_mass = mass_index > 0
    outs = [jax.ShapeDtypeStruct((len(sizes),) + state.shape[1:], state.dtype)]
    if next_count:
        outs += [plane_shape(next_count, state), plane_shape(next_count, state)]
    if emit_mass:
        outs.append(plane_shape(1, state))
    return pl.pallas_call(
        functools.partial(step_kernel, tuple(sizes), next_count, mass_index, emit_mass),
        out_shape=tuple(outs),
    )(state, stiffness, inv_mass, mass, from_left, from_right)


def start_kernel(step_size, gp_ref, gv_ref, ip_ref, iv_ref, m_ref, s_out, last_out, part_out):
    n = ip_ref.shape[0]
    for i in range(n):
        s_out[0, 0, i] = gp_ref[0, i]
        s_out[1, 0, i] = ip_ref[i]
        for c in range(3):
            s_out[0, 1 + c, i] = gv_ref[0, c, i]
            s_out[1, 1 + c, i] = iv_ref[c, i]
    last_out[0, 0] = gp_ref[0, n - 1]
    last_out[1, 0] = ip_ref[n - 1]
    part_out[0, 0] = outgoing(gp_ref[0, 0], [gv_ref[0, c, 0] for c in range(3)], m_ref[0], step_size)
    part_out[1, 0] = outgoing(ip_ref[0], [iv_ref[c, 0] for c in range(3)], m_ref[0], step_size)
    part_out[2, 0] = m_ref[0]


def prep_kernel(sizes, s_ref, m_ref, last_out, part_out):
    n = s_ref.shape[2]
    for b, step_size in enumerate(sizes):
        last_out[b, 0] = s_ref[b, 0, n - 1]
        part_out[b, 0] = outgoing(
            s_ref[b, 0, 0], [s_ref[b, 1 + c, 0] for c in range(3)], m_ref[0], step_size
        )


def prep(state, inv_mass, sizes):
    return pl.pallas_call(
        functools.partial(prep_kernel, tuple(sizes)),
        out_shape=(plane_shape(len(sizes), state), plane_shape(len(sizes), state)),
    )(state, inv_mass)


def coarse(carried, stiffness, inv_mass, mass):
    last, share = prep(carried, inv_mass, (DT_COARSE,))
    (out,) = advance(carried, last, share, stiffness, inv_mass, mass, (DT_COARSE,), 0)
    return out[0]


def on_device(
    guess_pressure, guess_velocity, initial_pressure, initial_velocity, stiffness, inv_mass
):
    fine_size = DT_COARSE / STEPS
    groups = lax.axis_size("tm")
    group = lax.axis_index("tm")
    n = stiffness.shape[0]

    state_shape = jax.ShapeDtypeStruct((2, 4) + stiffness.shape, stiffness.dtype)
    state, last, share = pl.pallas_call(
        functools.partial(start_kernel, fine_size),
        out_shape=(state_shape, plane_shape(2, stiffness), plane_shape(3, stiffness)),
    )(guess_pressure, guess_velocity, initial_pressure, initial_velocity, inv_mass)
    state, last, share, mass = advance(
        state, last, share, stiffness, inv_mass, None, (fine_size, fine_size), 2, mass_index=2
    )
    for repeat in range(1, STEPS):
        count = 2 if repeat + 1 < STEPS else 0
        outs = advance(state, last, share, stiffness, inv_mass, mass, (fine_size, fine_size), count)
        state = outs[0]
        if count:
            last, share = outs[1], outs[2]
    relaxed, own_end = state[0], state[1]
    early = own_end - relaxed

    got = from_behind(jnp.stack([relaxed, early]), "tm", 1)
    last, share = prep(got, inv_mass, (fine_size, DT_COARSE))
    both, last, share = advance(got, last, share, stiffness, inv_mass, mass, (fine_size, DT_COARSE), 1)
    late = both
    for repeat in range(1, STEPS):
        count = 1 if repeat + 1 < STEPS else 0
        outs = advance(late, last, share, stiffness, inv_mass, mass, (fine_size,), count)
        late = outs[0]
        if count:
            last, share = outs[1], outs[2]

    end = jnp.where(group == 0, own_end, late[0])
    resid = end - relaxed
    if groups == 2:
        error = resid + both[1]
    else:
        error, carried = resid, resid
        for repeat in range(groups - 1):
            carried = from_behind(carried, "tm", 1)
            carried = coarse(carried[None], stiffness, inv_mass, mass)
            error = error + carried
    corrected = relaxed + error
    return (corrected[0][None], corrected[1:][None], resid[0][None], resid[1:][None])


def solution(mesh):
    placed = (
        P("tm", "space", None, None),
        P("tm", None, "space", None, None),
        P("space", None, None),
        P(None, "space", None, None),
        P("space", None, None),
        P("space", None, None),
    )
    return jax.shard_map(
        on_device,
        mesh=mesh,
        in_specs=placed,
        out_specs=(
            P("tm", "space", None, None),
            P("tm", None, "space", None, None),
            P("tm", "space", None, None),
            P("tm", None, "space", None, None),
        ),
        check_vma=False,
    )
```

time: 127 us -> 122 us (0.961); the launches traced: 124 us -> 121 us
  waiting for transfers between devices: 30.3 us -> 41.6 us
  starting transfers between devices: 52.1 us -> 45.4 us
  other arithmetic: 4.96 us -> 2.12 us
  Pallas kernels: 25.8 us -> 23.6 us
  local copies, waits for them, and re-layouts: 10 us -> 7.88 us
    ppermute x23 -> x17, waiting for transfers between devices: 30.3 us -> 41.6 us  [from_behind(): return lax.ppermute(x, axis, pairs)]
    ppermute x23 -> x17, starting transfers between devices: 52.1 us -> 45.4 us  [from_behind(): return lax.ppermute(x, axis, pairs)]
    another operation x2 -> x1, other arithmetic: 2.49 us -> 0.04 us  [on_device(): got = from_behind(jnp.stack([relaxed, early]), 'tm', 1)]
    unnamed x62 -> x38, local copies, waits for them, and re-layouts: 8.15 us -> 5.85 us
    pallas_call x12 -> x10, Pallas kernels: 25.8 us -> 23.6 us  [the longest x8 19.6 us: advance(): pl.pallas_call(functools.partial(step_kernel, tuple(sizes), next_count, m...]
    squeeze x2 -> x0, local copies, waits for them, and re-layouts: 1.86 us -> none  [on_device(): relaxed_p, relaxed_v = (first_p[0], first_v[0])]
    add x2 -> x1, other arithmetic: 2.43 us -> 1.02 us  [on_device(): corrected = relaxed + error]
  transfers between devices with their start and end apart: 23 -> 17, of which waited for: 8 -> 10; matrix products, arithmetic and copies ran while one was open for 1% -> 0% of each run, Pallas kernels for 10% -> 0%
where the time goes in v4:
time: 122 us; the launch traced here: 121 us
  starting transfers between devices  45.4 us (37%)
  waiting for transfers between devices  41.6 us (34%)
  Pallas kernels  23.6 us (19%)
  local copies, waits for them, and re-layouts  7.88 us (6%)
  other arithmetic  2.12 us (2%)
    ppermute x17, starting transfers between devices, from_behind(): return lax.ppermute(x, axis, pairs)  45.4 us
    ppermute x17, waiting for transfers between devices, from_behind(): return lax.ppermute(x, axis, pairs)  41.6 us
    pallas_call x8, Pallas kernels, advance(): pl.pallas_call(functools.partial(step_kernel, tuple(sizes), next_count, m...  19.6 us
    unnamed x38, local copies, waits for them, and re-layouts  5.85 us
  transfers between devices with their start and end apart: 17, of which 10 were waited for; matrix products, arithmetic and copies ran while one was open for 0% of the time, Pallas kernels for 0%

profile of v4, /device:TPU:7, one launch (start us, length us, event | category | flops | bytes accessed | tf_op | source)
XLA Modules:
  0.0 121.5 jit_solution(8492996871049734406)
XLA Ops:
  0.6 2.1 %shard_map.93 = (f32[2,4,2,64,128]{4,3,2,1,0:T(8,128)}, f32[2,1,64,128]{3,2,1,0:T(8,128)}, f32[3,1,64,128]{3,2,1,0:T(8,128)}) custom-call(f32[1,2,64,128]{3,2,1,0:T(8,128)} %gp_ref.1, f32[1,3,2,64,128]{4,3,2,1,0:T(8,128)} %gv_ref.1, f32[2,64,128]{2,1,0:T(8,128)} %ip_ref.1, f32[3,2,64,128]{3,2,1,0:T(8,128)} %iv_ref.1, f32[2,64,128]{2,1,0:T(8,128)} %m_ref.19), custom_call_target="tpu_custom_call" | custom-call | tf_op jit(solution)/shard_map/pallas_call | solution.py:172
  2.7 2.6 %collective-permute-start = (f32[3,1,64,128]{3,2,1,0:T(8,128)}, f32[3,1,64,128]{3,2,1,0:T(8,128)S(1)}, u32[]{:S(2)}, u32[]{:S(2)}) collective-permute-start(f32[3,1,64,128]{3,2,1,0:T(8,128)} %get-tuple-element.29), channel_id=1, source_target_pairs={{2,0},{4,2},{6,4},{8,6},{10,8},{12,10},{14,12},{16,14},{18,16},{20... | collective-permute-start | bytes 294920 | tf_op jit(solution)/shard_map/ppermute | solution.py:19
  5.3 3.9 %collective-permute-start.1 = (f32[2,1,64,128]{3,2,1,0:T(8,128)}, f32[2,1,64,128]{3,2,1,0:T(8,128)S(1)}, u32[]{:S(2)}, u32[]{:S(2)}) collective-permute-start(f32[2,1,64,128]{3,2,1,0:T(8,128)} %get-tuple-element.30), channel_id=1, source_target_pairs={{0,2},{2,4},{4,6},{6,8},{8,10},{10,12},{12,14},{14,16},{16,18},{18... | collective-permute-start | bytes 196616 | tf_op jit(solution)/shard_map/ppermute | solution.py:19
  11.5 2.7 %shard_map.94 = (f32[2,4,2,64,128]{4,3,2,1,0:T(8,128)}, f32[2,1,64,128]{3,2,1,0:T(8,128)}, f32[2,1,64,128]{3,2,1,0:T(8,128)}, f32[1,1,64,128]{3,2,1,0:T(8,128)}) custom-call(f32[2,4,2,64,128]{4,3,2,1,0:T(8,128)} %get-tuple-element.28.s_ref, f32[2,64,128]{2,1,0:T(8,128)} %k_ref.15, f32[2,64,128]{2,1,0:T(8,128)} %m_ref.19, f32[3,1,64,128]{3,2,1,0:T(8,128)} %copy-done.3, ...), custom_call_target="tpu_custom_call" | custom-call | tf_op jit(solution)/shard_map/pallas_call | solution.py:120
  14.2 5.0 %collective-permute-start.2 = (f32[2,1,64,128]{3,2,1,0:T(8,128)}, f32[2,1,64,128]{3,2,1,0:T(8,128)S(1)}, u32[]{:S(2)}, u32[]{:S(2)}) collective-permute-start(f32[2,1,64,128]{3,2,1,0:T(8,128)} %get-tuple-element.33), channel_id=1, source_target_pairs={{0,2},{2,4},{4,6},{6,8},{8,10},{10,12},{12,14},{14,16},{16,18},{18... | collective-permute-start | bytes 196616 | tf_op jit(solution)/shard_map/ppermute | solution.py:19
  21.2 4.7 %collective-permute-done.3.right_ref = f32[2,1,64,128]{3,2,1,0:T(8,128)S(1)} collective-permute-done((f32[2,1,64,128]{3,2,1,0:T(8,128)}, f32[2,1,64,128]{3,2,1,0:T(8,128)S(1)}, u32[]{:S(2)}, u32[]{:S(2)}) %collective-permute-start.3) | collective-permute-done | bytes 65568 | tf_op jit(solution)/shard_map/ppermute | solution.py:19
  26.6 2.7 %shard_map.95 = (f32[2,4,2,64,128]{4,3,2,1,0:T(8,128)}, f32[2,1,64,128]{3,2,1,0:T(8,128)}, f32[2,1,64,128]{3,2,1,0:T(8,128)}) custom-call(f32[2,4,2,64,128]{4,3,2,1,0:T(8,128)} %get-tuple-element.31.s_ref, f32[2,64,128]{2,1,0:T(8,128)} %k_ref.15, f32[2,64,128]{2,1,0:T(8,128)} %m_ref.19, f32[1,1,64,128]{3,2,1,0:T(8,128)} %get-tuple-element.32.mn_ref, ...), custom_call_target="tpu_custom_call" | custom-call | tf_op jit(solution)/shard_map/pallas_call | solution.py:120
  31.2 2.4 %collective-permute-start.5 = (f32[2,1,64,128]{3,2,1,0:T(8,128)}, f32[2,1,64,128]{3,2,1,0:T(8,128)S(1)}, u32[]{:S(2)}, u32[]{:S(2)}) collective-permute-start(f32[2,1,64,128]{3,2,1,0:T(8,128)} %get-tuple-element.37), channel_id=1, source_target_pairs={{2,0},{4,2},{6,4},{8,6},{10,8},{12,10},{14,12},{16,14},{18,16},{20... | collective-permute-start | bytes 196616 | tf_op jit(solution)/shard_map/ppermute | solution.py:19
  33.6 4.3 %collective-permute-done.5.right_ref = f32[2,1,64,128]{3,2,1,0:T(8,128)S(1)} collective-permute-done((f32[2,1,64,128]{3,2,1,0:T(8,128)}, f32[2,1,64,128]{3,2,1,0:T(8,128)S(1)}, u32[]{:S(2)}, u32[]{:S(2)}) %collective-permute-start.5) | collective-permute-done | bytes 65568 | tf_op jit(solution)/shard_map/ppermute | solution.py:19
  38.6 2.6 %shard_map.96 = (f32[2,4,2,64,128]{4,3,2,1,0:T(8,128)}, f32[2,1,64,128]{3,2,1,0:T(8,128)}, f32[2,1,64,128]{3,2,1,0:T(8,128)}) custom-call(f32[2,4,2,64,128]{4,3,2,1,0:T(8,128)} %get-tuple-element.35.s_ref, f32[2,64,128]{2,1,0:T(8,128)} %k_ref.15, f32[2,64,128]{2,1,0:T(8,128)} %m_ref.19, f32[1,1,64,128]{3,2,1,0:T(8,128)} %get-tuple-element.32.mn_ref, ...), custom_call_target="tpu_custom_call" | custom-call | tf_op jit(solution)/shard_map/pallas_call | solution.py:120
  43.2 2.4 %collective-permute-start.7 = (f32[2,1,64,128]{3,2,1,0:T(8,128)}, f32[2,1,64,128]{3,2,1,0:T(8,128)S(1)}, u32[]{:S(2)}, u32[]{:S(2)}) collective-permute-start(f32[2,1,64,128]{3,2,1,0:T(8,128)} %get-tuple-element.40), channel_id=1, source_target_pairs={{2,0},{4,2},{6,4},{8,6},{10,8},{12,10},{14,12},{16,14},{18,16},{20... | collective-permute-start | bytes 196616 | tf_op jit(solution)/shard_map/ppermute | solution.py:19
  45.6 4.3 %collective-permute-done.7.right_ref = f32[2,1,64,128]{3,2,1,0:T(8,128)S(1)} collective-permute-done((f32[2,1,64,128]{3,2,1,0:T(8,128)}, f32[2,1,64,128]{3,2,1,0:T(8,128)S(1)}, u32[]{:S(2)}, u32[]{:S(2)}) %collective-permute-start.7) | collective-permute-done | bytes 65568 | tf_op jit(solution)/shard_map/ppermute | solution.py:19
  50.5 2.5 %shard_map.97 = f32[2,4,2,64,128]{4,3,2,1,0:T(8,128)} custom-call(f32[2,4,2,64,128]{4,3,2,1,0:T(8,128)} %get-tuple-element.38.s_ref, f32[2,64,128]{2,1,0:T(8,128)} %k_ref.15, f32[2,64,128]{2,1,0:T(8,128)} %m_ref.19, f32[1,1,64,128]{3,2,1,0:T(8,128)} %get-tuple-element.32.mn_ref, f32[2,1,64,128]{3,2,1,0:T(8,128)} %copy-done.11, f32[2,1,64,128]{3,2,1,0:T(8,128)} %copy-done.12), custom_call_target="tpu_custom_call" | custom-call | tf_op jit(solution)/shard_map/pallas_call | solution.py:120
  55.4 12.6 %collective-permute-done.8.s_ref = f32[2,4,2,64,128]{4,3,2,1,0:T(8,128)S(1)} collective-permute-done((f32[2,4,2,64,128]{4,3,2,1,0:T(8,128)S(1)}, f32[2,4,2,64,128]{4,3,2,1,0:T(8,128)S(1)}, u32[]{:S(2)}, u32[]{:S(2)}) %collective-permute-start.8) | collective-permute-done | bytes 524320 | tf_op jit(solution)/shard_map/ppermute | solution.py:19
  72.6 4.5 %collective-permute-start.9 = (f32[2,1,64,128]{3,2,1,0:T(8,128)}, f32[2,1,64,128]{3,2,1,0:T(8,128)S(1)}, u32[]{:S(2)}, u32[]{:S(2)}) collective-permute-start(f32[2,1,64,128]{3,2,1,0:T(8,128)} %get-tuple-element.41), channel_id=1, source_target_pairs={{0,2},{2,4},{4,6},{6,8},{8,10},{10,12},{12,14},{14,16},{16,18},{18... | collective-permute-start | bytes 196616 | tf_op jit(solution)/shard_map/ppermute | solution.py:19
  79.4 2.6 %shard_map.99 = (f32[2,4,2,64,128]{4,3,2,1,0:T(8,128)}, f32[1,1,64,128]{3,2,1,0:T(8,128)}, f32[1,1,64,128]{3,2,1,0:T(8,128)}) custom-call(f32[2,4,2,64,128]{4,3,2,1,0:T(8,128)} %copy-done.1, f32[2,64,128]{2,1,0:T(8,128)} %k_ref.15, f32[2,64,128]{2,1,0:T(8,128)} %m_ref.19, f32[1,1,64,128]{3,2,1,0:T(8,128)} %get-tuple-element.32.mn_ref, ...), custom_call_target="tpu_custom_call" | custom-call | tf_op jit(solution)/shard_map/pallas_call | solution.py:120
  82.0 5.0 %collective-permute-start.11 = (f32[1,1,64,128]{3,2,1,0:T(8,128)}, f32[1,1,64,128]{3,2,1,0:T(8,128)S(1)}, u32[]{:S(2)}, u32[]{:S(2)}) collective-permute-start(f32[1,1,64,128]{3,2,1,0:T(8,128)} %get-tuple-element.44), channel_id=1, source_target_pairs={{0,2},{2,4},{4,6},{6,8},{8,10},{10,12},{12,14},{14,16},{16,18},{18... | collective-permute-start | bytes 98312 | tf_op jit(solution)/shard_map/ppermute | solution.py:19
  89.0 4.4 %collective-permute-done.12.right_ref = f32[1,1,64,128]{3,2,1,0:T(8,128)S(1)} collective-permute-done((f32[1,1,64,128]{3,2,1,0:T(8,128)}, f32[1,1,64,128]{3,2,1,0:T(8,128)S(1)}, u32[]{:S(2)}, u32[]{:S(2)}) %collective-permute-start.12) | collective-permute-done | bytes 32800 | tf_op jit(solution)/shard_map/ppermute | solution.py:19
  94.1 2.2 %shard_map.100 = (f32[1,4,2,64,128]{4,3,2,1,0:T(8,128)}, f32[1,1,64,128]{3,2,1,0:T(8,128)}, f32[1,1,64,128]{3,2,1,0:T(8,128)}) custom-call(f32[2,4,2,64,128]{4,3,2,1,0:T(8,128)} %get-tuple-element.43.s_ref, f32[2,64,128]{2,1,0:T(8,128)} %k_ref.15, f32[2,64,128]{2,1,0:T(8,128)} %m_ref.19, f32[1,1,64,128]{3,2,1,0:T(8,128)} %get-tuple-element.32.mn_ref, ...), custom_call_target="tpu_custom_call" | custom-call | tf_op jit(solution)/shard_map/pallas_call | solution.py:120
  98.3 2.3 %collective-permute-start.14 = (f32[1,1,64,128]{3,2,1,0:T(8,128)}, f32[1,1,64,128]{3,2,1,0:T(8,128)S(1)}, u32[]{:S(2)}, u32[]{:S(2)}) collective-permute-start(f32[1,1,64,128]{3,2,1,0:T(8,128)} %get-tuple-element.48), channel_id=1, source_target_pairs={{2,0},{4,2},{6,4},{8,6},{10,8},{12,10},{14,12},{16,14},{18,16},{20... | collective-permute-start | bytes 98312 | tf_op jit(solution)/shard_map/ppermute | solution.py:19
  100.6 4.0 %collective-permute-done.14.right_ref = f32[1,1,64,128]{3,2,1,0:T(8,128)S(1)} collective-permute-done((f32[1,1,64,128]{3,2,1,0:T(8,128)}, f32[1,1,64,128]{3,2,1,0:T(8,128)S(1)}, u32[]{:S(2)}, u32[]{:S(2)}) %collective-permute-start.14) | collective-permute-done | bytes 32800 | tf_op jit(solution)/shard_map/ppermute | solution.py:19
  105.2 2.2 %shard_map.101 = (f32[1,4,2,64,128]{4,3,2,1,0:T(8,128)}, f32[1,1,64,128]{3,2,1,0:T(8,128)}, f32[1,1,64,128]{3,2,1,0:T(8,128)}) custom-call(f32[1,4,2,64,128]{4,3,2,1,0:T(8,128)} %get-tuple-element.46.s_ref, f32[2,64,128]{2,1,0:T(8,128)} %k_ref.15, f32[2,64,128]{2,1,0:T(8,128)} %m_ref.19, f32[1,1,64,128]{3,2,1,0:T(8,128)} %get-tuple-element.32.mn_ref, ...), custom_call_target="tpu_custom_call" | custom-call | tf_op jit(solution)/shard_map/pallas_call | solution.py:120
  109.5 2.3 %collective-permute-start.16 = (f32[1,1,64,128]{3,2,1,0:T(8,128)}, f32[1,1,64,128]{3,2,1,0:T(8,128)S(1)}, u32[]{:S(2)}, u32[]{:S(2)}) collective-permute-start(f32[1,1,64,128]{3,2,1,0:T(8,128)} %get-tuple-element.51), channel_id=1, source_target_pairs={{2,0},{4,2},{6,4},{8,6},{10,8},{12,10},{14,12},{16,14},{18,16},{20... | collective-permute-start | bytes 98312 | tf_op jit(solution)/shard_map/ppermute | solution.py:19
  111.8 4.0 %collective-permute-done.16.right_ref = f32[1,1,64,128]{3,2,1,0:T(8,128)S(1)} collective-permute-done((f32[1,1,64,128]{3,2,1,0:T(8,128)}, f32[1,1,64,128]{3,2,1,0:T(8,128)S(1)}, u32[]{:S(2)}, u32[]{:S(2)}) %collective-permute-start.16) | collective-permute-done | bytes 32800 | tf_op jit(solution)/shard_map/ppermute | solution.py:19
  (64 shorter events, 32.2 us)
Async XLA Ops:
  2.7 8.1 %collective-permute-start = (f32[3,1,64,128]{3,2,1,0:T(8,128)}, f32[3,1,64,128]{3,2,1,0:T(8,128)S(1)}, u32[]{:S(2)}, u32[]{:S(2)}) collective-permute-start(f32[3,1,64,128]{3,2,1,0:T(8,128)} %get-tuple-element.29), channel_id=1, source_target_pairs={{2,0},{4,2},{6,4},{8,6},{10,8},{12,10},{14,12},{16,14},{18,16},{20... | collective-permute-start | bytes 294920 | tf_op jit(solution)/shard_map/ppermute | solution.py:19
  5.3 5.5 %collective-permute-start.1 = (f32[2,1,64,128]{3,2,1,0:T(8,128)}, f32[2,1,64,128]{3,2,1,0:T(8,128)S(1)}, u32[]{:S(2)}, u32[]{:S(2)}) collective-permute-start(f32[2,1,64,128]{3,2,1,0:T(8,128)} %get-tuple-element.30), channel_id=1, source_target_pairs={{0,2},{2,4},{4,6},{6,8},{8,10},{10,12},{12,14},{14,16},{16,18},{18... | collective-permute-start | bytes 196616 | tf_op jit(solution)/shard_map/ppermute | solution.py:19
  14.2 7.0 %collective-permute-start.2 = (f32[2,1,64,128]{3,2,1,0:T(8,128)}, f32[2,1,64,128]{3,2,1,0:T(8,128)S(1)}, u32[]{:S(2)}, u32[]{:S(2)}) collective-permute-start(f32[2,1,64,128]{3,2,1,0:T(8,128)} %get-tuple-element.33), channel_id=1, source_target_pairs={{0,2},{2,4},{4,6},{6,8},{8,10},{10,12},{12,14},{14,16},{16,18},{18... | collective-permute-start | bytes 196616 | tf_op jit(solution)/shard_map/ppermute | solution.py:19
  19.3 6.7 %collective-permute-start.3 = (f32[2,1,64,128]{3,2,1,0:T(8,128)}, f32[2,1,64,128]{3,2,1,0:T(8,128)S(1)}, u32[]{:S(2)}, u32[]{:S(2)}) collective-permute-start(f32[2,1,64,128]{3,2,1,0:T(8,128)} %get-tuple-element.34), channel_id=1, source_target_pairs={{2,0},{4,2},{6,4},{8,6},{10,8},{12,10},{14,12},{16,14},{18,16},{20... | collective-permute-start | bytes 196616 | tf_op jit(solution)/shard_map/ppermute | solution.py:19
  21.2 4.8 %copy-start.5 = (f32[2,1,64,128]{3,2,1,0:T(8,128)}, f32[2,1,64,128]{3,2,1,0:T(8,128)S(1)}, u32[]{:S(2)}) copy-start(f32[2,1,64,128]{3,2,1,0:T(8,128)S(1)} %collective-permute-done.2.left_ref) | copy-start | bytes 196612
  29.3 4.3 %collective-permute-start.4 = (f32[2,1,64,128]{3,2,1,0:T(8,128)}, f32[2,1,64,128]{3,2,1,0:T(8,128)S(1)}, u32[]{:S(2)}, u32[]{:S(2)}) collective-permute-start(f32[2,1,64,128]{3,2,1,0:T(8,128)} %get-tuple-element.36), channel_id=1, source_target_pairs={{0,2},{2,4},{4,6},{6,8},{8,10},{10,12},{12,14},{14,16},{16,18},{18... | collective-permute-start | bytes 196616 | tf_op jit(solution)/shard_map/ppermute | solution.py:19
  31.2 6.7 %collective-permute-start.5 = (f32[2,1,64,128]{3,2,1,0:T(8,128)}, f32[2,1,64,128]{3,2,1,0:T(8,128)S(1)}, u32[]{:S(2)}, u32[]{:S(2)}) collective-permute-start(f32[2,1,64,128]{3,2,1,0:T(8,128)} %get-tuple-element.37), channel_id=1, source_target_pairs={{2,0},{4,2},{6,4},{8,6},{10,8},{12,10},{14,12},{16,14},{18,16},{20... | collective-permute-start | bytes 196616 | tf_op jit(solution)/shard_map/ppermute | solution.py:19
  33.6 4.3 %copy-start.6 = (f32[2,1,64,128]{3,2,1,0:T(8,128)}, f32[2,1,64,128]{3,2,1,0:T(8,128)S(1)}, u32[]{:S(2)}) copy-start(f32[2,1,64,128]{3,2,1,0:T(8,128)S(1)} %collective-permute-done.4.left_ref) | copy-start | bytes 196612
  41.2 4.3 %collective-permute-start.6 = (f32[2,1,64,128]{3,2,1,0:T(8,128)}, f32[2,1,64,128]{3,2,1,0:T(8,128)S(1)}, u32[]{:S(2)}, u32[]{:S(2)}) collective-permute-start(f32[2,1,64,128]{3,2,1,0:T(8,128)} %get-tuple-element.39), channel_id=1, source_target_pairs={{0,2},{2,4},{4,6},{6,8},{8,10},{10,12},{12,14},{14,16},{16,18},{18... | collective-permute-start | bytes 196616 | tf_op jit(solution)/shard_map/ppermute | solution.py:19
  43.2 6.7 %collective-permute-start.7 = (f32[2,1,64,128]{3,2,1,0:T(8,128)}, f32[2,1,64,128]{3,2,1,0:T(8,128)S(1)}, u32[]{:S(2)}, u32[]{:S(2)}) collective-permute-start(f32[2,1,64,128]{3,2,1,0:T(8,128)} %get-tuple-element.40), channel_id=1, source_target_pairs={{2,0},{4,2},{6,4},{8,6},{10,8},{12,10},{14,12},{16,14},{18,16},{20... | collective-permute-start | bytes 196616 | tf_op jit(solution)/shard_map/ppermute | solution.py:19
  45.5 4.3 %copy-start.11 = (f32[2,1,64,128]{3,2,1,0:T(8,128)}, f32[2,1,64,128]{3,2,1,0:T(8,128)S(1)}, u32[]{:S(2)}) copy-start(f32[2,1,64,128]{3,2,1,0:T(8,128)S(1)} %collective-permute-done.6.left_ref) | copy-start | bytes 196612
  54.1 13.9 %collective-permute-start.8 = (f32[2,4,2,64,128]{4,3,2,1,0:T(8,128)S(1)}, f32[2,4,2,64,128]{4,3,2,1,0:T(8,128)S(1)}, u32[]{:S(2)}, u32[]{:S(2)}) collective-permute-start(f32[2,4,2,64,128]{4,3,2,1,0:T(8,128)S(1)} %pad_maximum_fusion), channel_id=1, source_target_pairs={{0,1},{2,3},{4,5},{6,7},{8,9},{10,11},{12,13},{14,15},{16,17},{18,... | collective-permute-start | bytes 1572872 | tf_op jit(solution)/shard_map/ppermute | solution.py:19
  70.7 6.7 %collective-permute-start.10 = (f32[2,1,64,128]{3,2,1,0:T(8,128)}, f32[2,1,64,128]{3,2,1,0:T(8,128)S(1)}, u32[]{:S(2)}, u32[]{:S(2)}) collective-permute-start(f32[2,1,64,128]{3,2,1,0:T(8,128)} %get-tuple-element.42), channel_id=1, source_target_pairs={{2,0},{4,2},{6,4},{8,6},{10,8},{12,10},{14,12},{16,14},{18,16},{20... | collective-permute-start | bytes 196616 | tf_op jit(solution)/shard_map/ppermute | solution.py:19
  72.6 6.2 %collective-permute-start.9 = (f32[2,1,64,128]{3,2,1,0:T(8,128)}, f32[2,1,64,128]{3,2,1,0:T(8,128)S(1)}, u32[]{:S(2)}, u32[]{:S(2)}) collective-permute-start(f32[2,1,64,128]{3,2,1,0:T(8,128)} %get-tuple-element.41), channel_id=1, source_target_pairs={{0,2},{2,4},{4,6},{6,8},{8,10},{10,12},{12,14},{14,16},{16,18},{18... | collective-permute-start | bytes 196616 | tf_op jit(solution)/shard_map/ppermute | solution.py:19
  82.0 7.0 %collective-permute-start.11 = (f32[1,1,64,128]{3,2,1,0:T(8,128)}, f32[1,1,64,128]{3,2,1,0:T(8,128)S(1)}, u32[]{:S(2)}, u32[]{:S(2)}) collective-permute-start(f32[1,1,64,128]{3,2,1,0:T(8,128)} %get-tuple-element.44), channel_id=1, source_target_pairs={{0,2},{2,4},{4,6},{6,8},{8,10},{10,12},{12,14},{14,16},{16,18},{18... | collective-permute-start | bytes 98312 | tf_op jit(solution)/shard_map/ppermute | solution.py:19
  87.1 6.3 %collective-permute-start.12 = (f32[1,1,64,128]{3,2,1,0:T(8,128)}, f32[1,1,64,128]{3,2,1,0:T(8,128)S(1)}, u32[]{:S(2)}, u32[]{:S(2)}) collective-permute-start(f32[1,1,64,128]{3,2,1,0:T(8,128)} %get-tuple-element.45), channel_id=1, source_target_pairs={{2,0},{4,2},{6,4},{8,6},{10,8},{12,10},{14,12},{16,14},{18,16},{20... | collective-permute-start | bytes 98312 | tf_op jit(solution)/shard_map/ppermute | solution.py:19
  89.0 4.4 %copy-start.15 = (f32[1,1,64,128]{3,2,1,0:T(8,128)}, f32[1,1,64,128]{3,2,1,0:T(8,128)S(1)}, u32[]{:S(2)}) copy-start(f32[1,1,64,128]{3,2,1,0:T(8,128)S(1)} %collective-permute-done.11.left_ref) | copy-start | bytes 98308
  96.3 4.3 %collective-permute-start.13 = (f32[1,1,64,128]{3,2,1,0:T(8,128)}, f32[1,1,64,128]{3,2,1,0:T(8,128)S(1)}, u32[]{:S(2)}, u32[]{:S(2)}) collective-permute-start(f32[1,1,64,128]{3,2,1,0:T(8,128)} %get-tuple-element.47), channel_id=1, source_target_pairs={{0,2},{2,4},{4,6},{6,8},{8,10},{10,12},{12,14},{14,16},{16,18},{18... | collective-permute-start | bytes 98312 | tf_op jit(solution)/shard_map/ppermute | solution.py:19
  98.3 6.3 %collective-permute-start.14 = (f32[1,1,64,128]{3,2,1,0:T(8,128)}, f32[1,1,64,128]{3,2,1,0:T(8,128)S(1)}, u32[]{:S(2)}, u32[]{:S(2)}) collective-permute-start(f32[1,1,64,128]{3,2,1,0:T(8,128)} %get-tuple-element.48), channel_id=1, source_target_pairs={{2,0},{4,2},{6,4},{8,6},{10,8},{12,10},{14,12},{16,14},{18,16},{20... | collective-permute-start | bytes 98312 | tf_op jit(solution)/shard_map/ppermute | solution.py:19
  100.6 4.0 %copy-start.17 = (f32[1,1,64,128]{3,2,1,0:T(8,128)}, f32[1,1,64,128]{3,2,1,0:T(8,128)S(1)}, u32[]{:S(2)}) copy-start(f32[1,1,64,128]{3,2,1,0:T(8,128)S(1)} %collective-permute-done.13.left_ref) | copy-start | bytes 98308
  105.2 13.2 %copy-start = (f32[2,4,2,64,128]{4,3,2,1,0:T(8,128)S(1)}, f32[2,4,2,64,128]{4,3,2,1,0:T(8,128)}, u32[]{:S(2)}) copy-start(f32[2,4,2,64,128]{4,3,2,1,0:T(8,128)} %shard_map.97) | copy-start | bytes 1572868
  105.2 13.2 %copy-start.2 = (f32[2,4,2,64,128]{4,3,2,1,0:T(8,128)S(1)}, f32[2,4,2,64,128]{4,3,2,1,0:T(8,128)}, u32[]{:S(2)}) copy-start(f32[2,4,2,64,128]{4,3,2,1,0:T(8,128)} %get-tuple-element.43.s_ref) | copy-start | bytes 1572868
  107.4 4.3 %collective-permute-start.15 = (f32[1,1,64,128]{3,2,1,0:T(8,128)}, f32[1,1,64,128]{3,2,1,0:T(8,128)S(1)}, u32[]{:S(2)}, u32[]{:S(2)}) collective-permute-start(f32[1,1,64,128]{3,2,1,0:T(8,128)} %get-tuple-element.50), channel_id=1, source_target_pairs={{0,2},{2,4},{4,6},{6,8},{8,10},{10,12},{12,14},{14,16},{16,18},{18... | collective-permute-start | bytes 98312 | tf_op jit(solution)/shard_map/ppermute | solution.py:19
  109.5 6.3 %collective-permute-start.16 = (f32[1,1,64,128]{3,2,1,0:T(8,128)}, f32[1,1,64,128]{3,2,1,0:T(8,128)S(1)}, u32[]{:S(2)}, u32[]{:S(2)}) collective-permute-start(f32[1,1,64,128]{3,2,1,0:T(8,128)} %get-tuple-element.51), channel_id=1, source_target_pairs={{2,0},{4,2},{6,4},{8,6},{10,8},{12,10},{14,12},{16,14},{18,16},{20... | collective-permute-start | bytes 98312 | tf_op jit(solution)/shard_map/ppermute | solution.py:19
  (12 other events, 11.8 us)

commit v5 on v4

v5 whole, which is shorter than its diff:
```python
import functools

import jax
import jax.numpy as jnp
from jax import lax
from jax.experimental import pallas as pl
from jax.experimental.pallas import tpu as pltpu
from jax.sharding import PartitionSpec as P

STEPS = 4


DT_COARSE = 0.4


def from_behind(x, axis, by):
    size = lax.axis_size(axis)
    pairs = [(i, i + by) for i in range(size) if 0 <= i + by < size]
    return lax.ppermute(x, axis, pairs)


def roll(x, shift, axis):
    return pltpu.roll(x, shift % x.shape[axis], axis)


def nsum(values, offset, axis):
    return values + roll(values, offset, axis)


def forces(pressure, lower):
    combined = pressure + lower
    force_x = 0.25 * (nsum(nsum(lower, 1, 1), 1, 0) - nsum(nsum(pressure, 1, 1), 1, 0))
    across_z = nsum(combined, 1, 1)
    force_y = 0.25 * (roll(across_z, 1, 0) - across_z)
    across_y = nsum(combined, 1, 0)
    force_z = 0.25 * (roll(across_y, 1, 1) - across_y)
    return force_x, force_y, force_z


def divergence(v, u):
    diff_x = nsum(nsum(u[0] - v[0], -1, 1), -1, 0)
    sum_y = nsum(v[1] + u[1], -1, 1)
    diff_y = roll(sum_y, -1, 0) - sum_y
    sum_z = nsum(v[2] + u[2], -1, 0)
    diff_z = roll(sum_z, -1, 1) - sum_z
    return 0.25 * (diff_x + diff_y + diff_z)


def upper_part(u):
    diff_x = nsum(nsum(u[0], -1, 1), -1, 0)
    sum_y = nsum(u[1], -1, 1)
    diff_y = roll(sum_y, -1, 0) - sum_y
    sum_z = nsum(u[2], -1, 0)
    diff_z = roll(sum_z, -1, 1) - sum_z
    return diff_x + diff_y + diff_z


def lower_part(v):
    diff_x = nsum(nsum(-v[0], -1, 1), -1, 0)
    sum_y = nsum(v[1], -1, 1)
    diff_y = roll(sum_y, -1, 0) - sum_y
    sum_z = nsum(v[2], -1, 0)
    diff_z = roll(sum_z, -1, 1) - sum_z
    return diff_x + diff_y + diff_z


def outgoing(pressure_first, velocity_first, mass_first, step_size):
    f = forces(pressure_first, jnp.zeros_like(pressure_first))
    hm = step_size * mass_first
    return upper_part([velocity_first[c] + hm * f[c] for c in range(3)])


def messages(pres, vel, k_ref, m_ref, step_size):
    n = len(pres)
    last_node = [vel[n - 1][c] + step_size * m_ref[n - 1] * f
                 for c, f in enumerate(forces(pres[n - 1], pres[n - 2]))]
    behind = pres[n - 1] - step_size * k_ref[n - 1] * (0.25 * lower_part(last_node))
    f0 = forces(pres[0], jnp.zeros_like(pres[0]))
    partial = [vel[0][c] + step_size * m_ref[0] * f0[c] for c in range(3)]
    second = [vel[1][c] + step_size * m_ref[1] * f for c, f in enumerate(forces(pres[1], pres[0]))]
    ahead = pres[0] - step_size * k_ref[0] * (0.25 * (lower_part(partial) + upper_part(second)))
    return (pres[n - 1], behind), (upper_part(partial), ahead)


def plane_list(ref, b):
    n = ref.shape[2]
    return [ref[b, 0, i] for i in range(n)], [[ref[b, 1 + c, i] for c in range(3)] for i in range(n)]


def write_messages(b, msgs, right_out, left_out):
    (p_last, behind), (share, ahead) = msgs
    right_out[2 * b] = p_last
    right_out[2 * b + 1] = behind
    left_out[2 * b] = share
    left_out[2 * b + 1] = ahead


def pair_kernel(sizes, counts, next_count, first, s_ref, k_ref, m_ref, c_ref, fl_ref, fr_ref,
                s_out, *outs):
    n = s_ref.shape[2]
    width = 2 * len(sizes)
    if first:
        next_mass, next_stiff, prev_stiff = fr_ref[width], fr_ref[width + 1], fl_ref[width]
    else:
        next_mass, next_stiff, prev_stiff = c_ref[0], c_ref[1], c_ref[2]
    zero = jnp.zeros_like(next_mass)
    for b, (h, count) in enumerate(zip(sizes, counts)):
        pres, vel = plane_list(s_ref, b)
        lower = [fl_ref[2 * b]] + pres[:-1]
        vel1 = [[vel[i][c] + h * m_ref[i] * f for c, f in enumerate(forces(pres[i], lower[i]))]
                for i in range(n)]
        pres1 = [pres[i] - h * k_ref[i] * divergence(vel1[i], vel1[i + 1]) for i in range(n - 1)]
        below = [h * next_mass * f for f in forces(zero, pres[n - 1])]
        upper1 = fr_ref[2 * b] + upper_part(below)
        pres1.append(pres[n - 1] - h * k_ref[n - 1] * (0.25 * (lower_part(vel1[n - 1]) + upper1)))
        if count == 2:
            prev1 = fl_ref[2 * b + 1] - h * prev_stiff * (0.25 * upper_part(vel1[0]))
            next1 = fr_ref[2 * b + 1] - h * next_stiff * (0.25 * lower_part(below))
            lower = [prev1] + pres1[:-1]
            vel2 = [[vel1[i][c] + h * m_ref[i] * f for c, f in enumerate(forces(pres1[i], lower[i]))]
                    for i in range(n)]
            pres2 = [pres1[i] - h * k_ref[i] * divergence(vel2[i], vel2[i + 1]) for i in range(n - 1)]
            upper2 = upper1 + upper_part([h * next_mass * f for f in forces(next1, pres1[n - 1])])
            pres2.append(pres1[n - 1] - h * k_ref[n - 1] * (0.25 * (lower_part(vel2[n - 1]) + upper2)))
            pres1, vel1 = pres2, vel2
        for i in range(n):
            s_out[b, 0, i] = pres1[i]
            for c in range(3):
                s_out[b, 1 + c, i] = vel1[i][c]
        if b < next_count:
            write_messages(b, messages(pres1, vel1, k_ref, m_ref, h), outs[0], outs[1])
    if first:
        outs[-1][0] = next_mass
        outs[-1][1] = next_stiff
        outs[-1][2] = prev_stiff


def planes(count, like):
    return jax.ShapeDtypeStruct((count,) + like.shape[-2:], like.dtype)


def advance(state, to_right, to_left, stiffness, inv_mass, consts, sizes, counts, next_count):
    from_left = from_behind(to_right, "space", 1)
    from_right = from_behind(to_left, "space", -1)
    first = consts is None
    if first:
        consts = from_left
    outs = [jax.ShapeDtypeStruct((len(sizes),) + state.shape[1:], state.dtype)]
    if next_count:
        outs += [planes(2 * next_count, state), planes(2 * next_count, state)]
    if first:
        outs.append(planes(3, state))
    return pl.pallas_call(
        functools.partial(pair_kernel, tuple(sizes), tuple(counts), next_count, first),
        out_shape=tuple(outs),
    )(state, stiffness, inv_mass, consts, from_left, from_right)


def start_kernel(step_size, gp_ref, gv_ref, ip_ref, iv_ref, k_ref, m_ref, s_out, right_out, left_out):
    n = ip_ref.shape[0]
    sources = (
        ([gp_ref[0, i] for i in range(n)], [[gv_ref[0, c, i] for c in range(3)] for i in range(n)]),
        ([ip_ref[i] for i in range(n)], [[iv_ref[c, i] for c in range(3)] for i in range(n)]),
    )
    for b, (pres, vel) in enumerate(sources):
        for i in range(n):
            s_out[b, 0, i] = pres[i]
            for c in range(3):
                s_out[b, 1 + c, i] = vel[i][c]
        write_messages(b, messages(pres, vel, k_ref, m_ref, step_size), right_out, left_out)
    right_out[4] = k_ref[n - 1]
    left_out[4] = m_ref[0]
    left_out[5] = k_ref[0]


def late_kernel(sizes, got_ref, own_ref, k_ref, m_ref, s_out, right_out, left_out):
    n = got_ref.shape[1]
    for i in range(n):
        for c in range(4):
            s_out[0, c, i] = got_ref[c, i]
            s_out[1, c, i] = own_ref[1, c, i] - got_ref[c, i]
    for b, h in enumerate(sizes):
        pres, vel = plane_list(s_out, b)
        write_messages(b, messages(pres, vel, k_ref, m_ref, h), right_out, left_out)


def chain_kernel(step_size, s_ref, k_ref, m_ref, right_out, left_out):
    pres, vel = plane_list(s_ref, 0)
    write_messages(0, messages(pres, vel, k_ref, m_ref, step_size), right_out, left_out)


def coarse(carried, stiffness, inv_mass, consts):
    to_right, to_left = pl.pallas_call(
        functools.partial(chain_kernel, DT_COARSE),
        out_shape=(planes(2, carried), planes(2, carried)),
    )(carried, stiffness, inv_mass)
    (out,) = advance(carried, to_right, to_left, stiffness, inv_mass, consts, (DT_COARSE,), (1,), 0)
    return out[0]


def on_device(
    guess_pressure, guess_velocity, initial_pressure, initial_velocity, stiffness, inv_mass
):
    fine_size = DT_COARSE / STEPS
    groups = lax.axis_size("tm")
    group = lax.axis_index("tm")
    assert stiffness.shape[0] >= 2 and STEPS % 2 == 0

    state_shape = jax.ShapeDtypeStruct((2, 4) + stiffness.shape, stiffness.dtype)
    state, to_right, to_left = pl.pallas_call(
        functools.partial(start_kernel, fine_size),
        out_shape=(state_shape, planes(5, stiffness), planes(6, stiffness)),
    )(guess_pressure, guess_velocity, initial_pressure, initial_velocity, stiffness, inv_mass)
    rounds = STEPS // 2
    fine2 = (fine_size, fine_size)
    state, to_right, to_left, consts = advance(
        state, to_right, to_left, stiffness, inv_mass, None, fine2, (2, 2), 2 if rounds > 1 else 0
    )
    for repeat in range(1, rounds):
        count = 2 if repeat + 1 < rounds else 0
        outs = advance(state, to_right, to_left, stiffness, inv_mass, consts, fine2, (2, 2), count)
        state = outs[0]
        if count:
            to_right, to_left = outs[1], outs[2]
    relaxed, own_end = state[0], state[1]

    got = from_behind(relaxed, "tm", 1)
    late, to_right, to_left = pl.pallas_call(
        functools.partial(late_kernel, (fine_size, DT_COARSE)),
        out_shape=(state_shape, planes(4, stiffness), planes(4, stiffness)),
    )(got, state, stiffness, inv_mass)
    both = None
    for repeat in range(rounds):
        count = 1 if repeat + 1 < rounds else 0
        if repeat == 0:
            sizes, counts = (fine_size, DT_COARSE), (2, 1)
        else:
            sizes, counts = (fine_size,), (2,)
        outs = advance(late, to_right, to_left, stiffness, inv_mass, consts, sizes, counts, count)
        late = outs[0]
        if repeat == 0:
            both = late
        if count:
            to_right, to_left = outs[1], outs[2]

    end = jnp.where(group == 0, own_end, late[0])
    resid = end - relaxed
    if groups == 2:
        error = resid + jnp.where(group == 0, jnp.zeros_like(resid), both[1])
    else:
        error, carried = resid, resid
        for repeat in range(groups - 1):
            carried = from_behind(carried, "tm", 1)
            carried = coarse(carried[None], stiffness, inv_mass, consts)
            error = error + carried
    corrected = relaxed + error
    return (corrected[0][None], corrected[1:][None], resid[0][None], resid[1:][None])


def solution(mesh):
    placed = (
        P("tm", "space", None, None),
        P("tm", None, "space", None, None),
        P("space", None, None),
        P(None, "space", None, None),
        P("space", None, None),
        P("space", None, None),
    )
    return jax.shard_map(
        on_device,
        mesh=mesh,
        in_specs=placed,
        out_specs=(
            P("tm", "space", None, None),
            P("tm", None, "space", None, None),
            P("tm", "space", None, None),
            P("tm", None, "space", None, None),
        ),
        check_vma=False,
    )
```

time: 122 us -> 75.9 us (0.62)
  starting transfers between devices: 45.4 us -> 25.5 us
  waiting for transfers between devices: 41.6 us -> 24.1 us
  Pallas kernels: 23.6 us -> 17.6 us
  local copies, waits for them, and re-layouts: 7.88 us -> 6.37 us
    ppermute x17 -> x9, starting transfers between devices: 45.4 us -> 25.5 us  [from_behind(): return lax.ppermute(x, axis, pairs)]
    ppermute x17 -> x9, waiting for transfers between devices: 41.6 us -> 24.1 us  [from_behind(): return lax.ppermute(x, axis, pairs)]
    pallas_call x9 -> x5, Pallas kernels: 21.5 us -> 15.3 us  [the longest x4 13.1 us: advance(): pl.pallas_call(functools.partial(pair_kernel, tuple(sizes), tuple(counts)...]
    unnamed x38 -> x22, local copies, waits for them, and re-layouts: 5.85 us -> 3.37 us
  transfers between devices with their start and end apart: 17 -> 9, of which waited for: 10 -> 7; matrix products, arithmetic and copies ran while one was open for 0% -> 0% of each run, Pallas kernels for 0% -> 0%
where the time goes in v5:
time: 75.9 us; the launch traced here: 75.4 us
  starting transfers between devices  25.5 us (34%)
  waiting for transfers between devices  24.1 us (32%)
  Pallas kernels  17.6 us (23%)
  local copies, waits for them, and re-layouts  6.37 us (8%)
  other arithmetic  1.02 us (1%)
    ppermute x9, starting transfers between devices, from_behind(): return lax.ppermute(x, axis, pairs)  25.5 us
    ppermute x9, waiting for transfers between devices, from_behind(): return lax.ppermute(x, axis, pairs)  24.1 us
    pallas_call x4, Pallas kernels, advance(): pl.pallas_call(functools.partial(pair_kernel, tuple(sizes), tuple(counts)...  13.1 us
    unnamed x22, local copies, waits for them, and re-layouts  3.37 us
    pallas_call x1, Pallas kernels, on_device(): pl.pallas_call(functools.partial(late_kernel, (fine_size, DT_COARSE)), ou...  2.29 us
    pallas_call x1, Pallas kernels, on_device(): pl.pallas_call(functools.partial(start_kernel, fine_size), out_shape=(sta...  2.25 us
  transfers between devices with their start and end apart: 9, of which 7 were waited for; matrix products, arithmetic and copies ran while one was open for 0% of the time, Pallas kernels for 0%

profile of v5, /device:TPU:7, one launch (start us, length us, event | category | flops | bytes accessed | tf_op | source)
XLA Modules:
  0.0 75.4 jit_solution(4908491853854355519)
XLA Ops:
  0.6 2.3 %shard_map.93 = (f32[2,4,2,64,128]{4,3,2,1,0:T(8,128)}, f32[5,64,128]{2,1,0:T(8,128)}, f32[6,64,128]{2,1,0:T(8,128)}) custom-call(f32[1,2,64,128]{3,2,1,0:T(8,128)} %gp_ref.1, f32[1,3,2,64,128]{4,3,2,1,0:T(8,128)} %gv_ref.1, f32[2,64,128]{2,1,0:T(8,128)} %ip_ref.1, f32[3,2,64,128]{3,2,1,0:T(8,128)} %iv_ref.1, f32[2,64,128]{2,1,0:T(8,128)} %k_ref.11, ...), custom_call_target="tpu_custom_call" | custom-call | tf_op jit(solution)/shard_map/pallas_call | solution.py:210
  2.9 2.6 %collective-permute-start.1 = (f32[6,64,128]{2,1,0:T(8,128)}, f32[6,64,128]{2,1,0:T(8,128)S(1)}, u32[]{:S(2)}, u32[]{:S(2)}) collective-permute-start(f32[6,64,128]{2,1,0:T(8,128)} %get-tuple-element.19), channel_id=1, source_target_pairs={{2,0},{4,2},{6,4},{8,6},{10,8},{12,10},{14,12},{16,14},{18,16},{20... | collective-permute-start | bytes 589832 | tf_op jit(solution)/shard_map/ppermute | solution.py:19
  5.5 3.9 %collective-permute-start = (f32[5,64,128]{2,1,0:T(8,128)}, f32[5,64,128]{2,1,0:T(8,128)S(1)}, u32[]{:S(2)}, u32[]{:S(2)}) collective-permute-start(f32[5,64,128]{2,1,0:T(8,128)} %get-tuple-element.18), channel_id=1, source_target_pairs={{0,2},{2,4},{4,6},{6,8},{8,10},{10,12},{12,14},{14,16},{16,18},{18... | collective-permute-start | bytes 491528 | tf_op jit(solution)/shard_map/ppermute | solution.py:19
  9.3 2.6 %collective-permute-done.c_ref.fl_ref = f32[5,64,128]{2,1,0:T(8,128)S(1)} collective-permute-done((f32[5,64,128]{2,1,0:T(8,128)}, f32[5,64,128]{2,1,0:T(8,128)S(1)}, u32[]{:S(2)}, u32[]{:S(2)}) %collective-permute-start) | collective-permute-done | bytes 163872 | tf_op jit(solution)/shard_map/ppermute | solution.py:19
  12.6 3.8 %shard_map.94 = (f32[2,4,2,64,128]{4,3,2,1,0:T(8,128)}, f32[4,64,128]{2,1,0:T(8,128)}, f32[4,64,128]{2,1,0:T(8,128)}, f32[3,64,128]{2,1,0:T(8,128)}) custom-call(f32[2,4,2,64,128]{4,3,2,1,0:T(8,128)} %get-tuple-element.17.s_ref, f32[2,64,128]{2,1,0:T(8,128)} %k_ref.11, f32[2,64,128]{2,1,0:T(8,128)} %m_ref.11, f32[5,64,128]{2,1,0:T(8,128)} %copy-done.2, ...), custom_call_target="tpu_custom_call" | custom-call | tf_op jit(solution)/shard_map/pallas_call | solution.py:153
  16.5 5.2 %collective-permute-start.2 = (f32[4,64,128]{2,1,0:T(8,128)}, f32[4,64,128]{2,1,0:T(8,128)S(1)}, u32[]{:S(2)}, u32[]{:S(2)}) collective-permute-start(f32[4,64,128]{2,1,0:T(8,128)} %get-tuple-element.22), channel_id=1, source_target_pairs={{0,2},{2,4},{4,6},{6,8},{8,10},{10,12},{12,14},{14,16},{16,18},{18... | collective-permute-start | bytes 393224 | tf_op jit(solution)/shard_map/ppermute | solution.py:19
  21.6 1.9 %collective-permute-start.3 = (f32[4,64,128]{2,1,0:T(8,128)}, f32[4,64,128]{2,1,0:T(8,128)S(1)}, u32[]{:S(2)}, u32[]{:S(2)}) collective-permute-start(f32[4,64,128]{2,1,0:T(8,128)} %get-tuple-element.23), channel_id=1, source_target_pairs={{2,0},{4,2},{6,4},{8,6},{10,8},{12,10},{14,12},{16,14},{18,16},{20... | collective-permute-start | bytes 393224 | tf_op jit(solution)/shard_map/ppermute | solution.py:19
  23.9 5.2 %collective-permute-done.3.fr_ref = f32[4,64,128]{2,1,0:T(8,128)S(1)} collective-permute-done((f32[4,64,128]{2,1,0:T(8,128)}, f32[4,64,128]{2,1,0:T(8,128)S(1)}, u32[]{:S(2)}, u32[]{:S(2)}) %collective-permute-start.3) | collective-permute-done | bytes 131104 | tf_op jit(solution)/shard_map/ppermute | solution.py:19
  29.7 3.3 %shard_map.95.own_ref = f32[2,4,2,64,128]{4,3,2,1,0:T(8,128)} custom-call(f32[2,4,2,64,128]{4,3,2,1,0:T(8,128)} %get-tuple-element.20.s_ref, f32[2,64,128]{2,1,0:T(8,128)} %k_ref.11, f32[2,64,128]{2,1,0:T(8,128)} %m_ref.11, f32[3,64,128]{2,1,0:T(8,128)} %get-tuple-element.21.c_ref, f32[4,64,128]{2,1,0:T(8,128)} %copy-done.5, f32[4,64,128]{2,1,0:T(8,128)} %copy-done.6), custom_call_target="tpu_custom_call" | custom-call | tf_op jit(solution)/shard_map/pallas_call | solution.py:153
  33.0 1.0 %slice_bitcast_fusion = f32[4,2,64,128]{3,2,1,0:T(8,128)S(1)} fusion(f32[2,4,2,64,128]{4,3,2,1,0:T(8,128)} %shard_map.95.own_ref), kind=kLoop, calls=%fused_computation.3 | loop fusion | bytes 524288 | tf_op jit(solution)/shard_map/squeeze | solution.py:225
  34.0 1.3 %collective-permute-start.4 = (f32[4,2,64,128]{3,2,1,0:T(8,128)S(1)}, f32[4,2,64,128]{3,2,1,0:T(8,128)S(1)}, u32[]{:S(2)}, u32[]{:S(2)}) collective-permute-start(f32[4,2,64,128]{3,2,1,0:T(8,128)S(1)} %slice_bitcast_fusion), channel_id=1, source_target_pairs={{0,1},{2,3},{4,5},{6,7},{8,9},{10,11},{12,13},{14,15},{16,17},{18,... | collective-permute-start | bytes 786440 | tf_op jit(solution)/shard_map/ppermute | solution.py:19
  35.3 6.4 %collective-permute-done.4.got_ref = f32[4,2,64,128]{3,2,1,0:T(8,128)S(1)} collective-permute-done((f32[4,2,64,128]{3,2,1,0:T(8,128)S(1)}, f32[4,2,64,128]{3,2,1,0:T(8,128)S(1)}, u32[]{:S(2)}, u32[]{:S(2)}) %collective-permute-start.4) | collective-permute-done | bytes 262176 | tf_op jit(solution)/shard_map/ppermute | solution.py:19
  41.7 0.7 copy-done.3
  42.4 2.3 %shard_map.96 = (f32[2,4,2,64,128]{4,3,2,1,0:T(8,128)}, f32[4,64,128]{2,1,0:T(8,128)}, f32[4,64,128]{2,1,0:T(8,128)}) custom-call(f32[4,2,64,128]{3,2,1,0:T(8,128)} %copy-done.3, f32[2,4,2,64,128]{4,3,2,1,0:T(8,128)} %shard_map.95.own_ref, f32[2,64,128]{2,1,0:T(8,128)} %k_ref.11, f32[2,64,128]{2,1,0:T(8,128)} %m_ref.11), custom_call_target="tpu_custom_call" | custom-call | tf_op jit(solution)/shard_map/pallas_call | solution.py:228
  44.7 4.4 %collective-permute-start.5 = (f32[4,64,128]{2,1,0:T(8,128)}, f32[4,64,128]{2,1,0:T(8,128)S(1)}, u32[]{:S(2)}, u32[]{:S(2)}) collective-permute-start(f32[4,64,128]{2,1,0:T(8,128)} %get-tuple-element.25), channel_id=1, source_target_pairs={{0,2},{2,4},{4,6},{6,8},{8,10},{10,12},{12,14},{14,16},{16,18},{18... | collective-permute-start | bytes 393224 | tf_op jit(solution)/shard_map/ppermute | solution.py:19
  49.1 1.9 %collective-permute-start.6 = (f32[4,64,128]{2,1,0:T(8,128)}, f32[4,64,128]{2,1,0:T(8,128)S(1)}, u32[]{:S(2)}, u32[]{:S(2)}) collective-permute-start(f32[4,64,128]{2,1,0:T(8,128)} %get-tuple-element.26), channel_id=1, source_target_pairs={{2,0},{4,2},{6,4},{8,6},{10,8},{12,10},{14,12},{16,14},{18,16},{20... | collective-permute-start | bytes 393224 | tf_op jit(solution)/shard_map/ppermute | solution.py:19
  51.3 5.2 %collective-permute-done.6.fr_ref = f32[4,64,128]{2,1,0:T(8,128)S(1)} collective-permute-done((f32[4,64,128]{2,1,0:T(8,128)}, f32[4,64,128]{2,1,0:T(8,128)S(1)}, u32[]{:S(2)}, u32[]{:S(2)}) %collective-permute-start.6) | collective-permute-done | bytes 131104 | tf_op jit(solution)/shard_map/ppermute | solution.py:19
  57.2 3.3 %shard_map.97 = (f32[2,4,2,64,128]{4,3,2,1,0:T(8,128)}, f32[2,64,128]{2,1,0:T(8,128)}, f32[2,64,128]{2,1,0:T(8,128)}) custom-call(f32[2,4,2,64,128]{4,3,2,1,0:T(8,128)} %get-tuple-element.24.s_ref, f32[2,64,128]{2,1,0:T(8,128)} %k_ref.11, f32[2,64,128]{2,1,0:T(8,128)} %m_ref.11, f32[3,64,128]{2,1,0:T(8,128)} %get-tuple-element.21.c_ref, ...), custom_call_target="tpu_custom_call" | custom-call | tf_op jit(solution)/shard_map/pallas_call | solution.py:153
  60.4 1.9 %collective-permute-start.7 = (f32[2,64,128]{2,1,0:T(8,128)}, f32[2,64,128]{2,1,0:T(8,128)S(1)}, u32[]{:S(2)}, u32[]{:S(2)}) collective-permute-start(f32[2,64,128]{2,1,0:T(8,128)} %get-tuple-element.28), channel_id=1, source_target_pairs={{0,2},{2,4},{4,6},{6,8},{8,10},{10,12},{12,14},{14,16},{16,18},{18... | collective-permute-start | bytes 196616 | tf_op jit(solution)/shard_map/ppermute | solution.py:19
  62.3 2.4 %collective-permute-start.8 = (f32[2,64,128]{2,1,0:T(8,128)}, f32[2,64,128]{2,1,0:T(8,128)S(1)}, u32[]{:S(2)}, u32[]{:S(2)}) collective-permute-start(f32[2,64,128]{2,1,0:T(8,128)} %get-tuple-element.29), channel_id=1, source_target_pairs={{2,0},{4,2},{6,4},{8,6},{10,8},{12,10},{14,12},{16,14},{18,16},{20... | collective-permute-start | bytes 196616 | tf_op jit(solution)/shard_map/ppermute | solution.py:19
  64.8 4.3 %collective-permute-done.8.fr_ref = f32[2,64,128]{2,1,0:T(8,128)S(1)} collective-permute-done((f32[2,64,128]{2,1,0:T(8,128)}, f32[2,64,128]{2,1,0:T(8,128)S(1)}, u32[]{:S(2)}, u32[]{:S(2)}) %collective-permute-start.8) | collective-permute-done | bytes 65568 | tf_op jit(solution)/shard_map/ppermute | solution.py:19
  69.7 2.6 %shard_map.98 = f32[1,4,2,64,128]{4,3,2,1,0:T(8,128)} custom-call(f32[2,4,2,64,128]{4,3,2,1,0:T(8,128)} %get-tuple-element.27.s_ref, f32[2,64,128]{2,1,0:T(8,128)} %k_ref.11, f32[2,64,128]{2,1,0:T(8,128)} %m_ref.11, f32[3,64,128]{2,1,0:T(8,128)} %get-tuple-element.21.c_ref, f32[2,64,128]{2,1,0:T(8,128)} %copy-done.9, f32[2,64,128]{2,1,0:T(8,128)} %copy-done.10), custom_call_target="tpu_custom_call" | custom-call | tf_op jit(solution)/shard_map/pallas_call | solution.py:153
  72.3 1.0 %fusion.2 = (f32[4,2,64,128]{3,2,1,0:T(8,128)S(1)}, f32[4,2,64,128]{3,2,1,0:T(8,128)S(1)}) fusion(f32[2,4,2,64,128]{4,3,2,1,0:T(8,128)S(1)} %copy-done.1, pred[]{:T(512)S(6)} %eq.4, f32[2,4,2,64,128]{4,3,2,1,0:T(8,128)S(1)} %copy-done, f32[1,4,2,64,128]{4,3,2,1,0:T(8,128)} %shard_map.98), kind=kLoop, calls=%fused_computation.5 | loop fusion | flops 327680 | bytes 1572865 | tf_op jit(solution)/shard_map/add | solution.py:256
  73.9 0.8 %slice_bitcast_fusion.1 = (f32[1,3,2,64,128]{4,3,2,1,0:T(8,128)}, f32[1,3,2,64,128]{4,3,2,1,0:T(8,128)}) fusion(f32[4,2,64,128]{3,2,1,0:T(8,128)S(1)} %get-tuple-element.31, f32[4,2,64,128]{3,2,1,0:T(8,128)S(1)} %get-tuple-element.30), kind=kLoop, calls=%fused_computation.6 | loop fusion | bytes 786432 | tf_op jit(solution)/shard_map/broadcast_in_dim | solution.py:257
  (27 shorter events, 4.6 us)
Async XLA Ops:
  2.9 9.0 %collective-permute-start.1 = (f32[6,64,128]{2,1,0:T(8,128)}, f32[6,64,128]{2,1,0:T(8,128)S(1)}, u32[]{:S(2)}, u32[]{:S(2)}) collective-permute-start(f32[6,64,128]{2,1,0:T(8,128)} %get-tuple-element.19), channel_id=1, source_target_pairs={{2,0},{4,2},{6,4},{8,6},{10,8},{12,10},{14,12},{16,14},{18,16},{20... | collective-permute-start | bytes 589832 | tf_op jit(solution)/shard_map/ppermute | solution.py:19
  5.5 6.4 %collective-permute-start = (f32[5,64,128]{2,1,0:T(8,128)}, f32[5,64,128]{2,1,0:T(8,128)S(1)}, u32[]{:S(2)}, u32[]{:S(2)}) collective-permute-start(f32[5,64,128]{2,1,0:T(8,128)} %get-tuple-element.18), channel_id=1, source_target_pairs={{0,2},{2,4},{4,6},{6,8},{8,10},{10,12},{12,14},{14,16},{16,18},{18... | collective-permute-start | bytes 491528 | tf_op jit(solution)/shard_map/ppermute | solution.py:19
  11.9 0.7 copy-start.2
  11.9 0.7 copy-start.4
  16.5 7.4 %collective-permute-start.2 = (f32[4,64,128]{2,1,0:T(8,128)}, f32[4,64,128]{2,1,0:T(8,128)S(1)}, u32[]{:S(2)}, u32[]{:S(2)}) collective-permute-start(f32[4,64,128]{2,1,0:T(8,128)} %get-tuple-element.22), channel_id=1, source_target_pairs={{0,2},{2,4},{4,6},{6,8},{8,10},{10,12},{12,14},{14,16},{16,18},{18... | collective-permute-start | bytes 393224 | tf_op jit(solution)/shard_map/ppermute | solution.py:19
  21.6 7.4 %collective-permute-start.3 = (f32[4,64,128]{2,1,0:T(8,128)}, f32[4,64,128]{2,1,0:T(8,128)S(1)}, u32[]{:S(2)}, u32[]{:S(2)}) collective-permute-start(f32[4,64,128]{2,1,0:T(8,128)} %get-tuple-element.23), channel_id=1, source_target_pairs={{2,0},{4,2},{6,4},{8,6},{10,8},{12,10},{14,12},{16,14},{18,16},{20... | collective-permute-start | bytes 393224 | tf_op jit(solution)/shard_map/ppermute | solution.py:19
  23.9 5.2 %copy-start.5 = (f32[4,64,128]{2,1,0:T(8,128)}, f32[4,64,128]{2,1,0:T(8,128)S(1)}, u32[]{:S(2)}) copy-start(f32[4,64,128]{2,1,0:T(8,128)S(1)} %collective-permute-done.2.fl_ref) | copy-start | bytes 393220
  29.0 0.7 copy-start.6
  34.0 7.7 %collective-permute-start.4 = (f32[4,2,64,128]{3,2,1,0:T(8,128)S(1)}, f32[4,2,64,128]{3,2,1,0:T(8,128)S(1)}, u32[]{:S(2)}, u32[]{:S(2)}) collective-permute-start(f32[4,2,64,128]{3,2,1,0:T(8,128)S(1)} %slice_bitcast_fusion), channel_id=1, source_target_pairs={{0,1},{2,3},{4,5},{6,7},{8,9},{10,11},{12,13},{14,15},{16,17},{18,... | collective-permute-start | bytes 786440 | tf_op jit(solution)/shard_map/ppermute | solution.py:19
  41.7 0.7 copy-start.3
  44.7 6.6 %collective-permute-start.5 = (f32[4,64,128]{2,1,0:T(8,128)}, f32[4,64,128]{2,1,0:T(8,128)S(1)}, u32[]{:S(2)}, u32[]{:S(2)}) collective-permute-start(f32[4,64,128]{2,1,0:T(8,128)} %get-tuple-element.25), channel_id=1, source_target_pairs={{0,2},{2,4},{4,6},{6,8},{8,10},{10,12},{12,14},{14,16},{16,18},{18... | collective-permute-start | bytes 393224 | tf_op jit(solution)/shard_map/ppermute | solution.py:19
  49.1 7.4 %collective-permute-start.6 = (f32[4,64,128]{2,1,0:T(8,128)}, f32[4,64,128]{2,1,0:T(8,128)S(1)}, u32[]{:S(2)}, u32[]{:S(2)}) collective-permute-start(f32[4,64,128]{2,1,0:T(8,128)} %get-tuple-element.26), channel_id=1, source_target_pairs={{2,0},{4,2},{6,4},{8,6},{10,8},{12,10},{14,12},{16,14},{18,16},{20... | collective-permute-start | bytes 393224 | tf_op jit(solution)/shard_map/ppermute | solution.py:19
  51.3 5.2 %copy-start.7 = (f32[4,64,128]{2,1,0:T(8,128)}, f32[4,64,128]{2,1,0:T(8,128)S(1)}, u32[]{:S(2)}) copy-start(f32[4,64,128]{2,1,0:T(8,128)S(1)} %collective-permute-done.5.fl_ref) | copy-start | bytes 393220
  56.5 0.7 copy-start.8
  60.4 4.3 %collective-permute-start.7 = (f32[2,64,128]{2,1,0:T(8,128)}, f32[2,64,128]{2,1,0:T(8,128)S(1)}, u32[]{:S(2)}, u32[]{:S(2)}) collective-permute-start(f32[2,64,128]{2,1,0:T(8,128)} %get-tuple-element.28), channel_id=1, source_target_pairs={{0,2},{2,4},{4,6},{6,8},{8,10},{10,12},{12,14},{14,16},{16,18},{18... | collective-permute-start | bytes 196616 | tf_op jit(solution)/shard_map/ppermute | solution.py:19
  62.3 6.7 %collective-permute-start.8 = (f32[2,64,128]{2,1,0:T(8,128)}, f32[2,64,128]{2,1,0:T(8,128)S(1)}, u32[]{:S(2)}, u32[]{:S(2)}) collective-permute-start(f32[2,64,128]{2,1,0:T(8,128)} %get-tuple-element.29), channel_id=1, source_target_pairs={{2,0},{4,2},{6,4},{8,6},{10,8},{12,10},{14,12},{16,14},{18,16},{20... | collective-permute-start | bytes 196616 | tf_op jit(solution)/shard_map/ppermute | solution.py:19
  64.8 4.3 %copy-start.9 = (f32[2,64,128]{2,1,0:T(8,128)}, f32[2,64,128]{2,1,0:T(8,128)S(1)}, u32[]{:S(2)}) copy-start(f32[2,64,128]{2,1,0:T(8,128)S(1)} %collective-permute-done.7.fl_ref) | copy-start | bytes 196612
  69.0 0.6 copy-start.10
  69.7 2.6 %copy-start = (f32[2,4,2,64,128]{4,3,2,1,0:T(8,128)S(1)}, f32[2,4,2,64,128]{4,3,2,1,0:T(8,128)}, u32[]{:S(2)}) copy-start(f32[2,4,2,64,128]{4,3,2,1,0:T(8,128)} %shard_map.95.own_ref) | copy-start | bytes 1572868
  69.7 2.6 %copy-start.1 = (f32[2,4,2,64,128]{4,3,2,1,0:T(8,128)S(1)}, f32[2,4,2,64,128]{4,3,2,1,0:T(8,128)}, u32[]{:S(2)}) copy-start(f32[2,4,2,64,128]{4,3,2,1,0:T(8,128)} %get-tuple-element.27.s_ref) | copy-start | bytes 1572868

commit v6 on v5

--- a/solution.py
+++ b/solution.py
@@ -95,7 +95,7 @@
     left_out[2 * b + 1] = ahead
 
 
-def pair_kernel(sizes, counts, next_count, first, s_ref, k_ref, m_ref, c_ref, fl_ref, fr_ref,
+def pair_kernel(sizes, counts, next_count, first, split, s_ref, k_ref, m_ref, c_ref, fl_ref, fr_ref,
                 s_out, *outs):
     n = s_ref.shape[2]
     width = 2 * len(sizes)
@@ -127,19 +127,23 @@
             s_out[b, 0, i] = pres1[i]
             for c in range(3):
                 s_out[b, 1 + c, i] = vel1[i][c]
+            if split and b == 0:
+                outs[-1][0, i] = pres1[i]
+                for c in range(3):
+                    outs[-1][1 + c, i] = vel1[i][c]
         if b < next_count:
             write_messages(b, messages(pres1, vel1, k_ref, m_ref, h), outs[0], outs[1])
     if first:
-        outs[-1][0] = next_mass
-        outs[-1][1] = next_stiff
-        outs[-1][2] = prev_stiff
+        outs[2 if next_count else 0][0] = next_mass
+        outs[2 if next_count else 0][1] = next_stiff
+        outs[2 if next_count else 0][2] = prev_stiff
 
 
 def planes(count, like):
     return jax.ShapeDtypeStruct((count,) + like.shape[-2:], like.dtype)
 
 
-def advance(state, to_right, to_left, stiffness, inv_mass, consts, sizes, counts, next_count):
+def advance(state, to_right, to_left, stiffness, inv_mass, consts, sizes, counts, next_count, split=False):
     from_left = from_behind(to_right, "space", 1)
     from_right = from_behind(to_left, "space", -1)
     first = consts is None
@@ -150,8 +154,10 @@
         outs += [planes(2 * next_count, state), planes(2 * next_count, state)]
     if first:
         outs.append(planes(3, state))
+    if split:
+        outs.append(jax.ShapeDtypeStruct(state.shape[1:], state.dtype))
     return pl.pallas_call(
-        functools.partial(pair_kernel, tuple(sizes), tuple(counts), next_count, first),
+        functools.partial(pair_kernel, tuple(sizes), tuple(counts), next_count, first, split),
         out_shape=tuple(outs),
     )(state, stiffness, inv_mass, consts, from_left, from_right)
 
@@ -198,6 +204,31 @@
     return out[0]
 
 
+def finish_kernel(g_ref, s_ref, late_ref, both_ref, cp_out, cv_out, rp_out, rv_out):
+    n = s_ref.shape[2]
+
+    def write(end_ref, moved):
+        for i in range(n):
+            for c in range(4):
+                relaxed = s_ref[0, c, i]
+                resid = end_ref[c, i] - relaxed
+                error = resid if moved is None else resid + moved[c, i]
+                if c == 0:
+                    rp_out[0, i] = resid
+                    cp_out[0, i] = relaxed + error
+                else:
+                    rv_out[0, c - 1, i] = resid
+                    cv_out[0, c - 1, i] = relaxed + error
+
+    @pl.when(g_ref[0] == 0)
+    def _():
+        write(s_ref.at[1], None)
+
+    @pl.when(g_ref[0] != 0)
+    def _():
+        write(late_ref.at[0], both_ref.at[1])
+
+
 def on_device(
     guess_pressure, guess_velocity, initial_pressure, initial_velocity, stiffness, inv_mass
 ):
@@ -218,11 +249,14 @@
     )
     for repeat in range(1, rounds):
         count = 2 if repeat + 1 < rounds else 0
-        outs = advance(state, to_right, to_left, stiffness, inv_mass, consts, fine2, (2, 2), count)
+        outs = advance(
+            state, to_right, to_left, stiffness, inv_mass, consts, fine2, (2, 2), count,
+            split=repeat + 1 == rounds,
+        )
         state = outs[0]
         if count:
             to_right, to_left = outs[1], outs[2]
-    relaxed, own_end = state[0], state[1]
+    relaxed = outs[-1]
 
     got = from_behind(relaxed, "tm", 1)
     late, to_right, to_left = pl.pallas_call(
@@ -243,16 +277,22 @@
         if count:
             to_right, to_left = outs[1], outs[2]
 
-    end = jnp.where(group == 0, own_end, late[0])
+    if groups == 2:
+        flat = jax.ShapeDtypeStruct((1,) + stiffness.shape, stiffness.dtype)
+        vflat = jax.ShapeDtypeStruct((1, 3) + stiffness.shape, stiffness.dtype)
+        vmem = pl.BlockSpec(memory_space=pltpu.VMEM)
+        return pl.pallas_call(
+            finish_kernel,
+            out_shape=(flat, vflat, flat, vflat),
+            in_specs=[pl.BlockSpec(memory_space=pltpu.SMEM), vmem, vmem, vmem],
+        )(jnp.reshape(group, (1,)).astype(jnp.int32), state, late, both)
+    end = jnp.where(group == 0, state[1], late[0])
     resid = end - relaxed
-    if groups == 2:
-        error = resid + jnp.where(group == 0, jnp.zeros_like(resid), both[1])
-    else:
-        error, carried = resid, resid
-        for repeat in range(groups - 1):
-            carried = from_behind(carried, "tm", 1)
-            carried = coarse(carried[None], stiffness, inv_mass, consts)
-            error = error + carried
+    error, carried = resid, resid
+    for repeat in range(groups - 1):
+        carried = from_behind(carried, "tm", 1)
+        carried = coarse(carried[None], stiffness, inv_mass, consts)
+        error = error + carried
     corrected = relaxed + error
     return (corrected[0][None], corrected[1:][None], resid[0][None], resid[1:][None])
 

time: 75.9 us -> 74 us (0.975)
  local copies, waits for them, and re-layouts: 6.37 us -> 3.37 us
  Pallas kernels: 17.6 us -> 19.6 us
  other arithmetic: 1.02 us -> 0 us
    pallas_call x0 -> x1, Pallas kernels: none -> 2.11 us  [on_device(): pl.pallas_call(finish_kernel, out_shape=(flat, vflat, flat, vflat), in_sp...]
    slice x2 -> x0, local copies, waits for them, and re-layouts: 1.27 us -> none  [the longest x1 0.63 us: on_device(): corrected[0][None]]
    add x1 -> x0, other arithmetic: 1.02 us -> none  [on_device(): corrected = relaxed + error]
    squeeze x1 -> x0, local copies, waits for them, and re-layouts: 0.97 us -> none  [on_device(): relaxed, own_end = (state[0], state[1])]
    broadcast_in_dim x1 -> x0, local copies, waits for them, and re-layouts: 0.77 us -> none  [on_device(): resid[1:][None]]
    unnamed x22 -> x18, local copies, waits for them, and re-layouts: 3.37 us -> 3.37 us
where the time goes in v6:
time: 74 us; the launch traced here: 73.5 us
  starting transfers between devices  25.4 us (34%)
  waiting for transfers between devices  24.4 us (33%)
  Pallas kernels  19.6 us (26%)
  local copies, waits for them, and re-layouts  3.37 us (5%)
  between operations  0.74 us (1%)
    ppermute x9, starting transfers between devices, from_behind(): return lax.ppermute(x, axis, pairs)  25.4 us
    ppermute x9, waiting for transfers between devices, from_behind(): return lax.ppermute(x, axis, pairs)  24.4 us
    pallas_call x4, Pallas kernels, advance(): pl.pallas_call(functools.partial(pair_kernel, tuple(sizes), tuple(counts)...  13 us
    unnamed x18, local copies, waits for them, and re-layouts  3.37 us
    pallas_call x1, Pallas kernels, on_device(): pl.pallas_call(functools.partial(late_kernel, (fine_size, DT_COARSE)), ou...  2.29 us
    pallas_call x1, Pallas kernels, on_device(): pl.pallas_call(functools.partial(start_kernel, fine_size), out_shape=(sta...  2.25 us
    pallas_call x1, Pallas kernels, on_device(): pl.pallas_call(finish_kernel, out_shape=(flat, vflat, flat, vflat), in_sp...  2.11 us
  transfers between devices with their start and end apart: 9, of which 7 were waited for; matrix products, arithmetic and copies ran while one was open for 0% of the time, Pallas kernels for 0%

profile of v6, /device:TPU:7, one launch (start us, length us, event | category | flops | bytes accessed | tf_op | source)
XLA Modules:
  0.0 73.5 jit_solution(1574293540763442728)
XLA Ops:
  0.6 2.3 %shard_map.93 = (f32[2,4,2,64,128]{4,3,2,1,0:T(8,128)}, f32[5,64,128]{2,1,0:T(8,128)}, f32[6,64,128]{2,1,0:T(8,128)}) custom-call(f32[1,2,64,128]{3,2,1,0:T(8,128)} %gp_ref.1, f32[1,3,2,64,128]{4,3,2,1,0:T(8,128)} %gv_ref.1, f32[2,64,128]{2,1,0:T(8,128)} %ip_ref.1, f32[3,2,64,128]{3,2,1,0:T(8,128)} %iv_ref.1, f32[2,64,128]{2,1,0:T(8,128)} %k_ref.11, ...), custom_call_target="tpu_custom_call" | custom-call | tf_op jit(solution)/shard_map/pallas_call | solution.py:241
  2.9 2.6 %collective-permute-start.1 = (f32[6,64,128]{2,1,0:T(8,128)}, f32[6,64,128]{2,1,0:T(8,128)S(1)}, u32[]{:S(2)}, u32[]{:S(2)}) collective-permute-start(f32[6,64,128]{2,1,0:T(8,128)} %get-tuple-element.21), channel_id=1, source_target_pairs={{2,0},{4,2},{6,4},{8,6},{10,8},{12,10},{14,12},{16,14},{18,16},{20... | collective-permute-start | bytes 589832 | tf_op jit(solution)/shard_map/ppermute | solution.py:19
  5.5 3.9 %collective-permute-start = (f32[5,64,128]{2,1,0:T(8,128)}, f32[5,64,128]{2,1,0:T(8,128)S(1)}, u32[]{:S(2)}, u32[]{:S(2)}) collective-permute-start(f32[5,64,128]{2,1,0:T(8,128)} %get-tuple-element.20), channel_id=1, source_target_pairs={{0,2},{2,4},{4,6},{6,8},{8,10},{10,12},{12,14},{14,16},{16,18},{18... | collective-permute-start | bytes 491528 | tf_op jit(solution)/shard_map/ppermute | solution.py:19
  9.3 2.6 %collective-permute-done.c_ref.fl_ref = f32[5,64,128]{2,1,0:T(8,128)S(1)} collective-permute-done((f32[5,64,128]{2,1,0:T(8,128)}, f32[5,64,128]{2,1,0:T(8,128)S(1)}, u32[]{:S(2)}, u32[]{:S(2)}) %collective-permute-start) | collective-permute-done | bytes 163872 | tf_op jit(solution)/shard_map/ppermute | solution.py:19
  11.9 0.7 copy-done
  12.6 3.8 %shard_map.94 = (f32[2,4,2,64,128]{4,3,2,1,0:T(8,128)}, f32[4,64,128]{2,1,0:T(8,128)}, f32[4,64,128]{2,1,0:T(8,128)}, f32[3,64,128]{2,1,0:T(8,128)}) custom-call(f32[2,4,2,64,128]{4,3,2,1,0:T(8,128)} %get-tuple-element.19.s_ref, f32[2,64,128]{2,1,0:T(8,128)} %k_ref.11, f32[2,64,128]{2,1,0:T(8,128)} %m_ref.11, f32[5,64,128]{2,1,0:T(8,128)} %copy-done, ...), custom_call_target="tpu_custom_call" | custom-call | tf_op jit(solution)/shard_map/pallas_call | solution.py:159
  16.5 5.2 %collective-permute-start.2 = (f32[4,64,128]{2,1,0:T(8,128)}, f32[4,64,128]{2,1,0:T(8,128)S(1)}, u32[]{:S(2)}, u32[]{:S(2)}) collective-permute-start(f32[4,64,128]{2,1,0:T(8,128)} %get-tuple-element.24), channel_id=1, source_target_pairs={{0,2},{2,4},{4,6},{6,8},{8,10},{10,12},{12,14},{14,16},{16,18},{18... | collective-permute-start | bytes 393224 | tf_op jit(solution)/shard_map/ppermute | solution.py:19
  21.6 1.9 %collective-permute-start.3 = (f32[4,64,128]{2,1,0:T(8,128)}, f32[4,64,128]{2,1,0:T(8,128)S(1)}, u32[]{:S(2)}, u32[]{:S(2)}) collective-permute-start(f32[4,64,128]{2,1,0:T(8,128)} %get-tuple-element.25), channel_id=1, source_target_pairs={{2,0},{4,2},{6,4},{8,6},{10,8},{12,10},{14,12},{16,14},{18,16},{20... | collective-permute-start | bytes 393224 | tf_op jit(solution)/shard_map/ppermute | solution.py:19
  23.9 5.2 %collective-permute-done.3.fr_ref = f32[4,64,128]{2,1,0:T(8,128)S(1)} collective-permute-done((f32[4,64,128]{2,1,0:T(8,128)}, f32[4,64,128]{2,1,0:T(8,128)S(1)}, u32[]{:S(2)}, u32[]{:S(2)}) %collective-permute-start.3) | collective-permute-done | bytes 131104 | tf_op jit(solution)/shard_map/ppermute | solution.py:19
  29.0 0.7 copy-done.6
  29.7 3.4 %shard_map.95 = (f32[2,4,2,64,128]{4,3,2,1,0:T(8,128)}, f32[4,2,64,128]{3,2,1,0:T(8,128)}) custom-call(f32[2,4,2,64,128]{4,3,2,1,0:T(8,128)} %get-tuple-element.22.s_ref, f32[2,64,128]{2,1,0:T(8,128)} %k_ref.11, f32[2,64,128]{2,1,0:T(8,128)} %m_ref.11, f32[3,64,128]{2,1,0:T(8,128)} %get-tuple-element.23.c_ref, f32[4,64,128]{2,1,0:T(8,128)} %copy-done.4, ...), custom_call_target="tpu_custom_call" | custom-call | tf_op jit(solution)/shard_map/pallas_call | solution.py:159
  33.0 1.3 %collective-permute-start.4 = (f32[4,2,64,128]{3,2,1,0:T(8,128)}, f32[4,2,64,128]{3,2,1,0:T(8,128)S(1)}, u32[]{:S(2)}, u32[]{:S(2)}) collective-permute-start(f32[4,2,64,128]{3,2,1,0:T(8,128)} %get-tuple-element.27), channel_id=1, source_target_pairs={{0,1},{2,3},{4,5},{6,7},{8,9},{10,11},{12,13},{14,15},{16,17},{18,... | collective-permute-start | bytes 786440 | tf_op jit(solution)/shard_map/ppermute | solution.py:19
  34.3 6.6 %collective-permute-done.4.got_ref = f32[4,2,64,128]{3,2,1,0:T(8,128)S(1)} collective-permute-done((f32[4,2,64,128]{3,2,1,0:T(8,128)}, f32[4,2,64,128]{3,2,1,0:T(8,128)S(1)}, u32[]{:S(2)}, u32[]{:S(2)}) %collective-permute-start.4) | collective-permute-done | bytes 262176 | tf_op jit(solution)/shard_map/ppermute | solution.py:19
  40.9 0.7 copy-done.1
  41.6 2.3 %shard_map.96 = (f32[2,4,2,64,128]{4,3,2,1,0:T(8,128)}, f32[4,64,128]{2,1,0:T(8,128)}, f32[4,64,128]{2,1,0:T(8,128)}) custom-call(f32[4,2,64,128]{3,2,1,0:T(8,128)} %copy-done.1, f32[2,4,2,64,128]{4,3,2,1,0:T(8,128)} %get-tuple-element.26.own_ref.s_ref, f32[2,64,128]{2,1,0:T(8,128)} %k_ref.11, f32[2,64,128]{2,1,0:T(8,128)} %m_ref.11), custom_call_target="tpu_custom_call" | custom-call | tf_op jit(solution)/shard_map/pallas_call | solution.py:262
  43.9 4.4 %collective-permute-start.5 = (f32[4,64,128]{2,1,0:T(8,128)}, f32[4,64,128]{2,1,0:T(8,128)S(1)}, u32[]{:S(2)}, u32[]{:S(2)}) collective-permute-start(f32[4,64,128]{2,1,0:T(8,128)} %get-tuple-element.29), channel_id=1, source_target_pairs={{0,2},{2,4},{4,6},{6,8},{8,10},{10,12},{12,14},{14,16},{16,18},{18... | collective-permute-start | bytes 393224 | tf_op jit(solution)/shard_map/ppermute | solution.py:19
  48.3 1.9 %collective-permute-start.6 = (f32[4,64,128]{2,1,0:T(8,128)}, f32[4,64,128]{2,1,0:T(8,128)S(1)}, u32[]{:S(2)}, u32[]{:S(2)}) collective-permute-start(f32[4,64,128]{2,1,0:T(8,128)} %get-tuple-element.30), channel_id=1, source_target_pairs={{2,0},{4,2},{6,4},{8,6},{10,8},{12,10},{14,12},{16,14},{18,16},{20... | collective-permute-start | bytes 393224 | tf_op jit(solution)/shard_map/ppermute | solution.py:19
  50.6 5.2 %collective-permute-done.6.fr_ref = f32[4,64,128]{2,1,0:T(8,128)S(1)} collective-permute-done((f32[4,64,128]{2,1,0:T(8,128)}, f32[4,64,128]{2,1,0:T(8,128)S(1)}, u32[]{:S(2)}, u32[]{:S(2)}) %collective-permute-start.6) | collective-permute-done | bytes 131104 | tf_op jit(solution)/shard_map/ppermute | solution.py:19
  56.4 3.3 %shard_map.97 = (f32[2,4,2,64,128]{4,3,2,1,0:T(8,128)}, f32[2,64,128]{2,1,0:T(8,128)}, f32[2,64,128]{2,1,0:T(8,128)}) custom-call(f32[2,4,2,64,128]{4,3,2,1,0:T(8,128)} %get-tuple-element.28.s_ref, f32[2,64,128]{2,1,0:T(8,128)} %k_ref.11, f32[2,64,128]{2,1,0:T(8,128)} %m_ref.11, f32[3,64,128]{2,1,0:T(8,128)} %get-tuple-element.23.c_ref, ...), custom_call_target="tpu_custom_call" | custom-call | tf_op jit(solution)/shard_map/pallas_call | solution.py:159
  59.6 1.9 %collective-permute-start.7 = (f32[2,64,128]{2,1,0:T(8,128)}, f32[2,64,128]{2,1,0:T(8,128)S(1)}, u32[]{:S(2)}, u32[]{:S(2)}) collective-permute-start(f32[2,64,128]{2,1,0:T(8,128)} %get-tuple-element.32), channel_id=1, source_target_pairs={{0,2},{2,4},{4,6},{6,8},{8,10},{10,12},{12,14},{14,16},{16,18},{18... | collective-permute-start | bytes 196616 | tf_op jit(solution)/shard_map/ppermute | solution.py:19
  61.6 2.4 %collective-permute-start.8 = (f32[2,64,128]{2,1,0:T(8,128)}, f32[2,64,128]{2,1,0:T(8,128)S(1)}, u32[]{:S(2)}, u32[]{:S(2)}) collective-permute-start(f32[2,64,128]{2,1,0:T(8,128)} %get-tuple-element.33), channel_id=1, source_target_pairs={{2,0},{4,2},{6,4},{8,6},{10,8},{12,10},{14,12},{16,14},{18,16},{20... | collective-permute-start | bytes 196616 | tf_op jit(solution)/shard_map/ppermute | solution.py:19
  64.0 4.3 %collective-permute-done.8.fr_ref = f32[2,64,128]{2,1,0:T(8,128)S(1)} collective-permute-done((f32[2,64,128]{2,1,0:T(8,128)}, f32[2,64,128]{2,1,0:T(8,128)S(1)}, u32[]{:S(2)}, u32[]{:S(2)}) %collective-permute-start.8) | collective-permute-done | bytes 65568 | tf_op jit(solution)/shard_map/ppermute | solution.py:19
  68.9 2.5 %shard_map.98.late_ref = f32[1,4,2,64,128]{4,3,2,1,0:T(8,128)} custom-call(f32[2,4,2,64,128]{4,3,2,1,0:T(8,128)} %get-tuple-element.31.s_ref.both_ref, f32[2,64,128]{2,1,0:T(8,128)} %k_ref.11, f32[2,64,128]{2,1,0:T(8,128)} %m_ref.11, f32[3,64,128]{2,1,0:T(8,128)} %get-tuple-element.23.c_ref, f32[2,64,128]{2,1,0:T(8,128)} %copy-done.7, f32[2,64,128]{2,1,0:T(8,128)} %copy-done.8), custom_call_target="tpu_custom_call" | custom-call | tf_op jit(solution)/shard_map/pallas_call | solution.py:159
  71.4 2.1 %shard_map.99 = (f32[1,2,64,128]{3,2,1,0:T(8,128)}, f32[1,3,2,64,128]{4,3,2,1,0:T(8,128)}, f32[1,2,64,128]{3,2,1,0:T(8,128)}, f32[1,3,2,64,128]{4,3,2,1,0:T(8,128)}) custom-call(s32[1]{0:T(128)} %bitcast.g_ref, f32[2,4,2,64,128]{4,3,2,1,0:T(8,128)} %get-tuple-element.26.own_ref.s_ref, f32[1,4,2,64,128]{4,3,2,1,0:T(8,128)} %shard_map.98.late_ref, ...), custom_call_target="tpu_custom_call" | custom-call | tf_op jit(solution)/shard_map/pallas_call | solution.py:284
  (19 shorter events, 2.0 us)
Async XLA Ops:
  2.9 9.0 %collective-permute-start.1 = (f32[6,64,128]{2,1,0:T(8,128)}, f32[6,64,128]{2,1,0:T(8,128)S(1)}, u32[]{:S(2)}, u32[]{:S(2)}) collective-permute-start(f32[6,64,128]{2,1,0:T(8,128)} %get-tuple-element.21), channel_id=1, source_target_pairs={{2,0},{4,2},{6,4},{8,6},{10,8},{12,10},{14,12},{16,14},{18,16},{20... | collective-permute-start | bytes 589832 | tf_op jit(solution)/shard_map/ppermute | solution.py:19
  5.5 6.4 %collective-permute-start = (f32[5,64,128]{2,1,0:T(8,128)}, f32[5,64,128]{2,1,0:T(8,128)S(1)}, u32[]{:S(2)}, u32[]{:S(2)}) collective-permute-start(f32[5,64,128]{2,1,0:T(8,128)} %get-tuple-element.20), channel_id=1, source_target_pairs={{0,2},{2,4},{4,6},{6,8},{8,10},{10,12},{12,14},{14,16},{16,18},{18... | collective-permute-start | bytes 491528 | tf_op jit(solution)/shard_map/ppermute | solution.py:19
  11.9 0.7 copy-start
  11.9 0.7 copy-start.2
  16.5 7.4 %collective-permute-start.2 = (f32[4,64,128]{2,1,0:T(8,128)}, f32[4,64,128]{2,1,0:T(8,128)S(1)}, u32[]{:S(2)}, u32[]{:S(2)}) collective-permute-start(f32[4,64,128]{2,1,0:T(8,128)} %get-tuple-element.24), channel_id=1, source_target_pairs={{0,2},{2,4},{4,6},{6,8},{8,10},{10,12},{12,14},{14,16},{16,18},{18... | collective-permute-start | bytes 393224 | tf_op jit(solution)/shard_map/ppermute | solution.py:19
  21.6 7.4 %collective-permute-start.3 = (f32[4,64,128]{2,1,0:T(8,128)}, f32[4,64,128]{2,1,0:T(8,128)S(1)}, u32[]{:S(2)}, u32[]{:S(2)}) collective-permute-start(f32[4,64,128]{2,1,0:T(8,128)} %get-tuple-element.25), channel_id=1, source_target_pairs={{2,0},{4,2},{6,4},{8,6},{10,8},{12,10},{14,12},{16,14},{18,16},{20... | collective-permute-start | bytes 393224 | tf_op jit(solution)/shard_map/ppermute | solution.py:19
  23.9 5.2 %copy-start.4 = (f32[4,64,128]{2,1,0:T(8,128)}, f32[4,64,128]{2,1,0:T(8,128)S(1)}, u32[]{:S(2)}) copy-start(f32[4,64,128]{2,1,0:T(8,128)S(1)} %collective-permute-done.2.fl_ref) | copy-start | bytes 393220
  29.0 0.7 copy-start.6
  33.0 7.9 %collective-permute-start.4 = (f32[4,2,64,128]{3,2,1,0:T(8,128)}, f32[4,2,64,128]{3,2,1,0:T(8,128)S(1)}, u32[]{:S(2)}, u32[]{:S(2)}) collective-permute-start(f32[4,2,64,128]{3,2,1,0:T(8,128)} %get-tuple-element.27), channel_id=1, source_target_pairs={{0,1},{2,3},{4,5},{6,7},{8,9},{10,11},{12,13},{14,15},{16,17},{18,... | collective-permute-start | bytes 786440 | tf_op jit(solution)/shard_map/ppermute | solution.py:19
  40.9 0.7 copy-start.1
  43.9 6.6 %collective-permute-start.5 = (f32[4,64,128]{2,1,0:T(8,128)}, f32[4,64,128]{2,1,0:T(8,128)S(1)}, u32[]{:S(2)}, u32[]{:S(2)}) collective-permute-start(f32[4,64,128]{2,1,0:T(8,128)} %get-tuple-element.29), channel_id=1, source_target_pairs={{0,2},{2,4},{4,6},{6,8},{8,10},{10,12},{12,14},{14,16},{16,18},{18... | collective-permute-start | bytes 393224 | tf_op jit(solution)/shard_map/ppermute | solution.py:19
  48.3 7.4 %collective-permute-start.6 = (f32[4,64,128]{2,1,0:T(8,128)}, f32[4,64,128]{2,1,0:T(8,128)S(1)}, u32[]{:S(2)}, u32[]{:S(2)}) collective-permute-start(f32[4,64,128]{2,1,0:T(8,128)} %get-tuple-element.30), channel_id=1, source_target_pairs={{2,0},{4,2},{6,4},{8,6},{10,8},{12,10},{14,12},{16,14},{18,16},{20... | collective-permute-start | bytes 393224 | tf_op jit(solution)/shard_map/ppermute | solution.py:19
  50.6 5.2 %copy-start.3 = (f32[4,64,128]{2,1,0:T(8,128)}, f32[4,64,128]{2,1,0:T(8,128)S(1)}, u32[]{:S(2)}) copy-start(f32[4,64,128]{2,1,0:T(8,128)S(1)} %collective-permute-done.5.fl_ref) | copy-start | bytes 393220
  55.7 0.7 copy-start.5
  59.6 4.3 %collective-permute-start.7 = (f32[2,64,128]{2,1,0:T(8,128)}, f32[2,64,128]{2,1,0:T(8,128)S(1)}, u32[]{:S(2)}, u32[]{:S(2)}) collective-permute-start(f32[2,64,128]{2,1,0:T(8,128)} %get-tuple-element.32), channel_id=1, source_target_pairs={{0,2},{2,4},{4,6},{6,8},{8,10},{10,12},{12,14},{14,16},{16,18},{18... | collective-permute-start | bytes 196616 | tf_op jit(solution)/shard_map/ppermute | solution.py:19
  61.6 6.7 %collective-permute-start.8 = (f32[2,64,128]{2,1,0:T(8,128)}, f32[2,64,128]{2,1,0:T(8,128)S(1)}, u32[]{:S(2)}, u32[]{:S(2)}) collective-permute-start(f32[2,64,128]{2,1,0:T(8,128)} %get-tuple-element.33), channel_id=1, source_target_pairs={{2,0},{4,2},{6,4},{8,6},{10,8},{12,10},{14,12},{16,14},{18,16},{20... | collective-permute-start | bytes 196616 | tf_op jit(solution)/shard_map/ppermute | solution.py:19
  64.0 4.3 %copy-start.7 = (f32[2,64,128]{2,1,0:T(8,128)}, f32[2,64,128]{2,1,0:T(8,128)S(1)}, u32[]{:S(2)}) copy-start(f32[2,64,128]{2,1,0:T(8,128)S(1)} %collective-permute-done.7.fl_ref) | copy-start | bytes 196612
  68.3 0.6 copy-start.8

commit v7 on v5

v7 whole, which is shorter than its diff:
```python
import functools

import jax
import jax.numpy as jnp
from jax import lax
from jax.experimental import pallas as pl
from jax.experimental.pallas import tpu as pltpu
from jax.sharding import PartitionSpec as P

STEPS = 4


DT_COARSE = 0.4


def from_behind(x, axis, by):
    size = lax.axis_size(axis)
    pairs = [(i, i + by) for i in range(size) if 0 <= i + by < size]
    return lax.ppermute(x, axis, pairs)


def roll(x, shift, axis):
    return pltpu.roll(x, shift % x.shape[axis], axis)


def nsum(values, offset, axis):
    return values + roll(values, offset, axis)


def forces(pressure, lower):
    combined = pressure + lower
    force_x = 0.25 * (nsum(nsum(lower, 1, 1), 1, 0) - nsum(nsum(pressure, 1, 1), 1, 0))
    across_z = nsum(combined, 1, 1)
    force_y = 0.25 * (roll(across_z, 1, 0) - across_z)
    across_y = nsum(combined, 1, 0)
    force_z = 0.25 * (roll(across_y, 1, 1) - across_y)
    return force_x, force_y, force_z


def divergence(v, u):
    diff_x = nsum(nsum(u[0] - v[0], -1, 1), -1, 0)
    sum_y = nsum(v[1] + u[1], -1, 1)
    diff_y = roll(sum_y, -1, 0) - sum_y
    sum_z = nsum(v[2] + u[2], -1, 0)
    diff_z = roll(sum_z, -1, 1) - sum_z
    return 0.25 * (diff_x + diff_y + diff_z)


def upper_part(u):
    diff_x = nsum(nsum(u[0], -1, 1), -1, 0)
    sum_y = nsum(u[1], -1, 1)
    diff_y = roll(sum_y, -1, 0) - sum_y
    sum_z = nsum(u[2], -1, 0)
    diff_z = roll(sum_z, -1, 1) - sum_z
    return diff_x + diff_y + diff_z


def lower_part(v):
    diff_x = nsum(nsum(-v[0], -1, 1), -1, 0)
    sum_y = nsum(v[1], -1, 1)
    diff_y = roll(sum_y, -1, 0) - sum_y
    sum_z = nsum(v[2], -1, 0)
    diff_z = roll(sum_z, -1, 1) - sum_z
    return diff_x + diff_y + diff_z


def outgoing(pressure_first, velocity_first, mass_first, step_size):
    f = forces(pressure_first, jnp.zeros_like(pressure_first))
    hm = step_size * mass_first
    return upper_part([velocity_first[c] + hm * f[c] for c in range(3)])


def messages(pres, vel, k_ref, m_ref, step_size):
    n = len(pres)
    last_node = [vel[n - 1][c] + step_size * m_ref[n - 1] * f
                 for c, f in enumerate(forces(pres[n - 1], pres[n - 2]))]
    behind = pres[n - 1] - step_size * k_ref[n - 1] * (0.25 * lower_part(last_node))
    f0 = forces(pres[0], jnp.zeros_like(pres[0]))
    partial = [vel[0][c] + step_size * m_ref[0] * f0[c] for c in range(3)]
    second = [vel[1][c] + step_size * m_ref[1] * f for c, f in enumerate(forces(pres[1], pres[0]))]
    ahead = pres[0] - step_size * k_ref[0] * (0.25 * (lower_part(partial) + upper_part(second)))
    return (pres[n - 1], behind), (upper_part(partial), ahead)


def read_slot(source, refs, n):
    kind = source[0]
    if kind == "packed":
        ref, b = refs[source[1]], source[2]
        get = lambda c, i: ref[b, c, i]
    elif kind == "flat":
        ref = refs[source[1]]
        get = lambda c, i: ref[c, i]
    elif kind == "diff":
        ref, b, other = refs[source[1]], source[2], refs[source[3]]
        get = lambda c, i: ref[b, c, i] - other[c, i]
    else:
        pref, vref, lead = refs[source[1]], refs[source[2]], source[3]
        if lead:
            get = lambda c, i: pref[0, i] if c == 0 else vref[0, c - 1, i]
        else:
            get = lambda c, i: pref[i] if c == 0 else vref[c - 1, i]
    return [get(0, i) for i in range(n)], [[get(1 + c, i) for c in range(3)] for i in range(n)]


def write_messages(b, msgs, right_out, left_out):
    (p_last, behind), (share, ahead) = msgs
    right_out[2 * b] = p_last
    right_out[2 * b + 1] = behind
    left_out[2 * b] = share
    left_out[2 * b + 1] = ahead


def write_outputs(g_ref, st_ref, moved_ref, late, n, outs):
    cp_out, cv_out, rp_out, rv_out = outs

    def write(end_of, moved_of):
        for i in range(n):
            for c in range(4):
                relaxed = st_ref[0, c, i]
                resid = end_of(c, i) - relaxed
                error = resid if moved_of is None else resid + moved_of(c, i)
                if c == 0:
                    rp_out[0, i] = resid
                    cp_out[0, i] = relaxed + error
                else:
                    rv_out[0, c - 1, i] = resid
                    cv_out[0, c - 1, i] = relaxed + error

    @pl.when(g_ref[0] == 0)
    def _():
        write(lambda c, i: st_ref[1, c, i], None)

    @pl.when(g_ref[0] != 0)
    def _():
        write(lambda c, i: late[c][i], lambda c, i: moved_ref[1, c, i])


def pair_kernel(sizes, counts, sources, n_states, next_count, first, split, finish, *refs):
    states = refs[:n_states]
    k_ref, m_ref, c_ref, fl_ref, fr_ref = refs[n_states : n_states + 5]
    rest = refs[n_states + 5 :]
    if finish:
        g_ref, st_ref, moved_ref = rest[:3]
        outs = rest[3:]
    else:
        s_out = rest[0]
        outs = rest[1:]
    n = k_ref.shape[0]
    width = 2 * len(sizes)
    if first:
        next_mass, next_stiff, prev_stiff = fr_ref[width], fr_ref[width + 1], fl_ref[width]
    else:
        next_mass, next_stiff, prev_stiff = c_ref[0], c_ref[1], c_ref[2]
    zero = jnp.zeros_like(next_mass)
    for b, (h, count) in enumerate(zip(sizes, counts)):
        pres, vel = read_slot(sources[b], states, n)
        lower = [fl_ref[2 * b]] + pres[:-1]
        vel1 = [[vel[i][c] + h * m_ref[i] * f for c, f in enumerate(forces(pres[i], lower[i]))]
                for i in range(n)]
        pres1 = [pres[i] - h * k_ref[i] * divergence(vel1[i], vel1[i + 1]) for i in range(n - 1)]
        below = [h * next_mass * f for f in forces(zero, pres[n - 1])]
        upper1 = fr_ref[2 * b] + upper_part(below)
        pres1.append(pres[n - 1] - h * k_ref[n - 1] * (0.25 * (lower_part(vel1[n - 1]) + upper1)))
        if count == 2:
            prev1 = fl_ref[2 * b + 1] - h * prev_stiff * (0.25 * upper_part(vel1[0]))
            next1 = fr_ref[2 * b + 1] - h * next_stiff * (0.25 * lower_part(below))
            lower = [prev1] + pres1[:-1]
            vel2 = [[vel1[i][c] + h * m_ref[i] * f for c, f in enumerate(forces(pres1[i], lower[i]))]
                    for i in range(n)]
            pres2 = [pres1[i] - h * k_ref[i] * divergence(vel2[i], vel2[i + 1]) for i in range(n - 1)]
            upper2 = upper1 + upper_part([h * next_mass * f for f in forces(next1, pres1[n - 1])])
            pres2.append(pres1[n - 1] - h * k_ref[n - 1] * (0.25 * (lower_part(vel2[n - 1]) + upper2)))
            pres1, vel1 = pres2, vel2
        if finish:
            late = [pres1] + [[vel1[i][c] for i in range(n)] for c in range(3)]
            write_outputs(g_ref, st_ref, moved_ref, late, n, outs)
            continue
        for i in range(n):
            s_out[b, 0, i] = pres1[i]
            for c in range(3):
                s_out[b, 1 + c, i] = vel1[i][c]
            if split and b == 0:
                outs[-1][0, i] = pres1[i]
                for c in range(3):
                    outs[-1][1 + c, i] = vel1[i][c]
        if b < next_count:
            write_messages(b, messages(pres1, vel1, k_ref, m_ref, h), outs[0], outs[1])
    if first:
        outs[2 if next_count else 0][0] = next_mass
        outs[2 if next_count else 0][1] = next_stiff
        outs[2 if next_count else 0][2] = prev_stiff


def planes(count, like):
    return jax.ShapeDtypeStruct((count,) + like.shape[-2:], like.dtype)


def advance(states, sources, to_right, to_left, stiffness, inv_mass, consts, sizes, counts,
            next_count, split=False, finish=None):
    from_left = from_behind(to_right, "space", 1)
    from_right = from_behind(to_left, "space", -1)
    first = consts is None
    if first:
        consts = from_left
    n = stiffness.shape[0]
    args = list(states) + [stiffness, inv_mass, consts, from_left, from_right]
    vmem = pl.BlockSpec(memory_space=pltpu.VMEM)
    specs = [vmem] * len(args)
    if finish is not None:
        flat = jax.ShapeDtypeStruct((1,) + stiffness.shape, stiffness.dtype)
        vflat = jax.ShapeDtypeStruct((1, 3) + stiffness.shape, stiffness.dtype)
        outs = [flat, vflat, flat, vflat]
        args += list(finish)
        specs += [pl.BlockSpec(memory_space=pltpu.SMEM), vmem, vmem]
    else:
        outs = [jax.ShapeDtypeStruct((len(sizes), 4) + stiffness.shape, stiffness.dtype)]
        if next_count:
            outs += [planes(2 * next_count, stiffness), planes(2 * next_count, stiffness)]
        if first:
            outs.append(planes(3, stiffness))
        if split:
            outs.append(jax.ShapeDtypeStruct((4,) + stiffness.shape, stiffness.dtype))
    kernel = functools.partial(
        pair_kernel, tuple(sizes), tuple(counts), tuple(sources), len(states), next_count, first,
        split, finish is not None,
    )
    return pl.pallas_call(kernel, out_shape=tuple(outs), in_specs=specs)(*args)


def messages_kernel(sizes, sources, n_states, extras, *refs):
    states = refs[:n_states]
    k_ref, m_ref, right_out, left_out = refs[n_states:]
    n = k_ref.shape[0]
    for b, h in enumerate(sizes):
        pres, vel = read_slot(sources[b], states, n)
        write_messages(b, messages(pres, vel, k_ref, m_ref, h), right_out, left_out)
    if extras:
        width = 2 * len(sizes)
        right_out[width] = k_ref[n - 1]
        left_out[width] = m_ref[0]
        left_out[width + 1] = k_ref[0]


def first_messages(states, sources, stiffness, inv_mass, sizes, extras=False):
    width = 2 * len(sizes)
    kernel = functools.partial(messages_kernel, tuple(sizes), tuple(sources), len(states), extras)
    return pl.pallas_call(
        kernel,
        out_shape=(planes(width + (1 if extras else 0), stiffness), planes(width + (2 if extras else 0), stiffness)),
    )(*states, stiffness, inv_mass)


def coarse(carried, stiffness, inv_mass, consts):
    sources = (("flat", 0),)
    to_right, to_left = first_messages((carried,), sources, stiffness, inv_mass, (DT_COARSE,))
    (out,) = advance((carried,), sources, to_right, to_left, stiffness, inv_mass, consts,
                     (DT_COARSE,), (1,), 0)
    return out[0]


def on_device(
    guess_pressure, guess_velocity, initial_pressure, initial_velocity, stiffness, inv_mass
):
    fine_size = DT_COARSE / STEPS
    groups = lax.axis_size("tm")
    group = lax.axis_index("tm")
    assert stiffness.shape[0] >= 2 and STEPS % 2 == 0
    rounds = STEPS // 2
    fine2 = (fine_size, fine_size)

    inputs = (guess_pressure, guess_velocity, initial_pressure, initial_velocity)
    sources = (("input", 0, 1, True), ("input", 2, 3, False))
    to_right, to_left = first_messages(inputs, sources, stiffness, inv_mass, fine2, extras=True)
    state, to_right, to_left, consts = advance(
        inputs, sources, to_right, to_left, stiffness, inv_mass, None, fine2, (2, 2), 2,
    )
    packed = (("packed", 0, 0), ("packed", 0, 1))
    for repeat in range(1, rounds):
        count = 2 if repeat + 1 < rounds else 0
        outs = advance(
            (state,), packed, to_right, to_left, stiffness, inv_mass, consts, fine2, (2, 2), count,
            split=repeat + 1 == rounds,
        )
        state = outs[0]
        if count:
            to_right, to_left = outs[1], outs[2]
    relaxed = outs[-1]

    got = from_behind(relaxed, "tm", 1)
    late_states = (got, state)
    late_sources = (("flat", 0), ("diff", 1, 1, 0))
    to_right, to_left = first_messages(
        late_states, late_sources, stiffness, inv_mass, (fine_size, DT_COARSE)
    )
    flag = jnp.reshape(group, (1,)).astype(jnp.int32)
    both = None
    late = None
    for repeat in range(rounds):
        count = 1 if repeat + 1 < rounds else 0
        if repeat == 0:
            sizes, counts, states, srcs = (fine_size, DT_COARSE), (2, 1), late_states, late_sources
        else:
            sizes, counts, states, srcs = (fine_size,), (2,), (late,), (("packed", 0, 0),)
        finish = (flag, state, both) if (groups == 2 and repeat + 1 == rounds) else None
        outs = advance(states, srcs, to_right, to_left, stiffness, inv_mass, consts, sizes, counts,
                       count, finish=finish)
        if finish is not None:
            return outs
        late = outs[0]
        if repeat == 0:
            both = late
        if count:
            to_right, to_left = outs[1], outs[2]

    end = jnp.where(group == 0, state[1], late[0])
    resid = end - relaxed
    error, carried = resid, resid
    for repeat in range(groups - 1):
        carried = from_behind(carried, "tm", 1)
        carried = coarse(carried, stiffness, inv_mass, consts)
        error = error + carried
    corrected = relaxed + error
    return (corrected[0][None], corrected[1:][None], resid[0][None], resid[1:][None])


def solution(mesh):
    placed = (
        P("tm", "space", None, None),
        P("tm", None, "space", None, None),
        P("space", None, None),
        P(None, "space", None, None),
        P("space", None, None),
        P("space", None, None),
    )
    return jax.shard_map(
        on_device,
        mesh=mesh,
        in_specs=placed,
        out_specs=(
            P("tm", "space", None, None),
            P("tm", None, "space", None, None),
            P("tm", "space", None, None),
            P("tm", None, "space", None, None),
        ),
        check_vma=False,
    )
```

time: 75.9 us -> 73 us (0.962)
  local copies, waits for them, and re-layouts: 6.37 us -> 3.98 us
  other arithmetic: 1.02 us -> 0 us
    slice x2 -> x0, local copies, waits for them, and re-layouts: 1.27 us -> none  [the longest x1 0.63 us: on_device(): corrected[0][None]]
    add x1 -> x0, other arithmetic: 1.02 us -> none  [on_device(): corrected = relaxed + error]
    squeeze x1 -> x0, local copies, waits for them, and re-layouts: 0.97 us -> none  [on_device(): relaxed, own_end = (state[0], state[1])]
    broadcast_in_dim x1 -> x0, local copies, waits for them, and re-layouts: 0.77 us -> none  [on_device(): resid[1:][None]]
    unnamed x22 -> x18, local copies, waits for them, and re-layouts: 3.37 us -> 3.98 us
where the time goes in v7:
time: 73 us; the launch traced here: 72.6 us
  starting transfers between devices  25.4 us (35%)
  waiting for transfers between devices  24.4 us (33%)
  Pallas kernels  18 us (25%)
  local copies, waits for them, and re-layouts  3.98 us (5%)
  between operations  0.74 us (1%)
    ppermute x9, starting transfers between devices, from_behind(): return lax.ppermute(x, axis, pairs)  25.4 us
    ppermute x9, waiting for transfers between devices, from_behind(): return lax.ppermute(x, axis, pairs)  24.4 us
    pallas_call x4, Pallas kernels, advance(): return pl.pallas_call(kernel, out_shape=tuple(outs), in_specs=specs)(*args)  13.6 us
    pallas_call x2, Pallas kernels, first_messages(): pl.pallas_call(kernel, out_shape=(planes(width + (1 if extras else 0), st...  4.43 us
    unnamed x18, local copies, waits for them, and re-layouts  3.98 us
  transfers between devices with their start and end apart: 9, of which 7 were waited for; matrix products, arithmetic and copies ran while one was open for 0% of the time, Pallas kernels for 0%

profile of v7, /device:TPU:7, one launch (start us, length us, event | category | flops | bytes accessed | tf_op | source)
XLA Modules:
  0.0 72.6 jit_solution(9460404817023807467)
XLA Ops:
  0.6 2.2 %shard_map.93 = (f32[5,64,128]{2,1,0:T(8,128)}, f32[6,64,128]{2,1,0:T(8,128)}) custom-call(f32[1,2,64,128]{3,2,1,0:T(8,128)} %refs_0_.3, f32[1,3,2,64,128]{4,3,2,1,0:T(8,128)} %refs_1_.5, f32[2,64,128]{2,1,0:T(8,128)} %refs_2_.7, f32[3,2,64,128]{3,2,1,0:T(8,128)} %refs_3_.5, f32[2,64,128]{2,1,0:T(8,128)} %refs_1_.7, f32[2,64,128]{2,1,0:T(8,128)} %refs_2_.11), custom_call_target="tpu_custom_call" | custom-call | tf_op jit(solution)/shard_map/pallas_call | solution.py:247
  2.9 2.6 %collective-permute-start.1 = (f32[6,64,128]{2,1,0:T(8,128)}, f32[6,64,128]{2,1,0:T(8,128)S(1)}, u32[]{:S(2)}, u32[]{:S(2)}) collective-permute-start(f32[6,64,128]{2,1,0:T(8,128)} %get-tuple-element.18), channel_id=1, source_target_pairs={{2,0},{4,2},{6,4},{8,6},{10,8},{12,10},{14,12},{16,14},{18,16},{20... | collective-permute-start | bytes 589832 | tf_op jit(solution)/shard_map/ppermute | solution.py:19
  5.4 3.9 %collective-permute-start = (f32[5,64,128]{2,1,0:T(8,128)}, f32[5,64,128]{2,1,0:T(8,128)S(1)}, u32[]{:S(2)}, u32[]{:S(2)}) collective-permute-start(f32[5,64,128]{2,1,0:T(8,128)} %get-tuple-element.17), channel_id=1, source_target_pairs={{0,2},{2,4},{4,6},{6,8},{8,10},{10,12},{12,14},{14,16},{16,18},{18... | collective-permute-start | bytes 491528 | tf_op jit(solution)/shard_map/ppermute | solution.py:19
  9.3 2.6 %collective-permute-done.refs_6_.refs_7_ = f32[5,64,128]{2,1,0:T(8,128)S(1)} collective-permute-done((f32[5,64,128]{2,1,0:T(8,128)}, f32[5,64,128]{2,1,0:T(8,128)S(1)}, u32[]{:S(2)}, u32[]{:S(2)}) %collective-permute-start) | collective-permute-done | bytes 163872 | tf_op jit(solution)/shard_map/ppermute | solution.py:19
  11.9 0.7 copy-done.1
  12.5 0.7 copy-done.2
  13.2 3.9 %shard_map.94 = (f32[2,4,2,64,128]{4,3,2,1,0:T(8,128)}, f32[4,64,128]{2,1,0:T(8,128)}, f32[4,64,128]{2,1,0:T(8,128)}, f32[3,64,128]{2,1,0:T(8,128)}) custom-call(f32[1,2,64,128]{3,2,1,0:T(8,128)} %refs_0_.3, f32[1,3,2,64,128]{4,3,2,1,0:T(8,128)} %refs_1_.5, f32[2,64,128]{2,1,0:T(8,128)} %refs_2_.7, f32[3,2,64,128]{3,2,1,0:T(8,128)} %refs_3_.5, ...), custom_call_target="tpu_custom_call" | custom-call | tf_op jit(solution)/shard_map/pallas_call | solution.py:227
  17.1 5.2 %collective-permute-start.2 = (f32[4,64,128]{2,1,0:T(8,128)}, f32[4,64,128]{2,1,0:T(8,128)S(1)}, u32[]{:S(2)}, u32[]{:S(2)}) collective-permute-start(f32[4,64,128]{2,1,0:T(8,128)} %get-tuple-element.21), channel_id=1, source_target_pairs={{0,2},{2,4},{4,6},{6,8},{8,10},{10,12},{12,14},{14,16},{16,18},{18... | collective-permute-start | bytes 393224 | tf_op jit(solution)/shard_map/ppermute | solution.py:19
  22.3 1.9 %collective-permute-start.3 = (f32[4,64,128]{2,1,0:T(8,128)}, f32[4,64,128]{2,1,0:T(8,128)S(1)}, u32[]{:S(2)}, u32[]{:S(2)}) collective-permute-start(f32[4,64,128]{2,1,0:T(8,128)} %get-tuple-element.22), channel_id=1, source_target_pairs={{2,0},{4,2},{6,4},{8,6},{10,8},{12,10},{14,12},{16,14},{18,16},{20... | collective-permute-start | bytes 393224 | tf_op jit(solution)/shard_map/ppermute | solution.py:19
  24.5 5.2 %collective-permute-done.3.refs_5_ = f32[4,64,128]{2,1,0:T(8,128)S(1)} collective-permute-done((f32[4,64,128]{2,1,0:T(8,128)}, f32[4,64,128]{2,1,0:T(8,128)S(1)}, u32[]{:S(2)}, u32[]{:S(2)}) %collective-permute-start.3) | collective-permute-done | bytes 131104 | tf_op jit(solution)/shard_map/ppermute | solution.py:19
  30.3 3.4 %shard_map.95 = (f32[2,4,2,64,128]{4,3,2,1,0:T(8,128)}, f32[4,2,64,128]{3,2,1,0:T(8,128)}) custom-call(f32[2,4,2,64,128]{4,3,2,1,0:T(8,128)} %get-tuple-element.19.refs_0_, f32[2,64,128]{2,1,0:T(8,128)} %refs_1_.7, f32[2,64,128]{2,1,0:T(8,128)} %refs_2_.11, f32[3,64,128]{2,1,0:T(8,128)} %get-tuple-element.20.refs_3_.refs_4_, f32[4,64,128]{2,1,0:T(8,128)} %copy-done.5, ...), custom_call_target="tpu_custom_call" | custom-call | tf_op jit(solution)/shard_map/pallas_call | solution.py:227
  33.7 1.3 %collective-permute-start.4 = (f32[4,2,64,128]{3,2,1,0:T(8,128)}, f32[4,2,64,128]{3,2,1,0:T(8,128)S(1)}, u32[]{:S(2)}, u32[]{:S(2)}) collective-permute-start(f32[4,2,64,128]{3,2,1,0:T(8,128)} %get-tuple-element.23), channel_id=1, source_target_pairs={{0,1},{2,3},{4,5},{6,7},{8,9},{10,11},{12,13},{14,15},{16,17},{18,... | collective-permute-start | bytes 786440 | tf_op jit(solution)/shard_map/ppermute | solution.py:19
  35.0 6.6 %collective-permute-done.4.refs_0_ = f32[4,2,64,128]{3,2,1,0:T(8,128)S(1)} collective-permute-done((f32[4,2,64,128]{3,2,1,0:T(8,128)}, f32[4,2,64,128]{3,2,1,0:T(8,128)S(1)}, u32[]{:S(2)}, u32[]{:S(2)}) %collective-permute-start.4) | collective-permute-done | bytes 262176 | tf_op jit(solution)/shard_map/ppermute | solution.py:19
  41.6 0.7 copy-done
  42.3 2.2 %shard_map.96 = (f32[4,64,128]{2,1,0:T(8,128)}, f32[4,64,128]{2,1,0:T(8,128)}) custom-call(f32[4,2,64,128]{3,2,1,0:T(8,128)} %copy-done, f32[2,4,2,64,128]{4,3,2,1,0:T(8,128)} %get-tuple-element.24.refs_1_.refs_7_, f32[2,64,128]{2,1,0:T(8,128)} %refs_1_.7, f32[2,64,128]{2,1,0:T(8,128)} %refs_2_.11), custom_call_target="tpu_custom_call" | custom-call | tf_op jit(solution)/shard_map/pallas_call | solution.py:247
  44.5 4.4 %collective-permute-start.5 = (f32[4,64,128]{2,1,0:T(8,128)}, f32[4,64,128]{2,1,0:T(8,128)S(1)}, u32[]{:S(2)}, u32[]{:S(2)}) collective-permute-start(f32[4,64,128]{2,1,0:T(8,128)} %get-tuple-element.25), channel_id=1, source_target_pairs={{0,2},{2,4},{4,6},{6,8},{8,10},{10,12},{12,14},{14,16},{16,18},{18... | collective-permute-start | bytes 393224 | tf_op jit(solution)/shard_map/ppermute | solution.py:19
  48.9 1.9 %collective-permute-start.6 = (f32[4,64,128]{2,1,0:T(8,128)}, f32[4,64,128]{2,1,0:T(8,128)S(1)}, u32[]{:S(2)}, u32[]{:S(2)}) collective-permute-start(f32[4,64,128]{2,1,0:T(8,128)} %get-tuple-element.26), channel_id=1, source_target_pairs={{2,0},{4,2},{6,4},{8,6},{10,8},{12,10},{14,12},{16,14},{18,16},{20... | collective-permute-start | bytes 393224 | tf_op jit(solution)/shard_map/ppermute | solution.py:19
  51.1 5.2 %collective-permute-done.6.refs_6_ = f32[4,64,128]{2,1,0:T(8,128)S(1)} collective-permute-done((f32[4,64,128]{2,1,0:T(8,128)}, f32[4,64,128]{2,1,0:T(8,128)S(1)}, u32[]{:S(2)}, u32[]{:S(2)}) %collective-permute-start.6) | collective-permute-done | bytes 131104 | tf_op jit(solution)/shard_map/ppermute | solution.py:19
  56.3 0.7 copy-done.4
  57.0 3.3 %shard_map.97 = (f32[2,4,2,64,128]{4,3,2,1,0:T(8,128)}, f32[2,64,128]{2,1,0:T(8,128)}, f32[2,64,128]{2,1,0:T(8,128)}) custom-call(f32[4,2,64,128]{3,2,1,0:T(8,128)} %copy-done, f32[2,4,2,64,128]{4,3,2,1,0:T(8,128)} %get-tuple-element.24.refs_1_.refs_7_, f32[2,64,128]{2,1,0:T(8,128)} %refs_1_.7, f32[2,64,128]{2,1,0:T(8,128)} %refs_2_.11, ...), custom_call_target="tpu_custom_call" | custom-call | tf_op jit(solution)/shard_map/pallas_call | solution.py:227
  60.3 1.9 %collective-permute-start.7 = (f32[2,64,128]{2,1,0:T(8,128)}, f32[2,64,128]{2,1,0:T(8,128)S(1)}, u32[]{:S(2)}, u32[]{:S(2)}) collective-permute-start(f32[2,64,128]{2,1,0:T(8,128)} %get-tuple-element.28), channel_id=1, source_target_pairs={{0,2},{2,4},{4,6},{6,8},{8,10},{10,12},{12,14},{14,16},{16,18},{18... | collective-permute-start | bytes 196616 | tf_op jit(solution)/shard_map/ppermute | solution.py:19
  62.2 2.4 %collective-permute-start.8 = (f32[2,64,128]{2,1,0:T(8,128)}, f32[2,64,128]{2,1,0:T(8,128)S(1)}, u32[]{:S(2)}, u32[]{:S(2)}) collective-permute-start(f32[2,64,128]{2,1,0:T(8,128)} %get-tuple-element.29), channel_id=1, source_target_pairs={{2,0},{4,2},{6,4},{8,6},{10,8},{12,10},{14,12},{16,14},{18,16},{20... | collective-permute-start | bytes 196616 | tf_op jit(solution)/shard_map/ppermute | solution.py:19
  64.6 4.3 %collective-permute-done.8.refs_5_ = f32[2,64,128]{2,1,0:T(8,128)S(1)} collective-permute-done((f32[2,64,128]{2,1,0:T(8,128)}, f32[2,64,128]{2,1,0:T(8,128)S(1)}, u32[]{:S(2)}, u32[]{:S(2)}) %collective-permute-start.8) | collective-permute-done | bytes 65568 | tf_op jit(solution)/shard_map/ppermute | solution.py:19
  69.5 3.1 %shard_map.98 = (f32[1,2,64,128]{3,2,1,0:T(8,128)}, f32[1,3,2,64,128]{4,3,2,1,0:T(8,128)}, f32[1,2,64,128]{3,2,1,0:T(8,128)}, f32[1,3,2,64,128]{4,3,2,1,0:T(8,128)}) custom-call(f32[2,4,2,64,128]{4,3,2,1,0:T(8,128)} %get-tuple-element.27.refs_0_.refs_8_, f32[2,64,128]{2,1,0:T(8,128)} %refs_1_.7, f32[2,64,128]{2,1,0:T(8,128)} %refs_2_.11, ...), custom_call_target="tpu_custom_call" | custom-call | tf_op jit(solution)/shard_map/pallas_call | solution.py:227
  (18 shorter events, 1.9 us)
Async XLA Ops:
  2.9 9.0 %collective-permute-start.1 = (f32[6,64,128]{2,1,0:T(8,128)}, f32[6,64,128]{2,1,0:T(8,128)S(1)}, u32[]{:S(2)}, u32[]{:S(2)}) collective-permute-start(f32[6,64,128]{2,1,0:T(8,128)} %get-tuple-element.18), channel_id=1, source_target_pairs={{2,0},{4,2},{6,4},{8,6},{10,8},{12,10},{14,12},{16,14},{18,16},{20... | collective-permute-start | bytes 589832 | tf_op jit(solution)/shard_map/ppermute | solution.py:19
  5.4 6.4 %collective-permute-start = (f32[5,64,128]{2,1,0:T(8,128)}, f32[5,64,128]{2,1,0:T(8,128)S(1)}, u32[]{:S(2)}, u32[]{:S(2)}) collective-permute-start(f32[5,64,128]{2,1,0:T(8,128)} %get-tuple-element.17), channel_id=1, source_target_pairs={{0,2},{2,4},{4,6},{6,8},{8,10},{10,12},{12,14},{14,16},{16,18},{18... | collective-permute-start | bytes 491528 | tf_op jit(solution)/shard_map/ppermute | solution.py:19
  11.9 0.7 copy-start.1
  12.5 0.7 copy-start.2
  17.1 7.4 %collective-permute-start.2 = (f32[4,64,128]{2,1,0:T(8,128)}, f32[4,64,128]{2,1,0:T(8,128)S(1)}, u32[]{:S(2)}, u32[]{:S(2)}) collective-permute-start(f32[4,64,128]{2,1,0:T(8,128)} %get-tuple-element.21), channel_id=1, source_target_pairs={{0,2},{2,4},{4,6},{6,8},{8,10},{10,12},{12,14},{14,16},{16,18},{18... | collective-permute-start | bytes 393224 | tf_op jit(solution)/shard_map/ppermute | solution.py:19
  22.3 7.4 %collective-permute-start.3 = (f32[4,64,128]{2,1,0:T(8,128)}, f32[4,64,128]{2,1,0:T(8,128)S(1)}, u32[]{:S(2)}, u32[]{:S(2)}) collective-permute-start(f32[4,64,128]{2,1,0:T(8,128)} %get-tuple-element.22), channel_id=1, source_target_pairs={{2,0},{4,2},{6,4},{8,6},{10,8},{12,10},{14,12},{16,14},{18,16},{20... | collective-permute-start | bytes 393224 | tf_op jit(solution)/shard_map/ppermute | solution.py:19
  24.5 5.2 %copy-start.5 = (f32[4,64,128]{2,1,0:T(8,128)}, f32[4,64,128]{2,1,0:T(8,128)S(1)}, u32[]{:S(2)}) copy-start(f32[4,64,128]{2,1,0:T(8,128)S(1)} %collective-permute-done.2.refs_4_) | copy-start | bytes 393220
  29.7 0.7 copy-start.6
  33.7 7.9 %collective-permute-start.4 = (f32[4,2,64,128]{3,2,1,0:T(8,128)}, f32[4,2,64,128]{3,2,1,0:T(8,128)S(1)}, u32[]{:S(2)}, u32[]{:S(2)}) collective-permute-start(f32[4,2,64,128]{3,2,1,0:T(8,128)} %get-tuple-element.23), channel_id=1, source_target_pairs={{0,1},{2,3},{4,5},{6,7},{8,9},{10,11},{12,13},{14,15},{16,17},{18,... | collective-permute-start | bytes 786440 | tf_op jit(solution)/shard_map/ppermute | solution.py:19
  41.6 0.7 copy-start
  44.5 6.6 %collective-permute-start.5 = (f32[4,64,128]{2,1,0:T(8,128)}, f32[4,64,128]{2,1,0:T(8,128)S(1)}, u32[]{:S(2)}, u32[]{:S(2)}) collective-permute-start(f32[4,64,128]{2,1,0:T(8,128)} %get-tuple-element.25), channel_id=1, source_target_pairs={{0,2},{2,4},{4,6},{6,8},{8,10},{10,12},{12,14},{14,16},{16,18},{18... | collective-permute-start | bytes 393224 | tf_op jit(solution)/shard_map/ppermute | solution.py:19
  48.9 7.4 %collective-permute-start.6 = (f32[4,64,128]{2,1,0:T(8,128)}, f32[4,64,128]{2,1,0:T(8,128)S(1)}, u32[]{:S(2)}, u32[]{:S(2)}) collective-permute-start(f32[4,64,128]{2,1,0:T(8,128)} %get-tuple-element.26), channel_id=1, source_target_pairs={{2,0},{4,2},{6,4},{8,6},{10,8},{12,10},{14,12},{16,14},{18,16},{20... | collective-permute-start | bytes 393224 | tf_op jit(solution)/shard_map/ppermute | solution.py:19
  51.1 5.2 %copy-start.3 = (f32[4,64,128]{2,1,0:T(8,128)}, f32[4,64,128]{2,1,0:T(8,128)S(1)}, u32[]{:S(2)}) copy-start(f32[4,64,128]{2,1,0:T(8,128)S(1)} %collective-permute-done.5.refs_5_) | copy-start | bytes 393220
  56.3 0.7 copy-start.4
  60.3 4.3 %collective-permute-start.7 = (f32[2,64,128]{2,1,0:T(8,128)}, f32[2,64,128]{2,1,0:T(8,128)S(1)}, u32[]{:S(2)}, u32[]{:S(2)}) collective-permute-start(f32[2,64,128]{2,1,0:T(8,128)} %get-tuple-element.28), channel_id=1, source_target_pairs={{0,2},{2,4},{4,6},{6,8},{8,10},{10,12},{12,14},{14,16},{16,18},{18... | collective-permute-start | bytes 196616 | tf_op jit(solution)/shard_map/ppermute | solution.py:19
  62.2 6.7 %collective-permute-start.8 = (f32[2,64,128]{2,1,0:T(8,128)}, f32[2,64,128]{2,1,0:T(8,128)S(1)}, u32[]{:S(2)}, u32[]{:S(2)}) collective-permute-start(f32[2,64,128]{2,1,0:T(8,128)} %get-tuple-element.29), channel_id=1, source_target_pairs={{2,0},{4,2},{6,4},{8,6},{10,8},{12,10},{14,12},{16,14},{18,16},{20... | collective-permute-start | bytes 196616 | tf_op jit(solution)/shard_map/ppermute | solution.py:19
  64.6 4.3 %copy-start.7 = (f32[2,64,128]{2,1,0:T(8,128)}, f32[2,64,128]{2,1,0:T(8,128)S(1)}, u32[]{:S(2)}) copy-start(f32[2,64,128]{2,1,0:T(8,128)S(1)} %collective-permute-done.7.refs_4_) | copy-start | bytes 196612
  68.9 0.6 copy-start.8

commit v8 on v7

--- a/solution.py
+++ b/solution.py
@@ -135,7 +135,7 @@
         write(lambda c, i: late[c][i], lambda c, i: moved_ref[1, c, i])
 
 
-def pair_kernel(sizes, counts, sources, n_states, next_count, first, split, finish, *refs):
+def pair_kernel(sizes, counts, sources, n_states, next_count, first, split, finish, handoff, *refs):
     states = refs[:n_states]
     k_ref, m_ref, c_ref, fl_ref, fr_ref = refs[n_states : n_states + 5]
     rest = refs[n_states + 5 :]
@@ -152,6 +152,7 @@
     else:
         next_mass, next_stiff, prev_stiff = c_ref[0], c_ref[1], c_ref[2]
     zero = jnp.zeros_like(next_mass)
+    results = []
     for b, (h, count) in enumerate(zip(sizes, counts)):
         pres, vel = read_slot(sources[b], states, n)
         lower = [fl_ref[2 * b]] + pres[:-1]
@@ -180,25 +181,51 @@
             for c in range(3):
                 s_out[b, 1 + c, i] = vel1[i][c]
             if split and b == 0:
-                outs[-1][0, i] = pres1[i]
+                split_out = outs[(2 if next_count else 0) + (1 if first else 0)]
+                split_out[0, i] = pres1[i]
                 for c in range(3):
-                    outs[-1][1 + c, i] = vel1[i][c]
+                    split_out[1 + c, i] = vel1[i][c]
         if b < next_count:
             write_messages(b, messages(pres1, vel1, k_ref, m_ref, h), outs[0], outs[1])
+        if handoff:
+            results.append((pres1, vel1))
+    at = 2 if next_count else 0
     if first:
-        outs[2 if next_count else 0][0] = next_mass
-        outs[2 if next_count else 0][1] = next_stiff
-        outs[2 if next_count else 0][2] = prev_stiff
+        outs[at][0] = next_mass
+        outs[at][1] = next_stiff
+        outs[at][2] = prev_stiff
+        at += 1
+    if handoff:
+        at += 1 if split else 0
+        (p0, v0), (p1, v1) = results
+        diff_p = [p1[i] - p0[i] for i in range(n)]
+        diff_v = [[v1[i][c] - v0[i][c] for c in range(3)] for i in range(n)]
+        for b, (pres, vel) in enumerate(((p0, v0), (diff_p, diff_v))):
+            write_messages(b, messages(pres, vel, k_ref, m_ref, handoff[b]), outs[at], outs[at + 1])
 
 
 def planes(count, like):
     return jax.ShapeDtypeStruct((count,) + like.shape[-2:], like.dtype)
 
 
+def diagonal(x, by):
+    spaces, groups = lax.axis_size("space"), lax.axis_size("tm")
+    pairs = [
+        (s * groups + c, (s + by) * groups + c + 1)
+        for s in range(spaces)
+        for c in range(groups - 1)
+        if 0 <= s + by < spaces
+    ]
+    return lax.ppermute(x, ("space", "tm"), pairs)
+
+
 def advance(states, sources, to_right, to_left, stiffness, inv_mass, consts, sizes, counts,
-            next_count, split=False, finish=None):
-    from_left = from_behind(to_right, "space", 1)
-    from_right = from_behind(to_left, "space", -1)
+            next_count, split=False, finish=None, handoff=None, received=None):
+    if received is None:
+        from_left = from_behind(to_right, "space", 1)
+        from_right = from_behind(to_left, "space", -1)
+    else:
+        from_left, from_right = received
     first = consts is None
     if first:
         consts = from_left
@@ -220,9 +247,11 @@
             outs.append(planes(3, stiffness))
         if split:
             outs.append(jax.ShapeDtypeStruct((4,) + stiffness.shape, stiffness.dtype))
+        if handoff:
+            outs += [planes(4, stiffness), planes(4, stiffness)]
     kernel = functools.partial(
         pair_kernel, tuple(sizes), tuple(counts), tuple(sources), len(states), next_count, first,
-        split, finish is not None,
+        split, finish is not None, handoff,
     )
     return pl.pallas_call(kernel, out_shape=tuple(outs), in_specs=specs)(*args)
 
@@ -277,21 +306,20 @@
     packed = (("packed", 0, 0), ("packed", 0, 1))
     for repeat in range(1, rounds):
         count = 2 if repeat + 1 < rounds else 0
+        last_round = repeat + 1 == rounds
         outs = advance(
             (state,), packed, to_right, to_left, stiffness, inv_mass, consts, fine2, (2, 2), count,
-            split=repeat + 1 == rounds,
+            split=last_round, handoff=(fine_size, DT_COARSE) if last_round else None,
         )
         state = outs[0]
         if count:
             to_right, to_left = outs[1], outs[2]
-    relaxed = outs[-1]
+    relaxed, hand_right, hand_left = outs[-3], outs[-2], outs[-1]
 
     got = from_behind(relaxed, "tm", 1)
+    received = (diagonal(hand_right, 1), diagonal(hand_left, -1))
     late_states = (got, state)
     late_sources = (("flat", 0), ("diff", 1, 1, 0))
-    to_right, to_left = first_messages(
-        late_states, late_sources, stiffness, inv_mass, (fine_size, DT_COARSE)
-    )
     flag = jnp.reshape(group, (1,)).astype(jnp.int32)
     both = None
     late = None
@@ -303,7 +331,7 @@
             sizes, counts, states, srcs = (fine_size,), (2,), (late,), (("packed", 0, 0),)
         finish = (flag, state, both) if (groups == 2 and repeat + 1 == rounds) else None
         outs = advance(states, srcs, to_right, to_left, stiffness, inv_mass, consts, sizes, counts,
-                       count, finish=finish)
+                       count, finish=finish, received=received if repeat == 0 else None)
         if finish is not None:
             return outs
         late = outs[0]

time: 73 us -> 65.9 us (0.903)
  waiting for transfers between devices: 24.4 us -> 21 us
  Pallas kernels: 18 us -> 16.1 us
  starting transfers between devices: 25.4 us -> 24.3 us
    ppermute x9 -> x7, waiting for transfers between devices: 24.4 us -> 13.4 us  [from_behind(): return lax.ppermute(x, axis, pairs)]
    ppermute x0 -> x2, waiting for transfers between devices: none -> 7.59 us  [diagonal(): return lax.ppermute(x, ('space', 'tm'), pairs)]
    ppermute x9 -> x7, starting transfers between devices: 25.4 us -> 21.7 us  [from_behind(): return lax.ppermute(x, axis, pairs)]
    ppermute x0 -> x2, starting transfers between devices: none -> 2.58 us  [diagonal(): return lax.ppermute(x, ('space', 'tm'), pairs)]
    pallas_call x2 -> x1, Pallas kernels: 4.43 us -> 2.23 us  [first_messages(): pl.pallas_call(kernel, out_shape=(planes(width + (1 if extras else 0), st...]
  transfers between devices with their start and end apart: 9 -> 9, of which waited for: 7 -> 6; matrix products, arithmetic and copies ran while one was open for 0% -> 0% of each run, Pallas kernels for 0% -> 0%
where the time goes in v8:
time: 65.9 us; the launch traced here: 65.5 us
  starting transfers between devices  24.3 us (37%)
  waiting for transfers between devices  21 us (32%)
  Pallas kernels  16.1 us (24%)
  local copies, waits for them, and re-layouts  3.32 us (5%)
  between operations  0.74 us (1%)
    ppermute x7, starting transfers between devices, from_behind(): return lax.ppermute(x, axis, pairs)  21.7 us
    pallas_call x4, Pallas kernels, advance(): return pl.pallas_call(kernel, out_shape=tuple(outs), in_specs=specs)(*args)  13.9 us
    ppermute x7, waiting for transfers between devices, from_behind(): return lax.ppermute(x, axis, pairs)  13.4 us
    ppermute x2, waiting for transfers between devices, diagonal(): return lax.ppermute(x, ('space', 'tm'), pairs)  7.59 us
    unnamed x18, local copies, waits for them, and re-layouts  3.32 us
    ppermute x2, starting transfers between devices, diagonal(): return lax.ppermute(x, ('space', 'tm'), pairs)  2.58 us
    pallas_call x1, Pallas kernels, first_messages(): pl.pallas_call(kernel, out_shape=(planes(width + (1 if extras else 0), st...  2.23 us
  transfers between devices with their start and end apart: 9, of which 6 were waited for; matrix products, arithmetic and copies ran while one was open for 0% of the time, Pallas kernels for 0%

profile of v8, /device:TPU:7, one launch (start us, length us, event | category | flops | bytes accessed | tf_op | source)
XLA Modules:
  0.0 65.5 jit_solution(432949467816800983)
XLA Ops:
  0.6 2.2 %shard_map.93 = (f32[5,64,128]{2,1,0:T(8,128)}, f32[6,64,128]{2,1,0:T(8,128)}) custom-call(f32[1,2,64,128]{3,2,1,0:T(8,128)} %refs_0_.3, f32[1,3,2,64,128]{4,3,2,1,0:T(8,128)} %refs_1_.5, f32[2,64,128]{2,1,0:T(8,128)} %refs_2_.6, f32[3,2,64,128]{3,2,1,0:T(8,128)} %refs_3_.4, f32[2,64,128]{2,1,0:T(8,128)} %refs_1_.7, f32[2,64,128]{2,1,0:T(8,128)} %refs_2_.9), custom_call_target="tpu_custom_call" | custom-call | tf_op jit(solution)/shard_map/pallas_call | solution.py:276
  2.9 2.6 %collective-permute-start.1 = (f32[6,64,128]{2,1,0:T(8,128)}, f32[6,64,128]{2,1,0:T(8,128)S(1)}, u32[]{:S(2)}, u32[]{:S(2)}) collective-permute-start(f32[6,64,128]{2,1,0:T(8,128)} %get-tuple-element.18), channel_id=1, source_target_pairs={{2,0},{4,2},{6,4},{8,6},{10,8},{12,10},{14,12},{16,14},{18,16},{20... | collective-permute-start | bytes 589832 | tf_op jit(solution)/shard_map/ppermute | solution.py:19
  5.4 3.9 %collective-permute-start = (f32[5,64,128]{2,1,0:T(8,128)}, f32[5,64,128]{2,1,0:T(8,128)S(1)}, u32[]{:S(2)}, u32[]{:S(2)}) collective-permute-start(f32[5,64,128]{2,1,0:T(8,128)} %get-tuple-element.17), channel_id=1, source_target_pairs={{0,2},{2,4},{4,6},{6,8},{8,10},{10,12},{12,14},{14,16},{16,18},{18... | collective-permute-start | bytes 491528 | tf_op jit(solution)/shard_map/ppermute | solution.py:19
  9.3 2.6 %collective-permute-done.refs_6_.refs_7_ = f32[5,64,128]{2,1,0:T(8,128)S(1)} collective-permute-done((f32[5,64,128]{2,1,0:T(8,128)}, f32[5,64,128]{2,1,0:T(8,128)S(1)}, u32[]{:S(2)}, u32[]{:S(2)}) %collective-permute-start) | collective-permute-done | bytes 163872 | tf_op jit(solution)/shard_map/ppermute | solution.py:19
  11.9 0.7 %copy-done = f32[5,64,128]{2,1,0:T(8,128)} copy-done((f32[5,64,128]{2,1,0:T(8,128)}, f32[5,64,128]{2,1,0:T(8,128)S(1)}, u32[]{:S(2)}) %copy-start) | copy-done | bytes 163864
  12.5 0.7 %copy-done.2 = f32[6,64,128]{2,1,0:T(8,128)} copy-done((f32[6,64,128]{2,1,0:T(8,128)}, f32[6,64,128]{2,1,0:T(8,128)S(1)}, u32[]{:S(2)}) %copy-start.2) | copy-done | bytes 196632
  13.2 3.9 %shard_map.94 = (f32[2,4,2,64,128]{4,3,2,1,0:T(8,128)}, f32[4,64,128]{2,1,0:T(8,128)}, f32[4,64,128]{2,1,0:T(8,128)}, f32[3,64,128]{2,1,0:T(8,128)}) custom-call(f32[1,2,64,128]{3,2,1,0:T(8,128)} %refs_0_.3, f32[1,3,2,64,128]{4,3,2,1,0:T(8,128)} %refs_1_.5, f32[2,64,128]{2,1,0:T(8,128)} %refs_2_.6, f32[3,2,64,128]{3,2,1,0:T(8,128)} %refs_3_.4, ...), custom_call_target="tpu_custom_call" | custom-call | tf_op jit(solution)/shard_map/pallas_call | solution.py:256
  17.1 5.2 %collective-permute-start.2 = (f32[4,64,128]{2,1,0:T(8,128)}, f32[4,64,128]{2,1,0:T(8,128)S(1)}, u32[]{:S(2)}, u32[]{:S(2)}) collective-permute-start(f32[4,64,128]{2,1,0:T(8,128)} %get-tuple-element.21), channel_id=1, source_target_pairs={{0,2},{2,4},{4,6},{6,8},{8,10},{10,12},{12,14},{14,16},{16,18},{18... | collective-permute-start | bytes 393224 | tf_op jit(solution)/shard_map/ppermute | solution.py:19
  22.3 1.9 %collective-permute-start.3 = (f32[4,64,128]{2,1,0:T(8,128)}, f32[4,64,128]{2,1,0:T(8,128)S(1)}, u32[]{:S(2)}, u32[]{:S(2)}) collective-permute-start(f32[4,64,128]{2,1,0:T(8,128)} %get-tuple-element.22), channel_id=1, source_target_pairs={{2,0},{4,2},{6,4},{8,6},{10,8},{12,10},{14,12},{16,14},{18,16},{20... | collective-permute-start | bytes 393224 | tf_op jit(solution)/shard_map/ppermute | solution.py:19
  24.5 5.2 %collective-permute-done.3.refs_5_ = f32[4,64,128]{2,1,0:T(8,128)S(1)} collective-permute-done((f32[4,64,128]{2,1,0:T(8,128)}, f32[4,64,128]{2,1,0:T(8,128)S(1)}, u32[]{:S(2)}, u32[]{:S(2)}) %collective-permute-start.3) | collective-permute-done | bytes 131104 | tf_op jit(solution)/shard_map/ppermute | solution.py:19
  29.7 0.7 copy-done.6
  30.3 3.6 %shard_map.95 = (f32[2,4,2,64,128]{4,3,2,1,0:T(8,128)}, f32[4,2,64,128]{3,2,1,0:T(8,128)}, f32[4,64,128]{2,1,0:T(8,128)}, f32[4,64,128]{2,1,0:T(8,128)}) custom-call(f32[2,4,2,64,128]{4,3,2,1,0:T(8,128)} %get-tuple-element.19.refs_0_, f32[2,64,128]{2,1,0:T(8,128)} %refs_1_.7, f32[2,64,128]{2,1,0:T(8,128)} %refs_2_.9, ...), custom_call_target="tpu_custom_call" | custom-call | tf_op jit(solution)/shard_map/pallas_call | solution.py:256
  34.0 1.3 %collective-permute-start.4 = (f32[4,2,64,128]{3,2,1,0:T(8,128)}, f32[4,2,64,128]{3,2,1,0:T(8,128)S(1)}, u32[]{:S(2)}, u32[]{:S(2)}) collective-permute-start(f32[4,2,64,128]{3,2,1,0:T(8,128)} %get-tuple-element.23), channel_id=1, source_target_pairs={{0,1},{2,3},{4,5},{6,7},{8,9},{10,11},{12,13},{14,15},{16,17},{18,... | collective-permute-start | bytes 786440 | tf_op jit(solution)/shard_map/ppermute | solution.py:19
  35.3 1.3 %collective-permute-start.5 = (f32[4,64,128]{2,1,0:T(8,128)}, f32[4,64,128]{2,1,0:T(8,128)S(1)}, u32[]{:S(2)}, u32[]{:S(2)}) collective-permute-start(f32[4,64,128]{2,1,0:T(8,128)} %get-tuple-element.25), channel_id=1, source_target_pairs={{0,3},{2,5},{4,7},{6,9},{8,11},{10,13},{12,15},{14,17},{16,19},{18... | collective-permute-start | bytes 393224 | tf_op jit(solution)/shard_map/ppermute | solution.py:219
  36.6 1.3 %collective-permute-start.6 = (f32[4,64,128]{2,1,0:T(8,128)}, f32[4,64,128]{2,1,0:T(8,128)S(1)}, u32[]{:S(2)}, u32[]{:S(2)}) collective-permute-start(f32[4,64,128]{2,1,0:T(8,128)} %get-tuple-element.26), channel_id=1, source_target_pairs={{2,1},{4,3},{6,5},{8,7},{10,9},{12,11},{14,13},{16,15},{18,17},{20... | collective-permute-start | bytes 393224 | tf_op jit(solution)/shard_map/ppermute | solution.py:219
  37.9 7.6 %collective-permute-done.5.refs_5_ = f32[4,64,128]{2,1,0:T(8,128)S(1)} collective-permute-done((f32[4,64,128]{2,1,0:T(8,128)}, f32[4,64,128]{2,1,0:T(8,128)S(1)}, u32[]{:S(2)}, u32[]{:S(2)}) %collective-permute-start.5) | collective-permute-done | bytes 131104 | tf_op jit(solution)/shard_map/ppermute | solution.py:219
  45.5 0.6 collective-permute-done.4.refs_0_
  46.2 0.6 copy-done.1
  46.8 3.3 %shard_map.96 = (f32[2,4,2,64,128]{4,3,2,1,0:T(8,128)}, f32[2,64,128]{2,1,0:T(8,128)}, f32[2,64,128]{2,1,0:T(8,128)}) custom-call(f32[4,2,64,128]{3,2,1,0:T(8,128)} %copy-done.1, f32[2,4,2,64,128]{4,3,2,1,0:T(8,128)} %get-tuple-element.24.refs_1_.refs_7_, f32[2,64,128]{2,1,0:T(8,128)} %refs_1_.7, f32[2,64,128]{2,1,0:T(8,128)} %refs_2_.9, ...), custom_call_target="tpu_custom_call" | custom-call | tf_op jit(solution)/shard_map/pallas_call | solution.py:256
  50.1 5.0 %collective-permute-start.7 = (f32[2,64,128]{2,1,0:T(8,128)}, f32[2,64,128]{2,1,0:T(8,128)S(1)}, u32[]{:S(2)}, u32[]{:S(2)}) collective-permute-start(f32[2,64,128]{2,1,0:T(8,128)} %get-tuple-element.28), channel_id=1, source_target_pairs={{0,2},{2,4},{4,6},{6,8},{8,10},{10,12},{12,14},{14,16},{16,18},{18... | collective-permute-start | bytes 196616 | tf_op jit(solution)/shard_map/ppermute | solution.py:19
  55.1 1.9 %collective-permute-start.8 = (f32[2,64,128]{2,1,0:T(8,128)}, f32[2,64,128]{2,1,0:T(8,128)S(1)}, u32[]{:S(2)}, u32[]{:S(2)}) collective-permute-start(f32[2,64,128]{2,1,0:T(8,128)} %get-tuple-element.29), channel_id=1, source_target_pairs={{2,0},{4,2},{6,4},{8,6},{10,8},{12,10},{14,12},{16,14},{18,16},{20... | collective-permute-start | bytes 196616 | tf_op jit(solution)/shard_map/ppermute | solution.py:19
  57.1 4.7 %collective-permute-done.8.refs_5_ = f32[2,64,128]{2,1,0:T(8,128)S(1)} collective-permute-done((f32[2,64,128]{2,1,0:T(8,128)}, f32[2,64,128]{2,1,0:T(8,128)S(1)}, u32[]{:S(2)}, u32[]{:S(2)}) %collective-permute-start.8) | collective-permute-done | bytes 65568 | tf_op jit(solution)/shard_map/ppermute | solution.py:19
  61.8 0.6 copy-done.8
  62.4 3.1 %shard_map.97 = (f32[1,2,64,128]{3,2,1,0:T(8,128)}, f32[1,3,2,64,128]{4,3,2,1,0:T(8,128)}, f32[1,2,64,128]{3,2,1,0:T(8,128)}, f32[1,3,2,64,128]{4,3,2,1,0:T(8,128)}) custom-call(f32[2,4,2,64,128]{4,3,2,1,0:T(8,128)} %get-tuple-element.27.refs_0_.refs_8_, f32[2,64,128]{2,1,0:T(8,128)} %refs_1_.7, f32[2,64,128]{2,1,0:T(8,128)} %refs_2_.9, ...), custom_call_target="tpu_custom_call" | custom-call | tf_op jit(solution)/shard_map/pallas_call | solution.py:256
  (17 shorter events, 0.4 us)
Async XLA Ops:
  2.9 9.0 %collective-permute-start.1 = (f32[6,64,128]{2,1,0:T(8,128)}, f32[6,64,128]{2,1,0:T(8,128)S(1)}, u32[]{:S(2)}, u32[]{:S(2)}) collective-permute-start(f32[6,64,128]{2,1,0:T(8,128)} %get-tuple-element.18), channel_id=1, source_target_pairs={{2,0},{4,2},{6,4},{8,6},{10,8},{12,10},{14,12},{16,14},{18,16},{20... | collective-permute-start | bytes 589832 | tf_op jit(solution)/shard_map/ppermute | solution.py:19
  5.4 6.4 %collective-permute-start = (f32[5,64,128]{2,1,0:T(8,128)}, f32[5,64,128]{2,1,0:T(8,128)S(1)}, u32[]{:S(2)}, u32[]{:S(2)}) collective-permute-start(f32[5,64,128]{2,1,0:T(8,128)} %get-tuple-element.17), channel_id=1, source_target_pairs={{0,2},{2,4},{4,6},{6,8},{8,10},{10,12},{12,14},{14,16},{16,18},{18... | collective-permute-start | bytes 491528 | tf_op jit(solution)/shard_map/ppermute | solution.py:19
  11.9 0.7 %copy-start = (f32[5,64,128]{2,1,0:T(8,128)}, f32[5,64,128]{2,1,0:T(8,128)S(1)}, u32[]{:S(2)}) copy-start(f32[5,64,128]{2,1,0:T(8,128)S(1)} %collective-permute-done.refs_6_.refs_7_) | copy-start | bytes 491524
  12.5 0.7 %copy-start.2 = (f32[6,64,128]{2,1,0:T(8,128)}, f32[6,64,128]{2,1,0:T(8,128)S(1)}, u32[]{:S(2)}) copy-start(f32[6,64,128]{2,1,0:T(8,128)S(1)} %collective-permute-done.1.refs_8_) | copy-start | bytes 589828
  17.1 7.4 %collective-permute-start.2 = (f32[4,64,128]{2,1,0:T(8,128)}, f32[4,64,128]{2,1,0:T(8,128)S(1)}, u32[]{:S(2)}, u32[]{:S(2)}) collective-permute-start(f32[4,64,128]{2,1,0:T(8,128)} %get-tuple-element.21), channel_id=1, source_target_pairs={{0,2},{2,4},{4,6},{6,8},{8,10},{10,12},{12,14},{14,16},{16,18},{18... | collective-permute-start | bytes 393224 | tf_op jit(solution)/shard_map/ppermute | solution.py:19
  22.3 7.4 %collective-permute-start.3 = (f32[4,64,128]{2,1,0:T(8,128)}, f32[4,64,128]{2,1,0:T(8,128)S(1)}, u32[]{:S(2)}, u32[]{:S(2)}) collective-permute-start(f32[4,64,128]{2,1,0:T(8,128)} %get-tuple-element.22), channel_id=1, source_target_pairs={{2,0},{4,2},{6,4},{8,6},{10,8},{12,10},{14,12},{16,14},{18,16},{20... | collective-permute-start | bytes 393224 | tf_op jit(solution)/shard_map/ppermute | solution.py:19
  24.5 5.2 %copy-start.5 = (f32[4,64,128]{2,1,0:T(8,128)}, f32[4,64,128]{2,1,0:T(8,128)S(1)}, u32[]{:S(2)}) copy-start(f32[4,64,128]{2,1,0:T(8,128)S(1)} %collective-permute-done.2.refs_4_) | copy-start | bytes 393220
  29.7 0.7 %copy-start.6 = (f32[4,64,128]{2,1,0:T(8,128)}, f32[4,64,128]{2,1,0:T(8,128)S(1)}, u32[]{:S(2)}) copy-start(f32[4,64,128]{2,1,0:T(8,128)S(1)} %collective-permute-done.3.refs_5_) | copy-start | bytes 393220
  34.0 12.1 %collective-permute-start.4 = (f32[4,2,64,128]{3,2,1,0:T(8,128)}, f32[4,2,64,128]{3,2,1,0:T(8,128)S(1)}, u32[]{:S(2)}, u32[]{:S(2)}) collective-permute-start(f32[4,2,64,128]{3,2,1,0:T(8,128)} %get-tuple-element.23), channel_id=1, source_target_pairs={{0,1},{2,3},{4,5},{6,7},{8,9},{10,11},{12,13},{14,15},{16,17},{18,... | collective-permute-start | bytes 786440 | tf_op jit(solution)/shard_map/ppermute | solution.py:19
  35.3 10.2 %collective-permute-start.5 = (f32[4,64,128]{2,1,0:T(8,128)}, f32[4,64,128]{2,1,0:T(8,128)S(1)}, u32[]{:S(2)}, u32[]{:S(2)}) collective-permute-start(f32[4,64,128]{2,1,0:T(8,128)} %get-tuple-element.25), channel_id=1, source_target_pairs={{0,3},{2,5},{4,7},{6,9},{8,11},{10,13},{12,15},{14,17},{16,19},{18... | collective-permute-start | bytes 393224 | tf_op jit(solution)/shard_map/ppermute | solution.py:219
  36.6 8.9 %collective-permute-start.6 = (f32[4,64,128]{2,1,0:T(8,128)}, f32[4,64,128]{2,1,0:T(8,128)S(1)}, u32[]{:S(2)}, u32[]{:S(2)}) collective-permute-start(f32[4,64,128]{2,1,0:T(8,128)} %get-tuple-element.26), channel_id=1, source_target_pairs={{2,1},{4,3},{6,5},{8,7},{10,9},{12,11},{14,13},{16,15},{18,17},{20... | collective-permute-start | bytes 393224 | tf_op jit(solution)/shard_map/ppermute | solution.py:219
  45.5 0.7 %copy-start.3 = (f32[4,64,128]{2,1,0:T(8,128)}, f32[4,64,128]{2,1,0:T(8,128)S(1)}, u32[]{:S(2)}) copy-start(f32[4,64,128]{2,1,0:T(8,128)S(1)} %collective-permute-done.5.refs_5_) | copy-start | bytes 393220
  45.5 0.7 %copy-start.4 = (f32[4,64,128]{2,1,0:T(8,128)}, f32[4,64,128]{2,1,0:T(8,128)S(1)}, u32[]{:S(2)}) copy-start(f32[4,64,128]{2,1,0:T(8,128)S(1)} %collective-permute-done.6.refs_6_) | copy-start | bytes 393220
  46.1 0.7 %copy-start.1 = (f32[4,2,64,128]{3,2,1,0:T(8,128)}, f32[4,2,64,128]{3,2,1,0:T(8,128)S(1)}, u32[]{:S(2)}) copy-start(f32[4,2,64,128]{3,2,1,0:T(8,128)S(1)} %collective-permute-done.4.refs_0_) | copy-start | bytes 786436
  50.1 6.9 %collective-permute-start.7 = (f32[2,64,128]{2,1,0:T(8,128)}, f32[2,64,128]{2,1,0:T(8,128)S(1)}, u32[]{:S(2)}, u32[]{:S(2)}) collective-permute-start(f32[2,64,128]{2,1,0:T(8,128)} %get-tuple-element.28), channel_id=1, source_target_pairs={{0,2},{2,4},{4,6},{6,8},{8,10},{10,12},{12,14},{14,16},{16,18},{18... | collective-permute-start | bytes 196616 | tf_op jit(solution)/shard_map/ppermute | solution.py:19
  55.1 6.7 %collective-permute-start.8 = (f32[2,64,128]{2,1,0:T(8,128)}, f32[2,64,128]{2,1,0:T(8,128)S(1)}, u32[]{:S(2)}, u32[]{:S(2)}) collective-permute-start(f32[2,64,128]{2,1,0:T(8,128)} %get-tuple-element.29), channel_id=1, source_target_pairs={{2,0},{4,2},{6,4},{8,6},{10,8},{12,10},{14,12},{16,14},{18,16},{20... | collective-permute-start | bytes 196616 | tf_op jit(solution)/shard_map/ppermute | solution.py:19
  57.0 4.8 %copy-start.7 = (f32[2,64,128]{2,1,0:T(8,128)}, f32[2,64,128]{2,1,0:T(8,128)S(1)}, u32[]{:S(2)}) copy-start(f32[2,64,128]{2,1,0:T(8,128)S(1)} %collective-permute-done.7.refs_4_) | copy-start | bytes 196612
  61.8 0.6 copy-start.8

commit v9 on v8

--- a/solution.py
+++ b/solution.py
@@ -132,10 +132,11 @@
 
     @pl.when(g_ref[0] != 0)
     def _():
-        write(lambda c, i: late[c][i], lambda c, i: moved_ref[1, c, i])
-
-
-def pair_kernel(sizes, counts, sources, n_states, next_count, first, split, finish, handoff, *refs):
+        write(lambda c, i: late[c][i], lambda c, i: moved_ref[0, c, i])
+
+
+def pair_kernel(sizes, counts, sources, n_states, next_count, first, split, finish, handoff, offset,
+                *refs):
     states = refs[:n_states]
     k_ref, m_ref, c_ref, fl_ref, fr_ref = refs[n_states : n_states + 5]
     rest = refs[n_states + 5 :]
@@ -155,16 +156,17 @@
     results = []
     for b, (h, count) in enumerate(zip(sizes, counts)):
         pres, vel = read_slot(sources[b], states, n)
-        lower = [fl_ref[2 * b]] + pres[:-1]
+        m = b + offset
+        lower = [fl_ref[2 * m]] + pres[:-1]
         vel1 = [[vel[i][c] + h * m_ref[i] * f for c, f in enumerate(forces(pres[i], lower[i]))]
                 for i in range(n)]
         pres1 = [pres[i] - h * k_ref[i] * divergence(vel1[i], vel1[i + 1]) for i in range(n - 1)]
         below = [h * next_mass * f for f in forces(zero, pres[n - 1])]
-        upper1 = fr_ref[2 * b] + upper_part(below)
+        upper1 = fr_ref[2 * m] + upper_part(below)
         pres1.append(pres[n - 1] - h * k_ref[n - 1] * (0.25 * (lower_part(vel1[n - 1]) + upper1)))
         if count == 2:
-            prev1 = fl_ref[2 * b + 1] - h * prev_stiff * (0.25 * upper_part(vel1[0]))
-            next1 = fr_ref[2 * b + 1] - h * next_stiff * (0.25 * lower_part(below))
+            prev1 = fl_ref[2 * m + 1] - h * prev_stiff * (0.25 * upper_part(vel1[0]))
+            next1 = fr_ref[2 * m + 1] - h * next_stiff * (0.25 * lower_part(below))
             lower = [prev1] + pres1[:-1]
             vel2 = [[vel1[i][c] + h * m_ref[i] * f for c, f in enumerate(forces(pres1[i], lower[i]))]
                     for i in range(n)]
@@ -220,7 +222,7 @@
 
 
 def advance(states, sources, to_right, to_left, stiffness, inv_mass, consts, sizes, counts,
-            next_count, split=False, finish=None, handoff=None, received=None):
+            next_count, split=False, finish=None, handoff=None, received=None, offset=0):
     if received is None:
         from_left = from_behind(to_right, "space", 1)
         from_right = from_behind(to_left, "space", -1)
@@ -251,7 +253,7 @@
             outs += [planes(4, stiffness), planes(4, stiffness)]
     kernel = functools.partial(
         pair_kernel, tuple(sizes), tuple(counts), tuple(sources), len(states), next_count, first,
-        split, finish is not None, handoff,
+        split, finish is not None, handoff, offset,
     )
     return pl.pallas_call(kernel, out_shape=tuple(outs), in_specs=specs)(*args)
 
@@ -321,22 +323,21 @@
     late_states = (got, state)
     late_sources = (("flat", 0), ("diff", 1, 1, 0))
     flag = jnp.reshape(group, (1,)).astype(jnp.int32)
-    both = None
+    (moved,) = advance(late_states, (late_sources[1],), None, None, stiffness, inv_mass, consts,
+                       (DT_COARSE,), (1,), 0, received=received, offset=1)
     late = None
     for repeat in range(rounds):
         count = 1 if repeat + 1 < rounds else 0
         if repeat == 0:
-            sizes, counts, states, srcs = (fine_size, DT_COARSE), (2, 1), late_states, late_sources
+            states, srcs = late_states, late_sources[:1]
         else:
-            sizes, counts, states, srcs = (fine_size,), (2,), (late,), (("packed", 0, 0),)
-        finish = (flag, state, both) if (groups == 2 and repeat + 1 == rounds) else None
-        outs = advance(states, srcs, to_right, to_left, stiffness, inv_mass, consts, sizes, counts,
-                       count, finish=finish, received=received if repeat == 0 else None)
+            states, srcs = (late,), (("packed", 0, 0),)
+        finish = (flag, state, moved) if (groups == 2 and repeat + 1 == rounds) else None
+        outs = advance(states, srcs, to_right, to_left, stiffness, inv_mass, consts, (fine_size,),
+                       (2,), count, finish=finish, received=received if repeat == 0 else None)
         if finish is not None:
             return outs
         late = outs[0]
-        if repeat == 0:
-            both = late
         if count:
             to_right, to_left = outs[1], outs[2]
 

time: 65.9 us -> 65.3 us (level)
  waiting for transfers between devices: 21 us -> 18.8 us
  Pallas kernels: 16.1 us -> 17.7 us
    ppermute x7, waiting for transfers between devices: 13.4 us -> 11.2 us  [from_behind(): return lax.ppermute(x, axis, pairs)]
    pallas_call x4 -> x5, Pallas kernels: 13.9 us -> 15.5 us  [advance(): return pl.pallas_call(kernel, out_shape=tuple(outs), in_specs=specs)(*args)]
  transfers between devices with their start and end apart: 9 -> 9, of which waited for: 6 -> 6; matrix products, arithmetic and copies ran while one was open for 0% -> 0% of each run, Pallas kernels for 0% -> 3%
where the time goes in v9:
time: 65.3 us; the launch traced here: 64.8 us
  starting transfers between devices  24.3 us (37%)
  waiting for transfers between devices  18.8 us (29%)
  Pallas kernels  17.7 us (27%)
  local copies, waits for them, and re-layouts  3.31 us (5%)
  between operations  0.72 us (1%)
    ppermute x7, starting transfers between devices, from_behind(): return lax.ppermute(x, axis, pairs)  21.7 us
    pallas_call x5, Pallas kernels, advance(): return pl.pallas_call(kernel, out_shape=tuple(outs), in_specs=specs)(*args)  15.5 us
    ppermute x7, waiting for transfers between devices, from_behind(): return lax.ppermute(x, axis, pairs)  11.2 us
    ppermute x2, waiting for transfers between devices, diagonal(): return lax.ppermute(x, ('space', 'tm'), pairs)  7.59 us
    unnamed x18, local copies, waits for them, and re-layouts  3.31 us
    ppermute x2, starting transfers between devices, diagonal(): return lax.ppermute(x, ('space', 'tm'), pairs)  2.58 us
    pallas_call x1, Pallas kernels, first_messages(): pl.pallas_call(kernel, out_shape=(planes(width + (1 if extras else 0), st...  2.23 us
  transfers between devices with their start and end apart: 9, of which 6 were waited for; matrix products, arithmetic and copies ran while one was open for 0% of the time, Pallas kernels for 3%

profile of v9, /device:TPU:7, one launch (start us, length us, event | category | flops | bytes accessed | tf_op | source)
XLA Modules:
  0.0 64.8 jit_solution(8132459092800765516)
XLA Ops:
  0.6 2.2 %shard_map.93 = (f32[5,64,128]{2,1,0:T(8,128)}, f32[6,64,128]{2,1,0:T(8,128)}) custom-call(f32[1,2,64,128]{3,2,1,0:T(8,128)} %refs_0_.3, f32[1,3,2,64,128]{4,3,2,1,0:T(8,128)} %refs_1_.5, f32[2,64,128]{2,1,0:T(8,128)} %refs_2_.7, f32[3,2,64,128]{3,2,1,0:T(8,128)} %refs_3_.5, f32[2,64,128]{2,1,0:T(8,128)} %refs_1_.7, f32[2,64,128]{2,1,0:T(8,128)} %refs_2_.11), custom_call_target="tpu_custom_call" | custom-call | tf_op jit(solution)/shard_map/pallas_call | solution.py:278
  2.9 2.6 %collective-permute-start.1 = (f32[6,64,128]{2,1,0:T(8,128)}, f32[6,64,128]{2,1,0:T(8,128)S(1)}, u32[]{:S(2)}, u32[]{:S(2)}) collective-permute-start(f32[6,64,128]{2,1,0:T(8,128)} %get-tuple-element.18), channel_id=1, source_target_pairs={{2,0},{4,2},{6,4},{8,6},{10,8},{12,10},{14,12},{16,14},{18,16},{20... | collective-permute-start | bytes 589832 | tf_op jit(solution)/shard_map/ppermute | solution.py:19
  5.4 3.9 %collective-permute-start = (f32[5,64,128]{2,1,0:T(8,128)}, f32[5,64,128]{2,1,0:T(8,128)S(1)}, u32[]{:S(2)}, u32[]{:S(2)}) collective-permute-start(f32[5,64,128]{2,1,0:T(8,128)} %get-tuple-element.17), channel_id=1, source_target_pairs={{0,2},{2,4},{4,6},{6,8},{8,10},{10,12},{12,14},{14,16},{16,18},{18... | collective-permute-start | bytes 491528 | tf_op jit(solution)/shard_map/ppermute | solution.py:19
  9.3 2.6 %collective-permute-done.refs_6_.refs_7_ = f32[5,64,128]{2,1,0:T(8,128)S(1)} collective-permute-done((f32[5,64,128]{2,1,0:T(8,128)}, f32[5,64,128]{2,1,0:T(8,128)S(1)}, u32[]{:S(2)}, u32[]{:S(2)}) %collective-permute-start) | collective-permute-done | bytes 163872 | tf_op jit(solution)/shard_map/ppermute | solution.py:19
  11.9 0.7 %copy-done.1 = f32[5,64,128]{2,1,0:T(8,128)} copy-done((f32[5,64,128]{2,1,0:T(8,128)}, f32[5,64,128]{2,1,0:T(8,128)S(1)}, u32[]{:S(2)}) %copy-start.1) | copy-done | bytes 163864
  12.5 0.7 %copy-done.4 = f32[6,64,128]{2,1,0:T(8,128)} copy-done((f32[6,64,128]{2,1,0:T(8,128)}, f32[6,64,128]{2,1,0:T(8,128)S(1)}, u32[]{:S(2)}) %copy-start.4) | copy-done | bytes 196632
  13.2 3.9 %shard_map.94 = (f32[2,4,2,64,128]{4,3,2,1,0:T(8,128)}, f32[4,64,128]{2,1,0:T(8,128)}, f32[4,64,128]{2,1,0:T(8,128)}, f32[3,64,128]{2,1,0:T(8,128)}) custom-call(f32[1,2,64,128]{3,2,1,0:T(8,128)} %refs_0_.3, f32[1,3,2,64,128]{4,3,2,1,0:T(8,128)} %refs_1_.5, f32[2,64,128]{2,1,0:T(8,128)} %refs_2_.7, f32[3,2,64,128]{3,2,1,0:T(8,128)} %refs_3_.5, ...), custom_call_target="tpu_custom_call" | custom-call | tf_op jit(solution)/shard_map/pallas_call | solution.py:258
  17.1 5.2 %collective-permute-start.2 = (f32[4,64,128]{2,1,0:T(8,128)}, f32[4,64,128]{2,1,0:T(8,128)S(1)}, u32[]{:S(2)}, u32[]{:S(2)}) collective-permute-start(f32[4,64,128]{2,1,0:T(8,128)} %get-tuple-element.21), channel_id=1, source_target_pairs={{0,2},{2,4},{4,6},{6,8},{8,10},{10,12},{12,14},{14,16},{16,18},{18... | collective-permute-start | bytes 393224 | tf_op jit(solution)/shard_map/ppermute | solution.py:19
  22.3 1.9 %collective-permute-start.3 = (f32[4,64,128]{2,1,0:T(8,128)}, f32[4,64,128]{2,1,0:T(8,128)S(1)}, u32[]{:S(2)}, u32[]{:S(2)}) collective-permute-start(f32[4,64,128]{2,1,0:T(8,128)} %get-tuple-element.22), channel_id=1, source_target_pairs={{2,0},{4,2},{6,4},{8,6},{10,8},{12,10},{14,12},{16,14},{18,16},{20... | collective-permute-start | bytes 393224 | tf_op jit(solution)/shard_map/ppermute | solution.py:19
  24.5 5.2 %collective-permute-done.3.refs_5_ = f32[4,64,128]{2,1,0:T(8,128)S(1)} collective-permute-done((f32[4,64,128]{2,1,0:T(8,128)}, f32[4,64,128]{2,1,0:T(8,128)S(1)}, u32[]{:S(2)}, u32[]{:S(2)}) %collective-permute-start.3) | collective-permute-done | bytes 131104 | tf_op jit(solution)/shard_map/ppermute | solution.py:19
  29.7 0.7 %copy-done.6 = f32[4,64,128]{2,1,0:T(8,128)} copy-done((f32[4,64,128]{2,1,0:T(8,128)}, f32[4,64,128]{2,1,0:T(8,128)S(1)}, u32[]{:S(2)}) %copy-start.6) | copy-done | bytes 131096
  30.3 3.6 %shard_map.95 = (f32[2,4,2,64,128]{4,3,2,1,0:T(8,128)}, f32[4,2,64,128]{3,2,1,0:T(8,128)}, f32[4,64,128]{2,1,0:T(8,128)}, f32[4,64,128]{2,1,0:T(8,128)}) custom-call(f32[2,4,2,64,128]{4,3,2,1,0:T(8,128)} %get-tuple-element.19.refs_0_, f32[2,64,128]{2,1,0:T(8,128)} %refs_1_.7, f32[2,64,128]{2,1,0:T(8,128)} %refs_2_.11, ...), custom_call_target="tpu_custom_call" | custom-call | tf_op jit(solution)/shard_map/pallas_call | solution.py:258
  34.0 1.3 %collective-permute-start.4 = (f32[4,2,64,128]{3,2,1,0:T(8,128)}, f32[4,2,64,128]{3,2,1,0:T(8,128)S(1)}, u32[]{:S(2)}, u32[]{:S(2)}) collective-permute-start(f32[4,2,64,128]{3,2,1,0:T(8,128)} %get-tuple-element.23), channel_id=1, source_target_pairs={{0,1},{2,3},{4,5},{6,7},{8,9},{10,11},{12,13},{14,15},{16,17},{18,... | collective-permute-start | bytes 786440 | tf_op jit(solution)/shard_map/ppermute | solution.py:19
  35.3 1.3 %collective-permute-start.5 = (f32[4,64,128]{2,1,0:T(8,128)}, f32[4,64,128]{2,1,0:T(8,128)S(1)}, u32[]{:S(2)}, u32[]{:S(2)}) collective-permute-start(f32[4,64,128]{2,1,0:T(8,128)} %get-tuple-element.25), channel_id=1, source_target_pairs={{0,3},{2,5},{4,7},{6,9},{8,11},{10,13},{12,15},{14,17},{16,19},{18... | collective-permute-start | bytes 393224 | tf_op jit(solution)/shard_map/ppermute | solution.py:221
  36.6 1.3 %collective-permute-start.6 = (f32[4,64,128]{2,1,0:T(8,128)}, f32[4,64,128]{2,1,0:T(8,128)S(1)}, u32[]{:S(2)}, u32[]{:S(2)}) collective-permute-start(f32[4,64,128]{2,1,0:T(8,128)} %get-tuple-element.26), channel_id=1, source_target_pairs={{2,1},{4,3},{6,5},{8,7},{10,9},{12,11},{14,13},{16,15},{18,17},{20... | collective-permute-start | bytes 393224 | tf_op jit(solution)/shard_map/ppermute | solution.py:221
  37.9 7.6 %collective-permute-done.5.refs_5_ = f32[4,64,128]{2,1,0:T(8,128)S(1)} collective-permute-done((f32[4,64,128]{2,1,0:T(8,128)}, f32[4,64,128]{2,1,0:T(8,128)S(1)}, u32[]{:S(2)}, u32[]{:S(2)}) %collective-permute-start.5) | collective-permute-done | bytes 131104 | tf_op jit(solution)/shard_map/ppermute | solution.py:221
  45.5 0.6 collective-permute-done.4.refs_0_
  46.2 0.6 copy-done
  46.8 2.8 %shard_map.96 = (f32[1,4,2,64,128]{4,3,2,1,0:T(8,128)}, f32[2,64,128]{2,1,0:T(8,128)}, f32[2,64,128]{2,1,0:T(8,128)}) custom-call(f32[4,2,64,128]{3,2,1,0:T(8,128)} %copy-done, f32[2,4,2,64,128]{4,3,2,1,0:T(8,128)} %get-tuple-element.24.refs_1_.refs_7_, f32[2,64,128]{2,1,0:T(8,128)} %refs_1_.7, f32[2,64,128]{2,1,0:T(8,128)} %refs_2_.11, ...), custom_call_target="tpu_custom_call" | custom-call | tf_op jit(solution)/shard_map/pallas_call | solution.py:258
  49.6 5.0 %collective-permute-start.7 = (f32[2,64,128]{2,1,0:T(8,128)}, f32[2,64,128]{2,1,0:T(8,128)S(1)}, u32[]{:S(2)}, u32[]{:S(2)}) collective-permute-start(f32[2,64,128]{2,1,0:T(8,128)} %get-tuple-element.28), channel_id=1, source_target_pairs={{0,2},{2,4},{4,6},{6,8},{8,10},{10,12},{12,14},{14,16},{16,18},{18... | collective-permute-start | bytes 196616 | tf_op jit(solution)/shard_map/ppermute | solution.py:19
  54.6 1.9 %collective-permute-start.8 = (f32[2,64,128]{2,1,0:T(8,128)}, f32[2,64,128]{2,1,0:T(8,128)S(1)}, u32[]{:S(2)}, u32[]{:S(2)}) collective-permute-start(f32[2,64,128]{2,1,0:T(8,128)} %get-tuple-element.29), channel_id=1, source_target_pairs={{2,0},{4,2},{6,4},{8,6},{10,8},{12,10},{14,12},{16,14},{18,16},{20... | collective-permute-start | bytes 196616 | tf_op jit(solution)/shard_map/ppermute | solution.py:19
  56.5 2.2 %shard_map.97.refs_8_ = f32[1,4,2,64,128]{4,3,2,1,0:T(8,128)} custom-call(f32[4,2,64,128]{3,2,1,0:T(8,128)} %copy-done, f32[2,4,2,64,128]{4,3,2,1,0:T(8,128)} %get-tuple-element.24.refs_1_.refs_7_, f32[2,64,128]{2,1,0:T(8,128)} %refs_1_.7, f32[2,64,128]{2,1,0:T(8,128)} %refs_2_.11, f32[3,64,128]{2,1,0:T(8,128)} %get-tuple-element.20.refs_3_.refs_4_, ...), custom_call_target="tpu_custom_call" | custom-call | tf_op jit(solution)/shard_map/pallas_call | solution.py:258
  58.8 2.5 %collective-permute-done.8.refs_5_ = f32[2,64,128]{2,1,0:T(8,128)S(1)} collective-permute-done((f32[2,64,128]{2,1,0:T(8,128)}, f32[2,64,128]{2,1,0:T(8,128)S(1)}, u32[]{:S(2)}, u32[]{:S(2)}) %collective-permute-start.8) | collective-permute-done | bytes 65568 | tf_op jit(solution)/shard_map/ppermute | solution.py:19
  61.9 2.9 %shard_map.98 = (f32[1,2,64,128]{3,2,1,0:T(8,128)}, f32[1,3,2,64,128]{4,3,2,1,0:T(8,128)}, f32[1,2,64,128]{3,2,1,0:T(8,128)}, f32[1,3,2,64,128]{4,3,2,1,0:T(8,128)}) custom-call(f32[1,4,2,64,128]{4,3,2,1,0:T(8,128)} %get-tuple-element.27.refs_0_, f32[2,64,128]{2,1,0:T(8,128)} %refs_1_.7, f32[2,64,128]{2,1,0:T(8,128)} %refs_2_.11, ...), custom_call_target="tpu_custom_call" | custom-call | tf_op jit(solution)/shard_map/pallas_call | solution.py:258
  (18 shorter events, 1.0 us)
Async XLA Ops:
  2.9 9.0 %collective-permute-start.1 = (f32[6,64,128]{2,1,0:T(8,128)}, f32[6,64,128]{2,1,0:T(8,128)S(1)}, u32[]{:S(2)}, u32[]{:S(2)}) collective-permute-start(f32[6,64,128]{2,1,0:T(8,128)} %get-tuple-element.18), channel_id=1, source_target_pairs={{2,0},{4,2},{6,4},{8,6},{10,8},{12,10},{14,12},{16,14},{18,16},{20... | collective-permute-start | bytes 589832 | tf_op jit(solution)/shard_map/ppermute | solution.py:19
  5.4 6.4 %collective-permute-start = (f32[5,64,128]{2,1,0:T(8,128)}, f32[5,64,128]{2,1,0:T(8,128)S(1)}, u32[]{:S(2)}, u32[]{:S(2)}) collective-permute-start(f32[5,64,128]{2,1,0:T(8,128)} %get-tuple-element.17), channel_id=1, source_target_pairs={{0,2},{2,4},{4,6},{6,8},{8,10},{10,12},{12,14},{14,16},{16,18},{18... | collective-permute-start | bytes 491528 | tf_op jit(solution)/shard_map/ppermute | solution.py:19
  11.9 0.7 %copy-start.1 = (f32[5,64,128]{2,1,0:T(8,128)}, f32[5,64,128]{2,1,0:T(8,128)S(1)}, u32[]{:S(2)}) copy-start(f32[5,64,128]{2,1,0:T(8,128)S(1)} %collective-permute-done.refs_6_.refs_7_) | copy-start | bytes 491524
  12.5 0.7 %copy-start.4 = (f32[6,64,128]{2,1,0:T(8,128)}, f32[6,64,128]{2,1,0:T(8,128)S(1)}, u32[]{:S(2)}) copy-start(f32[6,64,128]{2,1,0:T(8,128)S(1)} %collective-permute-done.1.refs_8_) | copy-start | bytes 589828
  17.1 7.4 %collective-permute-start.2 = (f32[4,64,128]{2,1,0:T(8,128)}, f32[4,64,128]{2,1,0:T(8,128)S(1)}, u32[]{:S(2)}, u32[]{:S(2)}) collective-permute-start(f32[4,64,128]{2,1,0:T(8,128)} %get-tuple-element.21), channel_id=1, source_target_pairs={{0,2},{2,4},{4,6},{6,8},{8,10},{10,12},{12,14},{14,16},{16,18},{18... | collective-permute-start | bytes 393224 | tf_op jit(solution)/shard_map/ppermute | solution.py:19
  22.3 7.4 %collective-permute-start.3 = (f32[4,64,128]{2,1,0:T(8,128)}, f32[4,64,128]{2,1,0:T(8,128)S(1)}, u32[]{:S(2)}, u32[]{:S(2)}) collective-permute-start(f32[4,64,128]{2,1,0:T(8,128)} %get-tuple-element.22), channel_id=1, source_target_pairs={{2,0},{4,2},{6,4},{8,6},{10,8},{12,10},{14,12},{16,14},{18,16},{20... | collective-permute-start | bytes 393224 | tf_op jit(solution)/shard_map/ppermute | solution.py:19
  24.5 5.2 %copy-start.5 = (f32[4,64,128]{2,1,0:T(8,128)}, f32[4,64,128]{2,1,0:T(8,128)S(1)}, u32[]{:S(2)}) copy-start(f32[4,64,128]{2,1,0:T(8,128)S(1)} %collective-permute-done.2.refs_4_) | copy-start | bytes 393220
  29.7 0.7 %copy-start.6 = (f32[4,64,128]{2,1,0:T(8,128)}, f32[4,64,128]{2,1,0:T(8,128)S(1)}, u32[]{:S(2)}) copy-start(f32[4,64,128]{2,1,0:T(8,128)S(1)} %collective-permute-done.3.refs_5_) | copy-start | bytes 393220
  34.0 12.1 %collective-permute-start.4 = (f32[4,2,64,128]{3,2,1,0:T(8,128)}, f32[4,2,64,128]{3,2,1,0:T(8,128)S(1)}, u32[]{:S(2)}, u32[]{:S(2)}) collective-permute-start(f32[4,2,64,128]{3,2,1,0:T(8,128)} %get-tuple-element.23), channel_id=1, source_target_pairs={{0,1},{2,3},{4,5},{6,7},{8,9},{10,11},{12,13},{14,15},{16,17},{18,... | collective-permute-start | bytes 786440 | tf_op jit(solution)/shard_map/ppermute | solution.py:19
  35.3 10.2 %collective-permute-start.5 = (f32[4,64,128]{2,1,0:T(8,128)}, f32[4,64,128]{2,1,0:T(8,128)S(1)}, u32[]{:S(2)}, u32[]{:S(2)}) collective-permute-start(f32[4,64,128]{2,1,0:T(8,128)} %get-tuple-element.25), channel_id=1, source_target_pairs={{0,3},{2,5},{4,7},{6,9},{8,11},{10,13},{12,15},{14,17},{16,19},{18... | collective-permute-start | bytes 393224 | tf_op jit(solution)/shard_map/ppermute | solution.py:221
  36.6 8.9 %collective-permute-start.6 = (f32[4,64,128]{2,1,0:T(8,128)}, f32[4,64,128]{2,1,0:T(8,128)S(1)}, u32[]{:S(2)}, u32[]{:S(2)}) collective-permute-start(f32[4,64,128]{2,1,0:T(8,128)} %get-tuple-element.26), channel_id=1, source_target_pairs={{2,1},{4,3},{6,5},{8,7},{10,9},{12,11},{14,13},{16,15},{18,17},{20... | collective-permute-start | bytes 393224 | tf_op jit(solution)/shard_map/ppermute | solution.py:221
  45.5 0.7 %copy-start.2 = (f32[4,64,128]{2,1,0:T(8,128)}, f32[4,64,128]{2,1,0:T(8,128)S(1)}, u32[]{:S(2)}) copy-start(f32[4,64,128]{2,1,0:T(8,128)S(1)} %collective-permute-done.5.refs_5_) | copy-start | bytes 393220
  45.5 0.7 %copy-start.3 = (f32[4,64,128]{2,1,0:T(8,128)}, f32[4,64,128]{2,1,0:T(8,128)S(1)}, u32[]{:S(2)}) copy-start(f32[4,64,128]{2,1,0:T(8,128)S(1)} %collective-permute-done.6.refs_6_) | copy-start | bytes 393220
  46.1 0.7 %copy-start = (f32[4,2,64,128]{3,2,1,0:T(8,128)}, f32[4,2,64,128]{3,2,1,0:T(8,128)S(1)}, u32[]{:S(2)}) copy-start(f32[4,2,64,128]{3,2,1,0:T(8,128)S(1)} %collective-permute-done.4.refs_0_) | copy-start | bytes 786436
  49.6 9.2 %collective-permute-start.7 = (f32[2,64,128]{2,1,0:T(8,128)}, f32[2,64,128]{2,1,0:T(8,128)S(1)}, u32[]{:S(2)}, u32[]{:S(2)}) collective-permute-start(f32[2,64,128]{2,1,0:T(8,128)} %get-tuple-element.28), channel_id=1, source_target_pairs={{0,2},{2,4},{4,6},{6,8},{8,10},{10,12},{12,14},{14,16},{16,18},{18... | collective-permute-start | bytes 196616 | tf_op jit(solution)/shard_map/ppermute | solution.py:19
  54.6 6.7 %collective-permute-start.8 = (f32[2,64,128]{2,1,0:T(8,128)}, f32[2,64,128]{2,1,0:T(8,128)S(1)}, u32[]{:S(2)}, u32[]{:S(2)}) collective-permute-start(f32[2,64,128]{2,1,0:T(8,128)} %get-tuple-element.29), channel_id=1, source_target_pairs={{2,0},{4,2},{6,4},{8,6},{10,8},{12,10},{14,12},{16,14},{18,16},{20... | collective-permute-start | bytes 196616 | tf_op jit(solution)/shard_map/ppermute | solution.py:19
  58.8 2.5 %copy-start.7 = (f32[2,64,128]{2,1,0:T(8,128)}, f32[2,64,128]{2,1,0:T(8,128)S(1)}, u32[]{:S(2)}) copy-start(f32[2,64,128]{2,1,0:T(8,128)S(1)} %collective-permute-done.7.refs_4_) | copy-start | bytes 196612
  61.3 0.6 copy-start.8

commit v10 on v9

--- a/solution.py
+++ b/solution.py
@@ -29,7 +29,7 @@
 
 def forces(pressure, lower):
     combined = pressure + lower
-    force_x = 0.25 * (nsum(nsum(lower, 1, 1), 1, 0) - nsum(nsum(pressure, 1, 1), 1, 0))
+    force_x = 0.25 * nsum(nsum(lower - pressure, 1, 1), 1, 0)
     across_z = nsum(combined, 1, 1)
     force_y = 0.25 * (roll(across_z, 1, 0) - across_z)
     across_y = nsum(combined, 1, 0)

time: 65.3 us -> 65.3 us (level)
  transfers between devices with their start and end apart: 9 -> 9, of which waited for: 6 -> 6; matrix products, arithmetic and copies ran while one was open for 0% -> 0% of each run, Pallas kernels for 3% -> 4%
where the time goes in v10:
time: 65.3 us; the launch traced here: 64.8 us
  starting transfers between devices  24.3 us (37%)
  waiting for transfers between devices  18.7 us (29%)
  Pallas kernels  17.8 us (27%)
  local copies, waits for them, and re-layouts  3.31 us (5%)
  between operations  0.72 us (1%)
    ppermute x7, starting transfers between devices, from_behind(): return lax.ppermute(x, axis, pairs)  21.7 us
    pallas_call x5, Pallas kernels, advance(): return pl.pallas_call(kernel, out_shape=tuple(outs), in_specs=specs)(*args)  15.5 us
    ppermute x7, waiting for transfers between devices, from_behind(): return lax.ppermute(x, axis, pairs)  11.1 us
    ppermute x2, waiting for transfers between devices, diagonal(): return lax.ppermute(x, ('space', 'tm'), pairs)  7.59 us
    unnamed x18, local copies, waits for them, and re-layouts  3.31 us
    ppermute x2, starting transfers between devices, diagonal(): return lax.ppermute(x, ('space', 'tm'), pairs)  2.58 us
    pallas_call x1, Pallas kernels, first_messages(): pl.pallas_call(kernel, out_shape=(planes(width + (1 if extras else 0), st...  2.28 us
  transfers between devices with their start and end apart: 9, of which 6 were waited for; matrix products, arithmetic and copies ran while one was open for 0% of the time, Pallas kernels for 4%

profile of v10, /device:TPU:7, one launch (start us, length us, event | category | flops | bytes accessed | tf_op | source)
XLA Modules:
  0.0 64.8 jit_solution(14474531471801568242)
XLA Ops:
  0.6 2.3 %shard_map.93 = (f32[5,64,128]{2,1,0:T(8,128)}, f32[6,64,128]{2,1,0:T(8,128)}) custom-call(f32[1,2,64,128]{3,2,1,0:T(8,128)} %refs_0_.3, f32[1,3,2,64,128]{4,3,2,1,0:T(8,128)} %refs_1_.5, f32[2,64,128]{2,1,0:T(8,128)} %refs_2_.7, f32[3,2,64,128]{3,2,1,0:T(8,128)} %refs_3_.5, f32[2,64,128]{2,1,0:T(8,128)} %refs_1_.7, f32[2,64,128]{2,1,0:T(8,128)} %refs_2_.11), custom_call_target="tpu_custom_call" | custom-call | tf_op jit(solution)/shard_map/pallas_call | solution.py:278
  2.9 2.6 %collective-permute-start.1 = (f32[6,64,128]{2,1,0:T(8,128)}, f32[6,64,128]{2,1,0:T(8,128)S(1)}, u32[]{:S(2)}, u32[]{:S(2)}) collective-permute-start(f32[6,64,128]{2,1,0:T(8,128)} %get-tuple-element.18), channel_id=1, source_target_pairs={{2,0},{4,2},{6,4},{8,6},{10,8},{12,10},{14,12},{16,14},{18,16},{20... | collective-permute-start | bytes 589832 | tf_op jit(solution)/shard_map/ppermute | solution.py:19
  5.5 3.9 %collective-permute-start = (f32[5,64,128]{2,1,0:T(8,128)}, f32[5,64,128]{2,1,0:T(8,128)S(1)}, u32[]{:S(2)}, u32[]{:S(2)}) collective-permute-start(f32[5,64,128]{2,1,0:T(8,128)} %get-tuple-element.17), channel_id=1, source_target_pairs={{0,2},{2,4},{4,6},{6,8},{8,10},{10,12},{12,14},{14,16},{16,18},{18... | collective-permute-start | bytes 491528 | tf_op jit(solution)/shard_map/ppermute | solution.py:19
  9.4 2.6 %collective-permute-done.refs_6_.refs_7_ = f32[5,64,128]{2,1,0:T(8,128)S(1)} collective-permute-done((f32[5,64,128]{2,1,0:T(8,128)}, f32[5,64,128]{2,1,0:T(8,128)S(1)}, u32[]{:S(2)}, u32[]{:S(2)}) %collective-permute-start) | collective-permute-done | bytes 163872 | tf_op jit(solution)/shard_map/ppermute | solution.py:19
  11.9 0.7 %copy-done.1 = f32[5,64,128]{2,1,0:T(8,128)} copy-done((f32[5,64,128]{2,1,0:T(8,128)}, f32[5,64,128]{2,1,0:T(8,128)S(1)}, u32[]{:S(2)}) %copy-start.1) | copy-done | bytes 163864
  12.6 0.7 %copy-done.4 = f32[6,64,128]{2,1,0:T(8,128)} copy-done((f32[6,64,128]{2,1,0:T(8,128)}, f32[6,64,128]{2,1,0:T(8,128)S(1)}, u32[]{:S(2)}) %copy-start.4) | copy-done | bytes 196632
  13.3 3.9 %shard_map.94 = (f32[2,4,2,64,128]{4,3,2,1,0:T(8,128)}, f32[4,64,128]{2,1,0:T(8,128)}, f32[4,64,128]{2,1,0:T(8,128)}, f32[3,64,128]{2,1,0:T(8,128)}) custom-call(f32[1,2,64,128]{3,2,1,0:T(8,128)} %refs_0_.3, f32[1,3,2,64,128]{4,3,2,1,0:T(8,128)} %refs_1_.5, f32[2,64,128]{2,1,0:T(8,128)} %refs_2_.7, f32[3,2,64,128]{3,2,1,0:T(8,128)} %refs_3_.5, ...), custom_call_target="tpu_custom_call" | custom-call | tf_op jit(solution)/shard_map/pallas_call | solution.py:258
  17.2 5.2 %collective-permute-start.2 = (f32[4,64,128]{2,1,0:T(8,128)}, f32[4,64,128]{2,1,0:T(8,128)S(1)}, u32[]{:S(2)}, u32[]{:S(2)}) collective-permute-start(f32[4,64,128]{2,1,0:T(8,128)} %get-tuple-element.21), channel_id=1, source_target_pairs={{0,2},{2,4},{4,6},{6,8},{8,10},{10,12},{12,14},{14,16},{16,18},{18... | collective-permute-start | bytes 393224 | tf_op jit(solution)/shard_map/ppermute | solution.py:19
  22.4 1.9 %collective-permute-start.3 = (f32[4,64,128]{2,1,0:T(8,128)}, f32[4,64,128]{2,1,0:T(8,128)S(1)}, u32[]{:S(2)}, u32[]{:S(2)}) collective-permute-start(f32[4,64,128]{2,1,0:T(8,128)} %get-tuple-element.22), channel_id=1, source_target_pairs={{2,0},{4,2},{6,4},{8,6},{10,8},{12,10},{14,12},{16,14},{18,16},{20... | collective-permute-start | bytes 393224 | tf_op jit(solution)/shard_map/ppermute | solution.py:19
  24.6 5.2 %collective-permute-done.3.refs_5_ = f32[4,64,128]{2,1,0:T(8,128)S(1)} collective-permute-done((f32[4,64,128]{2,1,0:T(8,128)}, f32[4,64,128]{2,1,0:T(8,128)S(1)}, u32[]{:S(2)}, u32[]{:S(2)}) %collective-permute-start.3) | collective-permute-done | bytes 131104 | tf_op jit(solution)/shard_map/ppermute | solution.py:19
  29.8 0.7 %copy-done.6 = f32[4,64,128]{2,1,0:T(8,128)} copy-done((f32[4,64,128]{2,1,0:T(8,128)}, f32[4,64,128]{2,1,0:T(8,128)S(1)}, u32[]{:S(2)}) %copy-start.6) | copy-done | bytes 131096
  30.4 3.6 %shard_map.95 = (f32[2,4,2,64,128]{4,3,2,1,0:T(8,128)}, f32[4,2,64,128]{3,2,1,0:T(8,128)}, f32[4,64,128]{2,1,0:T(8,128)}, f32[4,64,128]{2,1,0:T(8,128)}) custom-call(f32[2,4,2,64,128]{4,3,2,1,0:T(8,128)} %get-tuple-element.19.refs_0_, f32[2,64,128]{2,1,0:T(8,128)} %refs_1_.7, f32[2,64,128]{2,1,0:T(8,128)} %refs_2_.11, ...), custom_call_target="tpu_custom_call" | custom-call | tf_op jit(solution)/shard_map/pallas_call | solution.py:258
  34.0 1.3 %collective-permute-start.4 = (f32[4,2,64,128]{3,2,1,0:T(8,128)}, f32[4,2,64,128]{3,2,1,0:T(8,128)S(1)}, u32[]{:S(2)}, u32[]{:S(2)}) collective-permute-start(f32[4,2,64,128]{3,2,1,0:T(8,128)} %get-tuple-element.23), channel_id=1, source_target_pairs={{0,1},{2,3},{4,5},{6,7},{8,9},{10,11},{12,13},{14,15},{16,17},{18,... | collective-permute-start | bytes 786440 | tf_op jit(solution)/shard_map/ppermute | solution.py:19
  35.3 1.3 %collective-permute-start.5 = (f32[4,64,128]{2,1,0:T(8,128)}, f32[4,64,128]{2,1,0:T(8,128)S(1)}, u32[]{:S(2)}, u32[]{:S(2)}) collective-permute-start(f32[4,64,128]{2,1,0:T(8,128)} %get-tuple-element.25), channel_id=1, source_target_pairs={{0,3},{2,5},{4,7},{6,9},{8,11},{10,13},{12,15},{14,17},{16,19},{18... | collective-permute-start | bytes 393224 | tf_op jit(solution)/shard_map/ppermute | solution.py:221
  36.6 1.3 %collective-permute-start.6 = (f32[4,64,128]{2,1,0:T(8,128)}, f32[4,64,128]{2,1,0:T(8,128)S(1)}, u32[]{:S(2)}, u32[]{:S(2)}) collective-permute-start(f32[4,64,128]{2,1,0:T(8,128)} %get-tuple-element.26), channel_id=1, source_target_pairs={{2,1},{4,3},{6,5},{8,7},{10,9},{12,11},{14,13},{16,15},{18,17},{20... | collective-permute-start | bytes 393224 | tf_op jit(solution)/shard_map/ppermute | solution.py:221
  37.9 7.6 %collective-permute-done.5.refs_5_ = f32[4,64,128]{2,1,0:T(8,128)S(1)} collective-permute-done((f32[4,64,128]{2,1,0:T(8,128)}, f32[4,64,128]{2,1,0:T(8,128)S(1)}, u32[]{:S(2)}, u32[]{:S(2)}) %collective-permute-start.5) | collective-permute-done | bytes 131104 | tf_op jit(solution)/shard_map/ppermute | solution.py:221
  45.5 0.6 collective-permute-done.4.refs_0_
  46.2 0.6 copy-done
  46.9 2.8 %shard_map.96 = (f32[1,4,2,64,128]{4,3,2,1,0:T(8,128)}, f32[2,64,128]{2,1,0:T(8,128)}, f32[2,64,128]{2,1,0:T(8,128)}) custom-call(f32[4,2,64,128]{3,2,1,0:T(8,128)} %copy-done, f32[2,4,2,64,128]{4,3,2,1,0:T(8,128)} %get-tuple-element.24.refs_1_.refs_7_, f32[2,64,128]{2,1,0:T(8,128)} %refs_1_.7, f32[2,64,128]{2,1,0:T(8,128)} %refs_2_.11, ...), custom_call_target="tpu_custom_call" | custom-call | tf_op jit(solution)/shard_map/pallas_call | solution.py:258
  49.7 5.0 %collective-permute-start.7 = (f32[2,64,128]{2,1,0:T(8,128)}, f32[2,64,128]{2,1,0:T(8,128)S(1)}, u32[]{:S(2)}, u32[]{:S(2)}) collective-permute-start(f32[2,64,128]{2,1,0:T(8,128)} %get-tuple-element.28), channel_id=1, source_target_pairs={{0,2},{2,4},{4,6},{6,8},{8,10},{10,12},{12,14},{14,16},{16,18},{18... | collective-permute-start | bytes 196616 | tf_op jit(solution)/shard_map/ppermute | solution.py:19
  54.7 1.9 %collective-permute-start.8 = (f32[2,64,128]{2,1,0:T(8,128)}, f32[2,64,128]{2,1,0:T(8,128)S(1)}, u32[]{:S(2)}, u32[]{:S(2)}) collective-permute-start(f32[2,64,128]{2,1,0:T(8,128)} %get-tuple-element.29), channel_id=1, source_target_pairs={{2,0},{4,2},{6,4},{8,6},{10,8},{12,10},{14,12},{16,14},{18,16},{20... | collective-permute-start | bytes 196616 | tf_op jit(solution)/shard_map/ppermute | solution.py:19
  56.6 2.3 %shard_map.97.refs_8_ = f32[1,4,2,64,128]{4,3,2,1,0:T(8,128)} custom-call(f32[4,2,64,128]{3,2,1,0:T(8,128)} %copy-done, f32[2,4,2,64,128]{4,3,2,1,0:T(8,128)} %get-tuple-element.24.refs_1_.refs_7_, f32[2,64,128]{2,1,0:T(8,128)} %refs_1_.7, f32[2,64,128]{2,1,0:T(8,128)} %refs_2_.11, f32[3,64,128]{2,1,0:T(8,128)} %get-tuple-element.20.refs_3_.refs_4_, ...), custom_call_target="tpu_custom_call" | custom-call | tf_op jit(solution)/shard_map/pallas_call | solution.py:258
  58.9 2.5 %collective-permute-done.8.refs_5_ = f32[2,64,128]{2,1,0:T(8,128)S(1)} collective-permute-done((f32[2,64,128]{2,1,0:T(8,128)}, f32[2,64,128]{2,1,0:T(8,128)S(1)}, u32[]{:S(2)}, u32[]{:S(2)}) %collective-permute-start.8) | collective-permute-done | bytes 65568 | tf_op jit(solution)/shard_map/ppermute | solution.py:19
  62.0 2.9 %shard_map.98 = (f32[1,2,64,128]{3,2,1,0:T(8,128)}, f32[1,3,2,64,128]{4,3,2,1,0:T(8,128)}, f32[1,2,64,128]{3,2,1,0:T(8,128)}, f32[1,3,2,64,128]{4,3,2,1,0:T(8,128)}) custom-call(f32[1,4,2,64,128]{4,3,2,1,0:T(8,128)} %get-tuple-element.27.refs_0_, f32[2,64,128]{2,1,0:T(8,128)} %refs_1_.7, f32[2,64,128]{2,1,0:T(8,128)} %refs_2_.11, ...), custom_call_target="tpu_custom_call" | custom-call | tf_op jit(solution)/shard_map/pallas_call | solution.py:258
  (18 shorter events, 1.0 us)
Async XLA Ops:
  2.9 9.0 %collective-permute-start.1 = (f32[6,64,128]{2,1,0:T(8,128)}, f32[6,64,128]{2,1,0:T(8,128)S(1)}, u32[]{:S(2)}, u32[]{:S(2)}) collective-permute-start(f32[6,64,128]{2,1,0:T(8,128)} %get-tuple-element.18), channel_id=1, source_target_pairs={{2,0},{4,2},{6,4},{8,6},{10,8},{12,10},{14,12},{16,14},{18,16},{20... | collective-permute-start | bytes 589832 | tf_op jit(solution)/shard_map/ppermute | solution.py:19
  5.5 6.4 %collective-permute-start = (f32[5,64,128]{2,1,0:T(8,128)}, f32[5,64,128]{2,1,0:T(8,128)S(1)}, u32[]{:S(2)}, u32[]{:S(2)}) collective-permute-start(f32[5,64,128]{2,1,0:T(8,128)} %get-tuple-element.17), channel_id=1, source_target_pairs={{0,2},{2,4},{4,6},{6,8},{8,10},{10,12},{12,14},{14,16},{16,18},{18... | collective-permute-start | bytes 491528 | tf_op jit(solution)/shard_map/ppermute | solution.py:19
  11.9 0.7 %copy-start.1 = (f32[5,64,128]{2,1,0:T(8,128)}, f32[5,64,128]{2,1,0:T(8,128)S(1)}, u32[]{:S(2)}) copy-start(f32[5,64,128]{2,1,0:T(8,128)S(1)} %collective-permute-done.refs_6_.refs_7_) | copy-start | bytes 491524
  12.6 0.7 %copy-start.4 = (f32[6,64,128]{2,1,0:T(8,128)}, f32[6,64,128]{2,1,0:T(8,128)S(1)}, u32[]{:S(2)}) copy-start(f32[6,64,128]{2,1,0:T(8,128)S(1)} %collective-permute-done.1.refs_8_) | copy-start | bytes 589828
  17.2 7.4 %collective-permute-start.2 = (f32[4,64,128]{2,1,0:T(8,128)}, f32[4,64,128]{2,1,0:T(8,128)S(1)}, u32[]{:S(2)}, u32[]{:S(2)}) collective-permute-start(f32[4,64,128]{2,1,0:T(8,128)} %get-tuple-element.21), channel_id=1, source_target_pairs={{0,2},{2,4},{4,6},{6,8},{8,10},{10,12},{12,14},{14,16},{16,18},{18... | collective-permute-start | bytes 393224 | tf_op jit(solution)/shard_map/ppermute | solution.py:19
  22.4 7.4 %collective-permute-start.3 = (f32[4,64,128]{2,1,0:T(8,128)}, f32[4,64,128]{2,1,0:T(8,128)S(1)}, u32[]{:S(2)}, u32[]{:S(2)}) collective-permute-start(f32[4,64,128]{2,1,0:T(8,128)} %get-tuple-element.22), channel_id=1, source_target_pairs={{2,0},{4,2},{6,4},{8,6},{10,8},{12,10},{14,12},{16,14},{18,16},{20... | collective-permute-start | bytes 393224 | tf_op jit(solution)/shard_map/ppermute | solution.py:19
  24.6 5.2 %copy-start.5 = (f32[4,64,128]{2,1,0:T(8,128)}, f32[4,64,128]{2,1,0:T(8,128)S(1)}, u32[]{:S(2)}) copy-start(f32[4,64,128]{2,1,0:T(8,128)S(1)} %collective-permute-done.2.refs_4_) | copy-start | bytes 393220
  29.8 0.7 %copy-start.6 = (f32[4,64,128]{2,1,0:T(8,128)}, f32[4,64,128]{2,1,0:T(8,128)S(1)}, u32[]{:S(2)}) copy-start(f32[4,64,128]{2,1,0:T(8,128)S(1)} %collective-permute-done.3.refs_5_) | copy-start | bytes 393220
  34.0 12.1 %collective-permute-start.4 = (f32[4,2,64,128]{3,2,1,0:T(8,128)}, f32[4,2,64,128]{3,2,1,0:T(8,128)S(1)}, u32[]{:S(2)}, u32[]{:S(2)}) collective-permute-start(f32[4,2,64,128]{3,2,1,0:T(8,128)} %get-tuple-element.23), channel_id=1, source_target_pairs={{0,1},{2,3},{4,5},{6,7},{8,9},{10,11},{12,13},{14,15},{16,17},{18,... | collective-permute-start | bytes 786440 | tf_op jit(solution)/shard_map/ppermute | solution.py:19
  35.3 10.2 %collective-permute-start.5 = (f32[4,64,128]{2,1,0:T(8,128)}, f32[4,64,128]{2,1,0:T(8,128)S(1)}, u32[]{:S(2)}, u32[]{:S(2)}) collective-permute-start(f32[4,64,128]{2,1,0:T(8,128)} %get-tuple-element.25), channel_id=1, source_target_pairs={{0,3},{2,5},{4,7},{6,9},{8,11},{10,13},{12,15},{14,17},{16,19},{18... | collective-permute-start | bytes 393224 | tf_op jit(solution)/shard_map/ppermute | solution.py:221
  36.6 8.9 %collective-permute-start.6 = (f32[4,64,128]{2,1,0:T(8,128)}, f32[4,64,128]{2,1,0:T(8,128)S(1)}, u32[]{:S(2)}, u32[]{:S(2)}) collective-permute-start(f32[4,64,128]{2,1,0:T(8,128)} %get-tuple-element.26), channel_id=1, source_target_pairs={{2,1},{4,3},{6,5},{8,7},{10,9},{12,11},{14,13},{16,15},{18,17},{20... | collective-permute-start | bytes 393224 | tf_op jit(solution)/shard_map/ppermute | solution.py:221
  45.5 0.7 %copy-start.2 = (f32[4,64,128]{2,1,0:T(8,128)}, f32[4,64,128]{2,1,0:T(8,128)S(1)}, u32[]{:S(2)}) copy-start(f32[4,64,128]{2,1,0:T(8,128)S(1)} %collective-permute-done.5.refs_5_) | copy-start | bytes 393220
  45.5 0.7 %copy-start.3 = (f32[4,64,128]{2,1,0:T(8,128)}, f32[4,64,128]{2,1,0:T(8,128)S(1)}, u32[]{:S(2)}) copy-start(f32[4,64,128]{2,1,0:T(8,128)S(1)} %collective-permute-done.6.refs_6_) | copy-start | bytes 393220
  46.2 0.7 %copy-start = (f32[4,2,64,128]{3,2,1,0:T(8,128)}, f32[4,2,64,128]{3,2,1,0:T(8,128)S(1)}, u32[]{:S(2)}) copy-start(f32[4,2,64,128]{3,2,1,0:T(8,128)S(1)} %collective-permute-done.4.refs_0_) | copy-start | bytes 786436
  49.7 9.2 %collective-permute-start.7 = (f32[2,64,128]{2,1,0:T(8,128)}, f32[2,64,128]{2,1,0:T(8,128)S(1)}, u32[]{:S(2)}, u32[]{:S(2)}) collective-permute-start(f32[2,64,128]{2,1,0:T(8,128)} %get-tuple-element.28), channel_id=1, source_target_pairs={{0,2},{2,4},{4,6},{6,8},{8,10},{10,12},{12,14},{14,16},{16,18},{18... | collective-permute-start | bytes 196616 | tf_op jit(solution)/shard_map/ppermute | solution.py:19
  54.7 6.7 %collective-permute-start.8 = (f32[2,64,128]{2,1,0:T(8,128)}, f32[2,64,128]{2,1,0:T(8,128)S(1)}, u32[]{:S(2)}, u32[]{:S(2)}) collective-permute-start(f32[2,64,128]{2,1,0:T(8,128)} %get-tuple-element.29), channel_id=1, source_target_pairs={{2,0},{4,2},{6,4},{8,6},{10,8},{12,10},{14,12},{16,14},{18,16},{20... | collective-permute-start | bytes 196616 | tf_op jit(solution)/shard_map/ppermute | solution.py:19
  58.9 2.5 %copy-start.7 = (f32[2,64,128]{2,1,0:T(8,128)}, f32[2,64,128]{2,1,0:T(8,128)S(1)}, u32[]{:S(2)}) copy-start(f32[2,64,128]{2,1,0:T(8,128)S(1)} %collective-permute-done.7.refs_4_) | copy-start | bytes 196612
  61.4 0.6 copy-start.8
